TPU v7x, 1024 devices: a whole 4x4x32 slice. The times are simulated.
1024 devices in a mesh: pipe: 8 (over y, core), seq: 32 (over z), tp: 4 (over x).
Axes of the slice: x: 4, y: 4, z: 32, core: 2. Of those that a mesh axis runs over, the one named last changes fastest.
Arguments:
- upstream: bfloat16 [8, 4, 3072, 2048], P('pipe', 'tp', 'seq'), may hold values from -6 to 6
- queries: bfloat16 [8, 4, 3072, 2048], P('pipe', 'tp', 'seq'), may hold values from -6 to 6
- attention_out: bfloat16 [8, 4, 3072, 2048], P('pipe', 'tp', 'seq'), may hold values from -6 to 6
- keys_values: bfloat16 [8, 4, 32, 3072, 128], P('pipe', 'tp', 'seq'), may hold values from -6 to 6
- log_totals: float32 [8, 4, 32, 3072], P('pipe', 'tp', 'seq'), may hold values from 3.5 to 5.5
- neighbours: int32 [192, 7], replicated, may hold values from -1 to 191, as said below
Outputs:
- query_grad: bfloat16 [8, 4, 32, 3072, 64], P('pipe', 'tp', 'seq')
- cache_grad: bfloat16 [8, 4, 32, 3072, 128], P('pipe', 'tp', 'seq')
Inputs may be any that keep to these rules, and one draw needn't show every extreme that they name: `neighbours`: in each row the used entries come first and are distinct; the first is the row's own block; every used entry lies within 4 blocks of the row's block; unused entries are -1. Some aligned run of 48 rows has every row listing as many blocks as lie within reach, up to 7; elsewhere rows list 1 to 3 blocks.
All inputs are finite; a program needn't handle non-finite values.
Results may differ from a plain program's by a relative error of at most 0.0055.
Values may be sent and summed in bfloat16 or wider, within the bound.
No kernel may reach another device: no remote copies, remote signals or barrier semaphores. Data moves between devices by JAX's collectives and lax.ppermute only.
A program may use at most 32 MiB of HBM per device.

v0:
```python
import jax
import jax.numpy as jnp
from jax import lax
from jax.sharding import PartitionSpec as P

H = 32
HD = 64
BLK = 64
REACH = 4
NBR = 7


pair_group = 32


def passed_along(value, axis, steps):
    count = lax.axis_size(axis)
    pairs = [(source, (source + steps) % count) for source in range(count)]
    return lax.ppermute(value, axis, pairs)


def padded_2(cells, sides, width):
    for axis, dim in sides:
        count = lax.axis_size(axis)
        ends = count - 1
        head = lax.slice_in_dim(cells, 0, width, axis=dim)
        tail = lax.slice_in_dim(cells, cells.shape[dim] - width, cells.shape[dim], axis=dim)
        cells = jnp.concatenate(
            [
                lax.ppermute(tail, axis, [(i, (i + 1) % count) for i in range(ends)]),
                cells,
                lax.ppermute(head, axis, [((i + 1) % count, i) for i in range(ends)]),
            ],
            axis=dim,
        )
    return cells


def block_layout(values, blocks_here):
    heads_here = values.shape[1]
    turned = jnp.transpose(values, (1, 0, 2))
    return turned.reshape(heads_here, blocks_here, BLK, values.shape[2])


def body(upstream, queries, attention_out, keys_values, log_totals, neighbours):
    tokens_here = queries.shape[2]
    inv_root = HD ** (-0.5)
    incoming = passed_along(upstream, "pipe", -1)
    query_tok = queries.reshape(tokens_here, H, HD)
    grad_tok = incoming.reshape(tokens_here, H, HD)
    out_tok = attention_out.reshape(tokens_here, H, HD)
    packed = jnp.concatenate([query_tok, grad_tok, out_tok], axis=2)
    regrouped = lax.all_to_all(packed, "seq", split_axis=1, concat_axis=0, tiled=True)
    query_heads = regrouped[:, :, :HD]
    grad_heads = regrouped[:, :, HD : 2 * HD]
    out_heads = regrouped[:, :, 2 * HD :]
    row_delta = jnp.sum(grad_heads.astype(jnp.float32) * out_heads.astype(jnp.float32), axis=2)
    rows_here = query_heads.shape[0]
    heads_here = query_heads.shape[1]
    blocks_here = rows_here // BLK
    query_blocks = block_layout(query_heads, blocks_here)
    grad_blocks = block_layout(grad_heads, blocks_here)
    delta_blocks = jnp.transpose(row_delta).reshape(heads_here, blocks_here, BLK)
    norm_blocks = log_totals.reshape(heads_here, blocks_here, BLK)
    cache_blocks = keys_values.reshape(heads_here, blocks_here, BLK, 2 * HD)
    padded = padded_2(cache_blocks, (("tp", 1),), REACH)
    first_block = lax.axis_index("tp") * blocks_here
    listed = lax.dynamic_slice_in_dim(neighbours, first_block, blocks_here, 0)
    present = (listed >= 0).reshape(-1)
    slot_count = blocks_here * NBR
    group_total = (slot_count + pair_group - 1) // pair_group
    capacity = group_total * pair_group
    running = jnp.cumsum(present.astype(jnp.int32)) - 1
    pair_count = jnp.sum(present.astype(jnp.int32))
    target = jnp.where(present, running, capacity)
    query_source = jnp.repeat(jnp.arange(blocks_here, dtype=jnp.int32), NBR)
    key_source = (listed - first_block + REACH).reshape(-1)
    pair_query = jnp.zeros((capacity,), jnp.int32).at[target].set(query_source, mode="drop")
    pair_key = jnp.zeros((capacity,), jnp.int32).at[target].set(key_source, mode="drop")

    def one_group(group_step, totals):
        query_acc, cache_acc = totals
        first_pair = group_step * pair_group
        query_pick = lax.dynamic_slice_in_dim(pair_query, first_pair, pair_group)
        key_pick = lax.dynamic_slice_in_dim(pair_key, first_pair, pair_group)
        live_mask = (first_pair + jnp.arange(pair_group) < pair_count).astype(jnp.float32)
        query_rows = query_blocks[:, query_pick]
        grad_rows = grad_blocks[:, query_pick]
        norm_rows = norm_blocks[:, query_pick]
        delta_rows = delta_blocks[:, query_pick]
        cache_rows = padded[:, key_pick]
        key_rows = cache_rows[..., :HD]
        value_rows = cache_rows[..., HD:]
        scores = (
            jnp.einsum("hgqd,hgkd->hgqk", query_rows, key_rows, preferred_element_type=jnp.float32)
            * inv_root
        )
        weights = jnp.exp(scores - norm_rows[..., None]) * live_mask[None, :, None, None]
        weights_half = weights.astype(jnp.bfloat16)
        grad_weights = jnp.einsum(
            "hgqd,hgkd->hgqk", grad_rows, value_rows, preferred_element_type=jnp.float32
        )
        grad_scores = (weights * (grad_weights - delta_rows[..., None])).astype(jnp.bfloat16)
        query_part = (
            jnp.einsum("hgqk,hgkd->hgqd", grad_scores, key_rows, preferred_element_type=jnp.float32)
            * inv_root
        )
        key_part = (
            jnp.einsum(
                "hgqk,hgqd->hgkd", grad_scores, query_rows, preferred_element_type=jnp.float32
            )
            * inv_root
        )
        value_part = jnp.einsum(
            "hgqk,hgqd->hgkd", weights_half, grad_rows, preferred_element_type=jnp.float32
        )
        query_acc = query_acc.at[:, query_pick].add(query_part)
        cache_acc = cache_acc.at[:, key_pick].add(jnp.concatenate([key_part, value_part], axis=-1))
        return (query_acc, cache_acc)

    group_live = (pair_count + pair_group - 1) // pair_group
    query_start = jnp.zeros((heads_here, blocks_here, BLK, HD), jnp.float32)
    cache_start = jnp.zeros((heads_here, blocks_here + 2 * REACH, BLK, 2 * HD), jnp.float32)
    query_acc, cache_acc = lax.fori_loop(0, group_live, one_group, (query_start, cache_start))
    rim_terms = jnp.concatenate([cache_acc[:, :REACH], cache_acc[:, REACH + blocks_here :]], axis=1)
    arrived = padded_2(rim_terms.astype(jnp.bfloat16), (("tp", 1),), REACH).astype(rim_terms.dtype)
    own_part = cache_acc[:, REACH : REACH + blocks_here]
    own_part = own_part.at[:, :REACH].add(arrived[:, :REACH])
    own_part = own_part.at[:, blocks_here - REACH :].add(arrived[:, 3 * REACH :])
    query_grad = query_acc.reshape(1, 1, heads_here, rows_here, HD).astype(jnp.bfloat16)
    cache_grad = own_part.reshape(1, 1, heads_here, rows_here, 2 * HD).astype(jnp.bfloat16)
    return (query_grad, cache_grad)


def solution(mesh):
    placed = (
        P("pipe", "tp", "seq", None),
        P("pipe", "tp", "seq", None),
        P("pipe", "tp", "seq", None),
        P("pipe", "tp", "seq", None, None),
        P("pipe", "tp", "seq", None),
        P(),
    )
    return jax.shard_map(
        body,
        mesh=mesh,
        in_specs=placed,
        out_specs=(P("pipe", "tp", "seq", None, None), P("pipe", "tp", "seq", None, None)),
        check_vma=False,
    )
```

profile of v0, /device:TPU:19, one launch (start us, length us, event | category | flops | bytes accessed | tf_op | source)
XLA Modules:
  0.0 412.7 jit_solution(9839579694332950777)
XLA Ops:
  0.6 1.3 copy.24
  2.7 1.3 copy.23
  4.2 6.4 %collective-permute-done = bf16[1,1,96,2048]{2,3,1,0:T(8,128)(2,1)S(1)} collective-permute-done((bf16[1,1,96,2048]{2,3,1,0:T(8,128)(2,1)S(1)}, bf16[1,1,96,2048]{2,3,1,0:T(8,128)(2,1)S(1)}, u32[]{:S(2)}, u32[]{:S(2)}) %collective-permute-start) | collective-permute-done | bytes 393248 | tf_op jit(solution)/shard_map/ppermute | solution.py:19
  10.6 1.6 pad_maximum_fusion
  12.1 28.6 %all-to-all-start = ((bf16[96,32,192]{0,2,1:T(8,128)(2,1)}), bf16[96,32,192]{0,2,1:T(8,128)(2,1)S(1)}, u32[]{:S(2)}, u32[]{:S(2)}) async-start(bf16[96,32,192]{0,2,1:T(8,128)(2,1)} %pad_maximum_fusion), calls=%async_computation | async-start | bytes 3145728 | tf_op jit(solution)/shard_map/all_to_all | solution.py:53
  40.8 3.1 collective-permute-start.1
  43.9 2.2 collective-permute-start.2
  49.9 2.9 scatter_custom_fusion.3
  52.9 2.9 scatter_custom_fusion.2
  55.8 1.1 pad_maximum_fusion.1
  56.9 138.8 %all-to-all-done = bf16[96,32,192]{0,2,1:T(8,128)(2,1)S(1)} async-done(((bf16[96,32,192]{0,2,1:T(8,128)(2,1)}), bf16[96,32,192]{0,2,1:T(8,128)(2,1)S(1)}, u32[]{:S(2)}, u32[]{:S(2)}) %all-to-all-start) | async-done | bytes 1179680 | tf_op jit(solution)/shard_map/all_to_all | solution.py:53
  195.7 2.2 copy.26
  197.9 3.3 all_to_all.16
  202.2 1.3 broadcast_in_dim.16
  203.5 1.5 broadcast_in_dim.32
  205.0 51.6 %while.14 = (s32[]{:T(128)}, f32[1,48,64,64]{3,2,1,0:T(8,128)}, f32[1,56,64,128]{3,2,1,0:T(8,128)}, s32[]{:T(128)}, s32[352]{0:T(512)S(1)}, /*index=5*/bf16[1,48...) while((s32[]{:T(128)}, f32[1,48,64,64]{3,2,1,0:T(8,128)}, ...), condition=%wide.region_9.10_spmd, body=%wide.region_6.9_spmd.sunk | while | flops 85723424 | bytes 18671752 | solution.py:124
  206.9 1.8 gather_fusion.2
  212.5 4.8 %scatter_fusion = f32[48,64,64]{2,1,0:T(8,128)} fusion(f32[48,64,64]{2,1,0:T(8,128)} %bitcast.86, s32[32]{0:T(128)S(1)} %get-tuple-element.215, f32[32,64,64]{2,1,0:T(8,128)S(1)} %convolution_multiply_fusion.4), kind=kCustom, calls=%fused_computation.5.clone.1 | custom fusion | flops 131072 | bytes 1572992 | tf_op jit(solution)/shard_map/while/body/scatter-add | solution.py:117
  217.3 4.8 %scatter_fusion.1 = f32[56,64,128]{2,1,0:T(8,128)} fusion(f32[56,64,128]{2,1,0:T(8,128)} %bitcast.94, s32[32]{0:T(128)S(1)} %get-tuple-element.216, f32[32,64,128]{2,1,0:T(8,128)S(1)} %maximum_bitcast_fusion.3), kind=kCustom, calls=%fused_computation.6.clone.1 | custom fusion | flops 262144 | bytes 3145856 | tf_op jit(solution)/shard_map/while/body/scatter-add | solution.py:118
  224.0 1.8 gather_fusion.2
  229.7 4.8 %scatter_fusion = f32[48,64,64]{2,1,0:T(8,128)} fusion(f32[48,64,64]{2,1,0:T(8,128)} %bitcast.86, s32[32]{0:T(128)S(1)} %get-tuple-element.215, f32[32,64,64]{2,1,0:T(8,128)S(1)} %convolution_multiply_fusion.4), kind=kCustom, calls=%fused_computation.5.clone.1 | custom fusion | flops 131072 | bytes 1572992 | tf_op jit(solution)/shard_map/while/body/scatter-add | solution.py:117
  234.4 4.8 %scatter_fusion.1 = f32[56,64,128]{2,1,0:T(8,128)} fusion(f32[56,64,128]{2,1,0:T(8,128)} %bitcast.94, s32[32]{0:T(128)S(1)} %get-tuple-element.216, f32[32,64,128]{2,1,0:T(8,128)S(1)} %maximum_bitcast_fusion.3), kind=kCustom, calls=%fused_computation.6.clone.1 | custom fusion | flops 262144 | bytes 3145856 | tf_op jit(solution)/shard_map/while/body/scatter-add | solution.py:118
  241.1 1.8 gather_fusion.2
  246.8 4.9 %scatter_fusion = f32[48,64,64]{2,1,0:T(8,128)} fusion(f32[48,64,64]{2,1,0:T(8,128)} %bitcast.86, s32[32]{0:T(128)S(1)} %get-tuple-element.215, f32[32,64,64]{2,1,0:T(8,128)S(1)} %convolution_multiply_fusion.4), kind=kCustom, calls=%fused_computation.5.clone.1 | custom fusion | flops 131072 | bytes 1572992 | tf_op jit(solution)/shard_map/while/body/scatter-add | solution.py:117
  251.7 5.0 %scatter_fusion.1 = f32[56,64,128]{2,1,0:T(8,128)} fusion(f32[56,64,128]{2,1,0:T(8,128)} %bitcast.94, s32[32]{0:T(128)S(1)} %get-tuple-element.216, f32[32,64,128]{2,1,0:T(8,128)S(1)} %maximum_bitcast_fusion.3), kind=kCustom, calls=%fused_computation.6.clone.1 | custom fusion | flops 262144 | bytes 3145856 | tf_op jit(solution)/shard_map/while/body/scatter-add | solution.py:118
  257.6 1.5 slice.117
  259.1 1.5 convert_element_type.84
  260.7 1.0 copy.35
  261.7 3.0 collective-permute-start.3
  264.7 18.3 %collective-permute-start.4 = (bf16[1,4,64,128]{3,2,1,0:T(8,128)(2,1)S(1)}, bf16[1,4,64,128]{3,2,1,0:T(8,128)(2,1)S(1)}, u32[]{:S(2)}, u32[]{:S(2)}) collective-permute-start(bf16[1,4,64,128]{3,2,1,0:T(8,128)(2,1)S(1)} %get-tuple-element.133), channel_id=1, source_target_pairs={{1,0},{2,1},{3,2},{5,4},{6,5},{7,6},{9,8},{10,9},{11,10},{13,12},{... | collective-permute-start | bytes 196616 | tf_op jit(solution)/shard_map/ppermute | solution.py:32
  283.1 127.6 %collective-permute-done.4 = bf16[1,4,64,128]{3,2,1,0:T(8,128)(2,1)S(1)} collective-permute-done((bf16[1,4,64,128]{3,2,1,0:T(8,128)(2,1)S(1)}, bf16[1,4,64,128]{3,2,1,0:T(8,128)(2,1)S(1)}, u32[]{:S(2)}, u32[]{:S(2)}) %collective-permute-start.4) | collective-permute-done | bytes 65568 | tf_op jit(solution)/shard_map/ppermute | solution.py:32
  411.7 1.0 convert_element_type.87
  (94 shorter events, 24.0 us)
Async XLA Ops:
  0.6 3.3 copy-start.3
  2.0 8.6 %collective-permute-start = (bf16[1,1,96,2048]{2,3,1,0:T(8,128)(2,1)S(1)}, bf16[1,1,96,2048]{2,3,1,0:T(8,128)(2,1)S(1)}, u32[]{:S(2)}, u32[]{:S(2)}) collective-permute-start(bf16[1,1,96,2048]{2,3,1,0:T(8,128)(2,1)S(1)} %copy.24), channel_id=1, source_target_pairs={{0,896},{128,0},{256,128},{384,256},{512,384},{640,512},{768,640},... | collective-permute-start | bytes 1179656 | tf_op jit(solution)/shard_map/ppermute | solution.py:19
  12.1 28.6 %copy-start.2 = (bf16[1,1,1,3072,128]{4,3,2,1,0:T(8,128)(2,1)S(1)}, bf16[1,1,1,3072,128]{4,3,2,1,0:T(8,128)(2,1)}, u32[]{:S(2)}) copy-start(bf16[1,1,1,3072,128]{4,3,2,1,0:T(8,128)(2,1)} %param.15) | copy-start | bytes 2359300
  12.1 33.9 %copy-start.5 = (s32[192,7]{0,1:T(8,128)S(1)}, s32[192,7]{0,1:T(8,128)}, u32[]{:S(2)}) copy-start(s32[192,7]{0,1:T(8,128)} %param.17) | copy-start | bytes 16132
  12.1 36.7 %copy-start.4 = (f32[1,1,1,3072]{3,2,1,0:T(1,128)S(1)}, f32[1,1,1,3072]{3,2,1,0:T(1,128)}, u32[]{:S(2)}) copy-start(f32[1,1,1,3072]{3,2,1,0:T(1,128)} %param.16) | copy-start | bytes 36868
  12.1 183.5 %all-to-all-start = ((bf16[96,32,192]{0,2,1:T(8,128)(2,1)}), bf16[96,32,192]{0,2,1:T(8,128)(2,1)S(1)}, u32[]{:S(2)}, u32[]{:S(2)}) async-start(bf16[96,32,192]{0,2,1:T(8,128)(2,1)} %pad_maximum_fusion), calls=%async_computation | async-start | bytes 3145728 | tf_op jit(solution)/shard_map/all_to_all | solution.py:53
  40.8 15.0 %collective-permute-start.1 = (bf16[1,4,64,128]{3,2,1,0:T(8,128)(2,1)S(1)}, bf16[1,4,64,128]{3,2,1,0:T(8,128)(2,1)S(1)}, u32[]{:S(2)}, u32[]{:S(2)}) collective-permute-start(bf16[1,4,64,128]{3,2,1,0:T(8,128)(2,1)S(1)} %get-tuple-element.136), channel_id=1, source_target_pairs={{0,1},{1,2},{2,3},{4,5},{5,6},{6,7},{8,9},{9,10},{10,11},{12,13},{... | collective-permute-start | bytes 196616 | tf_op jit(solution)/shard_map/ppermute | solution.py:30
  43.9 11.9 %collective-permute-start.2 = (bf16[1,4,64,128]{3,2,1,0:T(8,128)(2,1)S(1)}, bf16[1,4,64,128]{3,2,1,0:T(8,128)(2,1)S(1)}, u32[]{:S(2)}, u32[]{:S(2)}) collective-permute-start(bf16[1,4,64,128]{3,2,1,0:T(8,128)(2,1)S(1)} %get-tuple-element.137), channel_id=1, source_target_pairs={{1,0},{2,1},{3,2},{5,4},{6,5},{7,6},{9,8},{10,9},{11,10},{13,12},{... | collective-permute-start | bytes 196616 | tf_op jit(solution)/shard_map/ppermute | solution.py:32
  205.0 5.0 %copy-start = (bf16[1,48,64,64]{3,2,1,0:T(8,128)(2,1)}, bf16[1,48,64,64]{3,2,1,0:T(8,128)(2,1)S(1)}, u32[]{:S(2)}) copy-start(bf16[1,48,64,64]{3,2,1,0:T(8,128)(2,1)S(1)} %get-tuple-element.254) | copy-start | bytes 1179652 | tf_op jit(solution)/shard_map/while
  217.3 4.8 %copy-start.1 = (bf16[1,48,64,64]{3,2,1,0:T(8,128)(2,1)S(1)}, bf16[1,48,64,64]{3,2,1,0:T(8,128)(2,1)}, u32[]{:S(2)}) copy-start(bf16[1,48,64,64]{3,2,1,0:T(8,128)(2,1)} %copy-done) | copy-start | bytes 1179652 | tf_op jit(solution)/shard_map/while
  222.1 5.0 %copy-start = (bf16[1,48,64,64]{3,2,1,0:T(8,128)(2,1)}, bf16[1,48,64,64]{3,2,1,0:T(8,128)(2,1)S(1)}, u32[]{:S(2)}) copy-start(bf16[1,48,64,64]{3,2,1,0:T(8,128)(2,1)S(1)} %get-tuple-element.254) | copy-start | bytes 1179652 | tf_op jit(solution)/shard_map/while
  234.4 4.8 %copy-start.1 = (bf16[1,48,64,64]{3,2,1,0:T(8,128)(2,1)S(1)}, bf16[1,48,64,64]{3,2,1,0:T(8,128)(2,1)}, u32[]{:S(2)}) copy-start(bf16[1,48,64,64]{3,2,1,0:T(8,128)(2,1)} %copy-done) | copy-start | bytes 1179652 | tf_op jit(solution)/shard_map/while
  239.2 5.0 %copy-start = (bf16[1,48,64,64]{3,2,1,0:T(8,128)(2,1)}, bf16[1,48,64,64]{3,2,1,0:T(8,128)(2,1)S(1)}, u32[]{:S(2)}) copy-start(bf16[1,48,64,64]{3,2,1,0:T(8,128)(2,1)S(1)} %get-tuple-element.254) | copy-start | bytes 1179652 | tf_op jit(solution)/shard_map/while
  251.7 5.0 %copy-start.1 = (bf16[1,48,64,64]{3,2,1,0:T(8,128)(2,1)S(1)}, bf16[1,48,64,64]{3,2,1,0:T(8,128)(2,1)}, u32[]{:S(2)}) copy-start(bf16[1,48,64,64]{3,2,1,0:T(8,128)(2,1)} %copy-done) | copy-start | bytes 1179652 | tf_op jit(solution)/shard_map/while
  261.7 21.4 %collective-permute-start.3 = (bf16[1,4,64,128]{3,2,1,0:T(8,128)(2,1)S(1)}, bf16[1,4,64,128]{3,2,1,0:T(8,128)(2,1)S(1)}, u32[]{:S(2)}, u32[]{:S(2)}) collective-permute-start(bf16[1,4,64,128]{3,2,1,0:T(8,128)(2,1)S(1)} %get-tuple-element.132), channel_id=1, source_target_pairs={{0,1},{1,2},{2,3},{4,5},{5,6},{6,7},{8,9},{9,10},{10,11},{12,13},{... | collective-permute-start | bytes 196616 | tf_op jit(solution)/shard_map/ppermute | solution.py:30
  264.7 146.0 %collective-permute-start.4 = (bf16[1,4,64,128]{3,2,1,0:T(8,128)(2,1)S(1)}, bf16[1,4,64,128]{3,2,1,0:T(8,128)(2,1)S(1)}, u32[]{:S(2)}, u32[]{:S(2)}) collective-permute-start(bf16[1,4,64,128]{3,2,1,0:T(8,128)(2,1)S(1)} %get-tuple-element.133), channel_id=1, source_target_pairs={{1,0},{2,1},{3,2},{5,4},{6,5},{7,6},{9,8},{10,9},{11,10},{13,12},{... | collective-permute-start | bytes 196616 | tf_op jit(solution)/shard_map/ppermute | solution.py:32
where the time goes:
time: 418 us; the launch traced here: 413 us
  waiting for transfers between devices  273 us (65%)
  starting transfers between devices  55.9 us (13%)
  other arithmetic  40.3 us (10%)
  local copies, waits for them, and re-layouts  35.5 us (8%)
  matrix products  6.4 us (2%)
    all_to_all x1, waiting for transfers between devices, body(): lax.all_to_all(packed, 'seq', split_axis=1, concat_axis=0, tiled=True)  139 us
    ppermute x2, waiting for transfers between devices, padded_2(): lax.ppermute(head, axis, [((i + 1) % count, i) for i in range(ends)])  128 us
    all_to_all x1, starting transfers between devices, body(): lax.all_to_all(packed, 'seq', split_axis=1, concat_axis=0, tiled=True)  28.6 us
    ppermute x2, starting transfers between devices, padded_2(): lax.ppermute(head, axis, [((i + 1) % count, i) for i in range(ends)])  20.5 us
    scatter-add x3, other arithmetic, one_group(): query_acc = query_acc.at[:, query_pick].add(query_part)  14.5 us
    scatter-add x3, other arithmetic, one_group(): cache_acc.at[:, key_pick]  14.5 us
  transfers between devices with their start and end apart: 6, of which 3 were waited for; matrix products, arithmetic and copies ran while one was open for 3% of the time, Pallas kernels for 0%

commit v1 on v0

v1 whole, which is shorter than its diff:
```python
import functools

import jax
import jax.numpy as jnp
from jax import lax
from jax.experimental import pallas as pl
from jax.experimental.pallas import tpu as pltpu
from jax.sharding import PartitionSpec as P

H = 32
HD = 64
BLK = 64
REACH = 4
NBR = 7
WIDTH = 2 * REACH + 1


def passed_along(value, axis, steps):
    count = lax.axis_size(axis)
    pairs = [(source, (source + steps) % count) for source in range(count)]
    return lax.ppermute(value, axis, pairs)


def to_right(value, axis):
    count = lax.axis_size(axis)
    return lax.ppermute(value, axis, [(i, i + 1) for i in range(count - 1)])


def to_left(value, axis):
    count = lax.axis_size(axis)
    return lax.ppermute(value, axis, [(i + 1, i) for i in range(count - 1)])


def band_kernel(mask_ref, q_ref, g_ref, kv_ref, lse_ref, dl_ref, qg_ref, cache_ref):
    blocks = q_ref.shape[0] // BLK
    win = WIDTH * BLK
    cache_ref[...] = jnp.zeros_like(cache_ref)
    row_block = lax.broadcasted_iota(jnp.int32, (win, HD), 0) // BLK

    def step(a, carry):
        r = pl.multiple_of(a * BLK, BLK)
        q = q_ref[pl.ds(r, BLK), :]
        g = g_ref[pl.ds(r, BLK), :]
        kw = kv_ref[pl.ds(r, win), pl.ds(0, HD)]
        vw = kv_ref[pl.ds(r, win), pl.ds(HD, HD)]
        lse = lse_ref[pl.ds(a, 1), :]
        dl = dl_ref[pl.ds(a, 1), :]
        live = jnp.zeros((win, HD), jnp.int32)
        for o in range(WIDTH):
            live = jnp.where(row_block == o, mask_ref[a * WIDTH + o], live)
        nt = (((1,), (1,)), ((), ()))
        st = lax.dot_general(kw, q, nt, preferred_element_type=jnp.float32) * (HD ** -0.5)
        wt = jnp.where(live != 0, jnp.exp(st - lse), 0.0)
        gwt = lax.dot_general(vw, g, nt, preferred_element_type=jnp.float32)
        gst = (wt * (gwt - dl)).astype(jnp.bfloat16)
        wht = wt.astype(jnp.bfloat16)
        tn = (((0,), (0,)), ((), ()))
        qg = lax.dot_general(gst, kw, tn, preferred_element_type=jnp.float32) * (HD ** -0.5)
        qg_ref[pl.ds(r, BLK), :] = qg.astype(qg_ref.dtype)
        kt = jnp.dot(gst, q, preferred_element_type=jnp.float32) * (HD ** -0.5)
        vt = jnp.dot(wht, g, preferred_element_type=jnp.float32)
        cache_ref[pl.ds(r, win), pl.ds(0, HD)] += kt
        cache_ref[pl.ds(r, win), pl.ds(HD, HD)] += vt
        return carry

    lax.fori_loop(0, blocks, step, 0)


def band_grads(mask, q, g, kv_pad, lse, dl):
    rows = q.shape[0]
    blocks = rows // BLK
    pad_rows = kv_pad.shape[0]
    flops = blocks * 5 * 2 * BLK * WIDTH * BLK * HD
    vmem = pl.BlockSpec(memory_space=pltpu.VMEM)
    return pl.pallas_call(
        band_kernel,
        out_shape=(
            jax.ShapeDtypeStruct((rows, HD), jnp.bfloat16),
            jax.ShapeDtypeStruct((pad_rows, 2 * HD), jnp.float32),
        ),
        in_specs=[pl.BlockSpec(memory_space=pltpu.SMEM)] + [vmem] * 5,
        out_specs=(vmem, vmem),
        cost_estimate=pl.CostEstimate(
            flops=flops,
            transcendentals=blocks * WIDTH * BLK * BLK,
            bytes_accessed=rows * HD * 2 * 3 + pad_rows * 2 * HD * 6 + rows * 8,
        ),
    )(mask, q, g, kv_pad, lse, dl)


def body(upstream, queries, attention_out, keys_values, log_totals, neighbours):
    tokens_here = queries.shape[2]
    incoming = passed_along(upstream, "pipe", -1)
    query_tok = queries.reshape(tokens_here, H, HD)
    grad_tok = incoming.reshape(tokens_here, H, HD)
    out_tok = attention_out.reshape(tokens_here, H, HD)
    delta_tok = jnp.sum(grad_tok.astype(jnp.float32) * out_tok.astype(jnp.float32), axis=2)
    query_h = lax.all_to_all(query_tok, "seq", split_axis=1, concat_axis=0, tiled=True)
    grad_h = lax.all_to_all(grad_tok, "seq", split_axis=1, concat_axis=0, tiled=True)
    delta_h = lax.all_to_all(delta_tok, "seq", split_axis=1, concat_axis=0, tiled=True)
    rows_here = query_h.shape[0]
    blocks_here = rows_here // BLK
    query_h = query_h.reshape(rows_here, HD)
    grad_h = grad_h.reshape(rows_here, HD)
    delta_b = delta_h.reshape(blocks_here, BLK)
    lse_b = log_totals.reshape(blocks_here, BLK)
    cache = keys_values.reshape(rows_here, 2 * HD)
    rim = REACH * BLK
    left_halo = to_right(cache[rows_here - rim :], "tp")
    right_halo = to_left(cache[:rim], "tp")
    kv_pad = jnp.concatenate([left_halo, cache, right_halo], axis=0)

    first_block = lax.axis_index("tp") * blocks_here
    listed = lax.dynamic_slice_in_dim(neighbours, first_block, blocks_here, 0)
    own = first_block + jnp.arange(blocks_here, dtype=jnp.int32)
    offset = listed - own[:, None] + REACH
    live = (listed >= 0)[:, :, None] & (offset[:, :, None] == jnp.arange(WIDTH, dtype=jnp.int32)[None, None, :])
    mask = jnp.any(live, axis=1).astype(jnp.int32).reshape(-1)

    query_grad, cache_pad = band_grads(mask, query_h, grad_h, kv_pad, lse_b, delta_b)
    from_right = to_left(cache_pad[:rim], "tp")
    from_left = to_right(cache_pad[rim + rows_here :], "tp")
    own_part = cache_pad[rim : rim + rows_here]
    own_part = jnp.concatenate(
        [
            own_part[:rim] + from_left,
            own_part[rim : rows_here - rim],
            own_part[rows_here - rim :] + from_right,
        ],
        axis=0,
    )
    query_grad = query_grad.reshape(1, 1, 1, rows_here, HD)
    cache_grad = own_part.astype(jnp.bfloat16).reshape(1, 1, 1, rows_here, 2 * HD)
    return (query_grad, cache_grad)


def solution(mesh):
    placed = (
        P("pipe", "tp", "seq", None),
        P("pipe", "tp", "seq", None),
        P("pipe", "tp", "seq", None),
        P("pipe", "tp", "seq", None, None),
        P("pipe", "tp", "seq", None),
        P(),
    )
    return jax.shard_map(
        body,
        mesh=mesh,
        in_specs=placed,
        out_specs=(P("pipe", "tp", "seq", None, None), P("pipe", "tp", "seq", None, None)),
        check_vma=False,
    )
```

time: 418 us -> 253 us (0.61)
  the two profiles are of different devices: /device:TPU:19 before, /device:TPU:26 now
where the time goes in v1:
time: 253 us; the launch traced here: 252 us
  waiting for transfers between devices  88 us (35%)
  blocking collectives  68.9 us (27%)
  starting transfers between devices  44.1 us (17%)
  Pallas kernels  32.3 us (13%)
  local copies, waits for them, and re-layouts  11.3 us (4%)
  other arithmetic  6.67 us (3%)
    all_to_all x1, blocking collectives, body(): lax.all_to_all(query_tok, 'seq', split_axis=1, concat_axis=0, tiled=True)  68.9 us
    all_to_all x1, waiting for transfers between devices, body(): lax.all_to_all(grad_tok, 'seq', split_axis=1, concat_axis=0, tiled=True)  53.7 us
    pallas_call x1, Pallas kernels, band_grads(): pl.pallas_call(band_kernel, out_shape=(jax.ShapeDtypeStruct((rows, HD), j...  32.3 us
    all_to_all x1, starting transfers between devices, body(): lax.all_to_all(delta_tok, 'seq', split_axis=1, concat_axis=0, tiled=True)  28.9 us
    all_to_all x1, waiting for transfers between devices, body(): lax.all_to_all(delta_tok, 'seq', split_axis=1, concat_axis=0, tiled=True)  22 us
    ppermute x2, starting transfers between devices, to_right(): return lax.ppermute(value, axis, [(i, i + 1) for i in range(count - 1)])  6.8 us
    ppermute x1, waiting for transfers between devices, passed_along(): return lax.ppermute(value, axis, pairs)  5.43 us
  transfers between devices with their start and end apart: 7, of which 6 were waited for; matrix products, arithmetic and copies ran while one was open for 4% of the time, Pallas kernels for 0%

profile of v1, /device:TPU:26, one launch (start us, length us, event | category | flops | bytes accessed | tf_op | source)
XLA Modules:
  0.0 252.1 jit_solution(11366081864231582741)
XLA Ops:
  0.6 1.3 copy.32
  2.2 1.3 copy.34
  3.4 5.4 %collective-permute-done = bf16[1,1,96,2048]{2,3,1,0:T(8,128)(2,1)} collective-permute-done((bf16[1,1,96,2048]{2,3,1,0:T(8,128)(2,1)S(1)}, bf16[1,1,96,2048]{2,3,1,0:T(8,128)(2,1)}, u32[]{:S(2)}, u32[]{:S(2)}) %collective-permute-start) | collective-permute-done | bytes 393248 | tf_op jit(solution)/shard_map/ppermute | solution.py:21
  8.9 1.9 fusion
  10.8 28.9 %all-to-all-start.2 = ((f32[96,32,1]{0,2,1:T(1,128)}), f32[96,32,1]{0,2,1:T(1,128)S(1)}, u32[]{:S(2)}, u32[]{:S(2)}) async-start(f32[96,32,1]{0,2,1:T(1,128)} %bitcast.12), calls=%async_computation.2 | async-start | bytes 32768 | tf_op jit(solution)/shard_map/all_to_all | solution.py:100
  39.7 0.3 copy.30
  40.0 22.0 %all-to-all-done.2 = f32[96,32,1]{0,2,1:T(1,128)S(1)} async-done(((f32[96,32,1]{0,2,1:T(1,128)}), f32[96,32,1]{0,2,1:T(1,128)S(1)}, u32[]{:S(2)}, u32[]{:S(2)}) %all-to-all-start.2) | async-done | bytes 12320 | tf_op jit(solution)/shard_map/all_to_all | solution.py:100
  62.0 68.9 %all_to_all.46 = bf16[96,32,64]{0,2,1:T(8,128)(2,1)S(1)} all-to-all(bf16[96,32,64]{0,2,1:T(8,128)(2,1)S(1)} %bitcast.27), channel_id=1, replica_groups=mesh['pipe'=8,'seq'=32,'tp'=4] {'seq'}, dimensions={1} | all-to-all | bytes 786432 | tf_op jit(solution)/shard_map/all_to_all | solution.py:98
  130.9 3.9 %all-to-all-start.1 = ((bf16[96,32,64]{0,2,1:T(8,128)(2,1)}), bf16[96,32,64]{0,2,1:T(8,128)(2,1)S(1)}, u32[]{:S(2)}, u32[]{:S(2)}) async-start(bf16[96,32,64]{0,2,1:T(8,128)(2,1)} %bitcast.4), calls=%async_computation.1 | async-start | bytes 1048576 | tf_op jit(solution)/shard_map/all_to_all | solution.py:99
  134.8 3.4 %collective-permute-start.1 = (bf16[256,128]{1,0:T(8,128)(2,1)S(1)}, bf16[256,128]{1,0:T(8,128)(2,1)S(1)}, u32[]{:S(2)}, u32[]{:S(2)}) collective-permute-start(bf16[256,128]{1,0:T(8,128)(2,1)S(1)} %get-tuple-element.16), channel_id=1, source_target_pairs={{0,1},{1,2},{2,3},{4,5},{5,6},{6,7},{8,9},{9,10},{10,11},{12,13},{... | collective-permute-start | bytes 196616 | tf_op jit(solution)/shard_map/ppermute | solution.py:26
  138.2 2.4 collective-permute-start.2
  140.9 0.5 broadcast.12
  141.4 0.7 reduce.7
  142.1 0.7 reshape.100.lse_ref
  142.9 0.7 reshape.103.mask_ref
  143.6 0.8 collective-permute-done.2
  144.4 1.0 pad_maximum_fusion.kv_ref
  145.5 0.7 reshape.101.dl_ref
  146.2 1.2 copy.31
  147.3 53.7 %all-to-all-done.1 = bf16[96,32,64]{0,2,1:T(8,128)(2,1)S(1)} async-done(((bf16[96,32,64]{0,2,1:T(8,128)(2,1)}), bf16[96,32,64]{0,2,1:T(8,128)(2,1)S(1)}, u32[]{:S(2)}, u32[]{:S(2)}) %all-to-all-start.1) | async-done | bytes 393248 | tf_op jit(solution)/shard_map/all_to_all | solution.py:99
  201.1 1.2 copy.33
  202.2 32.3 %shard_map.77 = (bf16[3072,64]{1,0:T(8,128)(2,1)}, f32[3584,128]{1,0:T(8,128)}) custom-call(s32[432]{0:T(512)} %reshape.103.mask_ref, bf16[3072,64]{1,0:T(8,128)(2,1)} %bitcast.33, bf16[3072,64]{1,0:T(8,128)(2,1)} %bitcast.34, bf16[3584,128]{1,0:T(8,128)(2,1)} %pad_maximum_fusion.kv_ref, f32[48,64]{1,0:T(8,128)} %reshape.100.lse_ref, f32[48,64]{1,0:T(8,128)} %reshape.101.dl_ref), custom_call_target="tpu_custom_call" | custom-call | flops 1132462080 | bytes 3956736 | tf_op jit(solution)/shard_map/pallas_call | solution.py:75
  234.5 1.0 slice.37
  235.5 3.4 %collective-permute-start.3 = (f32[256,128]{1,0:T(8,128)S(1)}, f32[256,128]{1,0:T(8,128)S(1)}, u32[]{:S(2)}, u32[]{:S(2)}) collective-permute-start(f32[256,128]{1,0:T(8,128)S(1)} %slice.37), channel_id=1, source_target_pairs={{0,1},{1,2},{2,3},{4,5},{5,6},{6,7},{8,9},{9,10},{10,11},{12,13},{... | collective-permute-start | bytes 393224 | tf_op jit(solution)/shard_map/ppermute | solution.py:26
  238.9 3.5 %collective-permute-done.3 = f32[256,128]{1,0:T(8,128)S(1)} collective-permute-done((f32[256,128]{1,0:T(8,128)S(1)}, f32[256,128]{1,0:T(8,128)S(1)}, u32[]{:S(2)}, u32[]{:S(2)}) %collective-permute-start.3) | collective-permute-done | bytes 131104 | tf_op jit(solution)/shard_map/ppermute | solution.py:26
  242.3 1.0 fusion.2
  243.3 1.9 collective-permute-start.4
  245.3 1.4 fusion.1
  246.7 1.0 copy.35
  247.7 2.5 %collective-permute-done.4 = f32[256,128]{1,0:T(8,128)S(1)} collective-permute-done((f32[256,128]{1,0:T(8,128)S(1)}, f32[256,128]{1,0:T(8,128)S(1)}, u32[]{:S(2)}, u32[]{:S(2)}) %collective-permute-start.4) | collective-permute-done | bytes 131104 | tf_op jit(solution)/shard_map/ppermute | solution.py:31
  250.2 0.9 fusion.3
  251.1 0.9 pad_maximum_fusion.1
  (20 shorter events, 0.6 us)
Async XLA Ops:
  0.6 39.1 %copy-start.2 = (bf16[1,1,96,2048]{3,2,1,0:T(8,128)(2,1)S(1)}, bf16[1,1,96,2048]{3,2,1,0:T(8,128)(2,1)}, u32[]{:S(2)}) copy-start(bf16[1,1,96,2048]{3,2,1,0:T(8,128)(2,1)} %param.7) | copy-start | bytes 1179652
  2.0 6.9 %collective-permute-start = (bf16[1,1,96,2048]{2,3,1,0:T(8,128)(2,1)S(1)}, bf16[1,1,96,2048]{2,3,1,0:T(8,128)(2,1)}, u32[]{:S(2)}, u32[]{:S(2)}) collective-permute-start(bf16[1,1,96,2048]{2,3,1,0:T(8,128)(2,1)S(1)} %copy.32), channel_id=1, source_target_pairs={{0,896},{128,0},{256,128},{384,256},{512,384},{640,512},{768,640},... | collective-permute-start | bytes 1179656 | tf_op jit(solution)/shard_map/ppermute | solution.py:21
  8.9 125.9 %copy-start = (bf16[1,1,1,3072,128]{4,3,2,1,0:T(8,128)(2,1)S(1)}, bf16[1,1,1,3072,128]{4,3,2,1,0:T(8,128)(2,1)}, u32[]{:S(2)}) copy-start(bf16[1,1,1,3072,128]{4,3,2,1,0:T(8,128)(2,1)} %param.9) | copy-start | bytes 2359300
  10.8 129.9 %copy-start.4 = (s32[192,7]{0,1:T(8,128)S(1)}, s32[192,7]{0,1:T(8,128)}, u32[]{:S(2)}) copy-start(s32[192,7]{0,1:T(8,128)} %param.11) | copy-start | bytes 16132
  10.8 130.6 %copy-start.3 = (f32[1,1,1,3072]{3,2,1,0:T(1,128)S(1)}, f32[1,1,1,3072]{3,2,1,0:T(1,128)}, u32[]{:S(2)}) copy-start(f32[1,1,1,3072]{3,2,1,0:T(1,128)} %param.10) | copy-start | bytes 36868
  10.8 51.2 %all-to-all-start.2 = ((f32[96,32,1]{0,2,1:T(1,128)}), f32[96,32,1]{0,2,1:T(1,128)S(1)}, u32[]{:S(2)}, u32[]{:S(2)}) async-start(f32[96,32,1]{0,2,1:T(1,128)} %bitcast.12), calls=%async_computation.2 | async-start | bytes 32768 | tf_op jit(solution)/shard_map/all_to_all | solution.py:100
  130.9 70.2 %all-to-all-start.1 = ((bf16[96,32,64]{0,2,1:T(8,128)(2,1)}), bf16[96,32,64]{0,2,1:T(8,128)(2,1)S(1)}, u32[]{:S(2)}, u32[]{:S(2)}) async-start(bf16[96,32,64]{0,2,1:T(8,128)(2,1)} %bitcast.4), calls=%async_computation.1 | async-start | bytes 1048576 | tf_op jit(solution)/shard_map/all_to_all | solution.py:99
  134.8 8.8 %collective-permute-start.1 = (bf16[256,128]{1,0:T(8,128)(2,1)S(1)}, bf16[256,128]{1,0:T(8,128)(2,1)S(1)}, u32[]{:S(2)}, u32[]{:S(2)}) collective-permute-start(bf16[256,128]{1,0:T(8,128)(2,1)S(1)} %get-tuple-element.16), channel_id=1, source_target_pairs={{0,1},{1,2},{2,3},{4,5},{5,6},{6,7},{8,9},{9,10},{10,11},{12,13},{... | collective-permute-start | bytes 196616 | tf_op jit(solution)/shard_map/ppermute | solution.py:26
  138.2 6.2 %collective-permute-start.2 = (bf16[256,128]{1,0:T(8,128)(2,1)S(1)}, bf16[256,128]{1,0:T(8,128)(2,1)S(1)}, u32[]{:S(2)}, u32[]{:S(2)}) collective-permute-start(bf16[256,128]{1,0:T(8,128)(2,1)S(1)} %get-tuple-element.17), channel_id=1, source_target_pairs={{1,0},{2,1},{3,2},{5,4},{6,5},{7,6},{9,8},{10,9},{11,10},{13,12},{... | collective-permute-start | bytes 196616 | tf_op jit(solution)/shard_map/ppermute | solution.py:31
  234.5 12.2 %copy-start.1 = (bf16[3072,64]{1,0:T(8,128)(2,1)S(1)}, bf16[3072,64]{1,0:T(8,128)(2,1)}, u32[]{:S(2)}) copy-start(bf16[3072,64]{1,0:T(8,128)(2,1)} %get-tuple-element.4) | copy-start | bytes 1179652
  235.5 6.9 %collective-permute-start.3 = (f32[256,128]{1,0:T(8,128)S(1)}, f32[256,128]{1,0:T(8,128)S(1)}, u32[]{:S(2)}, u32[]{:S(2)}) collective-permute-start(f32[256,128]{1,0:T(8,128)S(1)} %slice.37), channel_id=1, source_target_pairs={{0,1},{1,2},{2,3},{4,5},{5,6},{6,7},{8,9},{9,10},{10,11},{12,13},{... | collective-permute-start | bytes 393224 | tf_op jit(solution)/shard_map/ppermute | solution.py:26
  243.3 6.9 %collective-permute-start.4 = (f32[256,128]{1,0:T(8,128)S(1)}, f32[256,128]{1,0:T(8,128)S(1)}, u32[]{:S(2)}, u32[]{:S(2)}) collective-permute-start(f32[256,128]{1,0:T(8,128)S(1)} %get-tuple-element.15), channel_id=1, source_target_pairs={{1,0},{2,1},{3,2},{5,4},{6,5},{7,6},{9,8},{10,9},{11,10},{13,12},{... | collective-permute-start | bytes 393224 | tf_op jit(solution)/shard_map/ppermute | solution.py:31

commit v2 on v1

v2 whole, which is shorter than its diff:
```python
import functools

import jax
import jax.numpy as jnp
from jax import lax
from jax.experimental import pallas as pl
from jax.experimental.pallas import tpu as pltpu
from jax.sharding import PartitionSpec as P

H = 32
HD = 64
BLK = 64
REACH = 4
NBR = 7
WIDTH = 2 * REACH + 1


def passed_along(value, axis, steps):
    count = lax.axis_size(axis)
    pairs = [(source, (source + steps) % count) for source in range(count)]
    return lax.ppermute(value, axis, pairs)


def to_right(value, axis):
    count = lax.axis_size(axis)
    return lax.ppermute(value, axis, [(i, i + 1) for i in range(count - 1)])


def to_left(value, axis):
    count = lax.axis_size(axis)
    return lax.ppermute(value, axis, [(i + 1, i) for i in range(count - 1)])


def band_kernel(rz_ref, kv_ref, live_ref, lse_ref, dl_ref, qg_ref, cache_ref):
    steps = rz_ref.shape[0]
    span = 2 * BLK
    win = (WIDTH + 1) * BLK
    cache_ref[...] = jnp.zeros_like(cache_ref)

    def step(i, carry):
        r = pl.multiple_of(i * span, span)
        rz = rz_ref[i]
        kvw = kv_ref[pl.ds(r, win), :]
        nt = (((1,), (1,)), ((), ()))
        both = lax.dot_general(kvw, rz, nt, preferred_element_type=jnp.float32)
        live = jnp.broadcast_to(live_ref[i][:, None, :], (WIDTH + 1, BLK, span)).reshape(win, span)
        lse = lse_ref[pl.ds(i, 1), :]
        dl = dl_ref[pl.ds(i, 1), :]
        wt = jnp.where(live != 0, jnp.exp(both[:, :span] - lse), 0.0)
        gst = (wt * (both[:, span:] - dl)).astype(jnp.bfloat16)
        wht = wt.astype(jnp.bfloat16)
        terms = jnp.dot(
            jnp.concatenate([gst, wht], axis=1), rz, preferred_element_type=jnp.float32
        )
        cache_ref[pl.ds(r, win), :] += terms
        tn = (((0,), (0,)), ((), ()))
        qg = lax.dot_general(gst, kvw, tn, preferred_element_type=jnp.float32)
        qg_ref[pl.ds(r, span), :] = (qg[:, :HD] * (HD ** -0.5)).astype(qg_ref.dtype)
        return carry

    lax.fori_loop(0, steps, step, 0)


def band_grads(rz, kv_pad, live, lse, dl):
    steps = rz.shape[0]
    rows = steps * 2 * BLK
    pad_rows = kv_pad.shape[0]
    win = (WIDTH + 1) * BLK
    flops = steps * 3 * 2 * win * 256 * 128
    vmem = pl.BlockSpec(memory_space=pltpu.VMEM)
    return pl.pallas_call(
        band_kernel,
        out_shape=(
            jax.ShapeDtypeStruct((rows, HD), jnp.bfloat16),
            jax.ShapeDtypeStruct((pad_rows, 2 * HD), jnp.float32),
        ),
        in_specs=[vmem] * 5,
        out_specs=(vmem, vmem),
        cost_estimate=pl.CostEstimate(
            flops=flops,
            transcendentals=steps * win * 128,
            bytes_accessed=rz.size * 2 + pad_rows * 128 * 10 + rows * 10,
        ),
    )(rz, kv_pad, live, lse, dl)


def split3(x):
    hi = lax.reduce_precision(x, exponent_bits=8, mantissa_bits=7)
    rest = x - hi
    mid = lax.reduce_precision(rest, exponent_bits=8, mantissa_bits=7)
    lo = rest - mid
    return jnp.stack([hi, mid, lo], axis=1).astype(jnp.bfloat16)


def local_grads(query_h, grad_h, delta_h, lse_h, kv_pad, listed, first_block):
    rows_here = query_h.shape[0]
    blocks_here = rows_here // BLK
    steps = blocks_here // 2
    lane = 128
    delta_h = delta_h.reshape(steps, 2 * BLK)
    lse_h = lse_h.reshape(steps, 2 * BLK)
    zeros = jnp.zeros((rows_here, HD), jnp.bfloat16)
    top = jnp.concatenate([query_h * jnp.bfloat16(HD ** -0.5), zeros], axis=1)
    bottom = jnp.concatenate([zeros, grad_h], axis=1)
    rz = jnp.concatenate(
        [top.reshape(steps, 2 * BLK, lane), bottom.reshape(steps, 2 * BLK, lane)], axis=1
    )
    own = first_block + jnp.arange(blocks_here, dtype=jnp.int32)
    offset = listed - own[:, None] + REACH
    hit = (listed >= 0)[:, :, None] & (offset[:, :, None] == jnp.arange(WIDTH, dtype=jnp.int32)[None, None, :])
    mask = jnp.any(hit, axis=1).astype(jnp.int32).reshape(steps, 2, WIDTH)
    first_half = jnp.pad(mask[:, 0], ((0, 0), (0, 1)))
    second_half = jnp.pad(mask[:, 1], ((0, 0), (1, 0)))
    live = jnp.concatenate(
        [
            jnp.broadcast_to(first_half[:, :, None], (steps, WIDTH + 1, BLK)),
            jnp.broadcast_to(second_half[:, :, None], (steps, WIDTH + 1, BLK)),
        ],
        axis=2,
    )
    return band_grads(rz, kv_pad, live, lse_h, delta_h)


def body(upstream, queries, attention_out, keys_values, log_totals, neighbours):
    tokens_here = queries.shape[2]
    heads = lax.axis_size("seq")
    incoming = passed_along(upstream, "pipe", -1)
    query_tok = queries.reshape(tokens_here, H, HD)
    grad_tok = incoming.reshape(tokens_here, H, HD)
    out_tok = attention_out.reshape(tokens_here, H, HD)
    delta_tok = jnp.sum(grad_tok.astype(jnp.float32) * out_tok.astype(jnp.float32), axis=2)
    lane = 128
    part_rows = tokens_here * HD // lane
    d_vals = 3 * tokens_here
    d_rows = -(-d_vals // (16 * lane)) * 16
    delta_parts = split3(jnp.transpose(delta_tok)).reshape(H, d_vals)
    delta_parts = jnp.pad(delta_parts, ((0, 0), (0, d_rows * lane - d_vals)))
    send = jnp.concatenate(
        [
            jnp.transpose(query_tok, (1, 0, 2)).reshape(H, part_rows, lane),
            jnp.transpose(grad_tok, (1, 0, 2)).reshape(H, part_rows, lane),
            delta_parts.reshape(H, d_rows, lane),
        ],
        axis=1,
    )
    got = lax.all_to_all(send, "seq", split_axis=0, concat_axis=0, tiled=True)
    rows_here = heads * tokens_here
    blocks_here = rows_here // BLK
    query_h = got[:, :part_rows].reshape(rows_here, HD)
    grad_h = got[:, part_rows : 2 * part_rows].reshape(rows_here, HD)
    d3 = got[:, 2 * part_rows :].reshape(heads, d_rows * lane)[:, :d_vals]
    d3 = d3.reshape(heads, 3, tokens_here).astype(jnp.float32)
    delta_h = ((d3[:, 0] + d3[:, 1]) + d3[:, 2]).reshape(rows_here)
    cache = keys_values.reshape(rows_here, 2 * HD)
    rim = REACH * BLK
    left_halo = to_right(cache[rows_here - rim :], "tp")
    right_halo = to_left(cache[:rim], "tp")
    kv_pad = jnp.concatenate([left_halo, cache, right_halo], axis=0)
    first_block = lax.axis_index("tp") * blocks_here
    listed = lax.dynamic_slice_in_dim(neighbours, first_block, blocks_here, 0)
    query_grad, cache_pad = local_grads(
        query_h, grad_h, delta_h, log_totals.reshape(rows_here), kv_pad, listed, first_block
    )
    from_right = to_left(cache_pad[:rim], "tp")
    from_left = to_right(cache_pad[rim + rows_here :], "tp")
    own_part = cache_pad[rim : rim + rows_here]
    own_part = jnp.concatenate(
        [
            own_part[:rim] + from_left,
            own_part[rim : rows_here - rim],
            own_part[rows_here - rim :] + from_right,
        ],
        axis=0,
    )
    query_grad = query_grad.reshape(1, 1, 1, rows_here, HD)
    cache_grad = own_part.astype(jnp.bfloat16).reshape(1, 1, 1, rows_here, 2 * HD)
    return (query_grad, cache_grad)


def solution(mesh):
    placed = (
        P("pipe", "tp", "seq", None),
        P("pipe", "tp", "seq", None),
        P("pipe", "tp", "seq", None),
        P("pipe", "tp", "seq", None, None),
        P("pipe", "tp", "seq", None),
        P(),
    )
    return jax.shard_map(
        body,
        mesh=mesh,
        in_specs=placed,
        out_specs=(P("pipe", "tp", "seq", None, None), P("pipe", "tp", "seq", None, None)),
        check_vma=False,
    )
```

time: 253 us -> 175 us (0.69)
  the two profiles are of different devices: /device:TPU:26 before, /device:TPU:2 now
where the time goes in v2:
time: 175 us
  waiting for transfers between devices  98 us (56%)
  starting transfers between devices  42.4 us (24%)
  Pallas kernels  15.6 us (9%)
  local copies, waits for them, and re-layouts  10.1 us (6%)
  other arithmetic  7.5 us (4%)
    all_to_all x1, waiting for transfers between devices, body(): got = lax.all_to_all(send, 'seq', split_axis=0, concat_axis=0, tiled=True)  85.4 us
    all_to_all x1, starting transfers between devices, body(): got = lax.all_to_all(send, 'seq', split_axis=0, concat_axis=0, tiled=True)  28.7 us
    pallas_call x1, Pallas kernels, band_grads(): pl.pallas_call(band_kernel, out_shape=(jax.ShapeDtypeStruct((rows, HD), j...  15.6 us
    ppermute x2, starting transfers between devices, to_right(): return lax.ppermute(value, axis, [(i, i + 1) for i in range(count - 1)])  6.8 us
    ppermute x2, waiting for transfers between devices, to_left(): return lax.ppermute(value, axis, [(i + 1, i) for i in range(count - 1)])  4.76 us
    ppermute x1, waiting for transfers between devices, passed_along(): return lax.ppermute(value, axis, pairs)  4.41 us
    ppermute x2, starting transfers between devices, to_left(): return lax.ppermute(value, axis, [(i + 1, i) for i in range(count - 1)])  4.36 us
    unnamed x15, local copies, waits for them, and re-layouts  3.91 us
  transfers between devices with their start and end apart: 6, of which 5 were waited for; matrix products, arithmetic and copies ran while one was open for 4% of the time, Pallas kernels for 0%

profile of v2, /device:TPU:2, one launch (start us, length us, event | category | flops | bytes accessed | tf_op | source)
XLA Modules:
  0.0 174.5 jit_solution(11690355386813964991)
XLA Ops:
  0.6 1.3 copy.24
  1.9 2.5 %collective-permute-start = (bf16[1,1,96,2048]{2,3,1,0:T(8,128)(2,1)S(1)}, bf16[1,1,96,2048]{2,3,1,0:T(8,128)(2,1)S(1)}, u32[]{:S(2)}, u32[]{:S(2)}) collective-permute-start(bf16[1,1,96,2048]{2,3,1,0:T(8,128)(2,1)S(1)} %copy.24), channel_id=1, source_target_pairs={{0,896},{128,0},{256,128},{384,256},{512,384},{640,512},{768,640},... | collective-permute-start | bytes 1179656 | tf_op jit(solution)/shard_map/ppermute | solution.py:21
  4.4 1.3 copy.22
  5.7 0.4 copy.23
  6.0 0.3 reshape.115
  6.7 4.4 %collective-permute-done = bf16[1,1,96,2048]{2,3,1,0:T(8,128)(2,1)S(1)} collective-permute-done((bf16[1,1,96,2048]{2,3,1,0:T(8,128)(2,1)S(1)}, bf16[1,1,96,2048]{2,3,1,0:T(8,128)(2,1)S(1)}, u32[]{:S(2)}, u32[]{:S(2)}) %collective-permute-start) | collective-permute-done | bytes 393248 | tf_op jit(solution)/shard_map/ppermute | solution.py:21
  11.5 0.4 copy.25
  11.9 0.3 reshape.117
  12.3 1.0 pad_maximum_fusion.1
  13.3 28.7 %all-to-all-start = ((bf16[32,112,128]{2,1,0:T(8,128)(2,1)}), bf16[32,112,128]{2,1,0:T(8,128)(2,1)S(1)}, u32[]{:S(2)}, u32[]{:S(2)}) async-start(bf16[32,112,128]{2,1,0:T(8,128)(2,1)} %pad_maximum_fusion.1), calls=%async_computation | async-start | bytes 1835008 | tf_op jit(solution)/shard_map/all_to_all | solution.py:146
  42.0 3.4 %collective-permute-start.1 = (bf16[256,128]{1,0:T(8,128)(2,1)S(1)}, bf16[256,128]{1,0:T(8,128)(2,1)S(1)}, u32[]{:S(2)}, u32[]{:S(2)}) collective-permute-start(bf16[256,128]{1,0:T(8,128)(2,1)S(1)} %get-tuple-element.16), channel_id=1, source_target_pairs={{0,1},{1,2},{2,3},{4,5},{5,6},{6,7},{8,9},{9,10},{10,11},{12,13},{... | collective-permute-start | bytes 196616 | tf_op jit(solution)/shard_map/ppermute | solution.py:26
  45.4 2.4 %collective-permute-start.2 = (bf16[256,128]{1,0:T(8,128)(2,1)S(1)}, bf16[256,128]{1,0:T(8,128)(2,1)S(1)}, u32[]{:S(2)}, u32[]{:S(2)}) collective-permute-start(bf16[256,128]{1,0:T(8,128)(2,1)S(1)} %get-tuple-element.17), channel_id=1, source_target_pairs={{1,0},{2,1},{3,2},{5,4},{6,5},{7,6},{9,8},{10,9},{11,10},{13,12},{... | collective-permute-start | bytes 196616 | tf_op jit(solution)/shard_map/ppermute | solution.py:31
  48.6 0.8 pad_add_fusion.live_ref
  49.4 2.2 %collective-permute-done.2 = bf16[256,128]{1,0:T(8,128)(2,1)S(1)} collective-permute-done((bf16[256,128]{1,0:T(8,128)(2,1)S(1)}, bf16[256,128]{1,0:T(8,128)(2,1)S(1)}, u32[]{:S(2)}, u32[]{:S(2)}) %collective-permute-start.2) | collective-permute-done | bytes 65568 | tf_op jit(solution)/shard_map/ppermute | solution.py:31
  51.6 1.0 pad_maximum_fusion.2.kv_ref
  52.6 85.4 %all-to-all-done = bf16[32,112,128]{2,1,0:T(8,128)(2,1)S(1)} async-done(((bf16[32,112,128]{2,1,0:T(8,128)(2,1)}), bf16[32,112,128]{2,1,0:T(8,128)(2,1)S(1)}, u32[]{:S(2)}, u32[]{:S(2)}) %all-to-all-start) | async-done | bytes 917536 | tf_op jit(solution)/shard_map/all_to_all | solution.py:146
  138.2 0.7 add.54.dl_ref
  139.0 0.3 mul.22
  139.3 0.3 reshape.120
  139.8 0.3 concatenate.37
  140.1 1.3 pad_maximum_fusion.rz_ref
  141.4 15.6 %shard_map.77 = (bf16[3072,64]{1,0:T(8,128)(2,1)}, f32[3584,128]{1,0:T(8,128)}) custom-call(bf16[24,256,128]{2,1,0:T(8,128)(2,1)} %pad_maximum_fusion.rz_ref, bf16[3584,128]{1,0:T(8,128)(2,1)} %pad_maximum_fusion.2.kv_ref, s32[24,10,128]{2,1,0:T(8,128)} %pad_add_fusion.live_ref, f32[24,128]{1,0:T(8,128)} %bitcast.66, f32[24,128]{1,0:T(8,128)} %add.54.dl_ref), custom_call_target="tpu_custom_call" | custom-call | flops 3019898880 | bytes 6191104 | tf_op jit(solution)/shard_map/pallas_call | solution.py:71
  157.0 1.0 slice.73
  158.0 3.4 %collective-permute-start.3 = (f32[256,128]{1,0:T(8,128)S(1)}, f32[256,128]{1,0:T(8,128)S(1)}, u32[]{:S(2)}, u32[]{:S(2)}) collective-permute-start(f32[256,128]{1,0:T(8,128)S(1)} %slice.73), channel_id=1, source_target_pairs={{0,1},{1,2},{2,3},{4,5},{5,6},{6,7},{8,9},{9,10},{10,11},{12,13},{... | collective-permute-start | bytes 393224 | tf_op jit(solution)/shard_map/ppermute | solution.py:26
  161.4 3.5 %collective-permute-done.3 = f32[256,128]{1,0:T(8,128)S(1)} collective-permute-done((f32[256,128]{1,0:T(8,128)S(1)}, f32[256,128]{1,0:T(8,128)S(1)}, u32[]{:S(2)}, u32[]{:S(2)}) %collective-permute-start.3) | collective-permute-done | bytes 131104 | tf_op jit(solution)/shard_map/ppermute | solution.py:26
  164.8 1.0 fusion.2
  165.8 1.9 %collective-permute-start.4 = (f32[256,128]{1,0:T(8,128)S(1)}, f32[256,128]{1,0:T(8,128)S(1)}, u32[]{:S(2)}, u32[]{:S(2)}) collective-permute-start(f32[256,128]{1,0:T(8,128)S(1)} %get-tuple-element.13), channel_id=1, source_target_pairs={{1,0},{2,1},{3,2},{5,4},{6,5},{7,6},{9,8},{10,9},{11,10},{13,12},{... | collective-permute-start | bytes 393224 | tf_op jit(solution)/shard_map/ppermute | solution.py:31
  167.7 1.4 fusion.1
  169.1 1.0 copy.29
  170.1 2.5 %collective-permute-done.4 = f32[256,128]{1,0:T(8,128)S(1)} collective-permute-done((f32[256,128]{1,0:T(8,128)S(1)}, f32[256,128]{1,0:T(8,128)S(1)}, u32[]{:S(2)}, u32[]{:S(2)}) %collective-permute-start.4) | collective-permute-done | bytes 131104 | tf_op jit(solution)/shard_map/ppermute | solution.py:31
  172.7 0.9 fusion.3
  173.6 0.9 pad_maximum_fusion.3
  (36 shorter events, 1.7 us)
Async XLA Ops:
  1.9 4.5 %copy-start.2 = (bf16[1,1,96,2048]{3,2,1,0:T(8,128)(2,1)S(1)}, bf16[1,1,96,2048]{3,2,1,0:T(8,128)(2,1)}, u32[]{:S(2)}) copy-start(bf16[1,1,96,2048]{3,2,1,0:T(8,128)(2,1)} %param.8) | copy-start | bytes 1179652
  1.9 9.2 %collective-permute-start = (bf16[1,1,96,2048]{2,3,1,0:T(8,128)(2,1)S(1)}, bf16[1,1,96,2048]{2,3,1,0:T(8,128)(2,1)S(1)}, u32[]{:S(2)}, u32[]{:S(2)}) collective-permute-start(bf16[1,1,96,2048]{2,3,1,0:T(8,128)(2,1)S(1)} %copy.24), channel_id=1, source_target_pairs={{0,896},{128,0},{256,128},{384,256},{512,384},{640,512},{768,640},... | collective-permute-start | bytes 1179656 | tf_op jit(solution)/shard_map/ppermute | solution.py:21
  12.2 29.8 %copy-start = (bf16[1,1,1,3072,128]{4,3,2,1,0:T(8,128)(2,1)S(1)}, bf16[1,1,1,3072,128]{4,3,2,1,0:T(8,128)(2,1)}, u32[]{:S(2)}) copy-start(bf16[1,1,1,3072,128]{4,3,2,1,0:T(8,128)(2,1)} %param.9) | copy-start | bytes 2359300
  12.2 35.7 %copy-start.3 = (s32[192,7]{0,1:T(8,128)S(1)}, s32[192,7]{0,1:T(8,128)}, u32[]{:S(2)}) copy-start(s32[192,7]{0,1:T(8,128)} %param.11) | copy-start | bytes 16132
  13.3 124.7 %all-to-all-start = ((bf16[32,112,128]{2,1,0:T(8,128)(2,1)}), bf16[32,112,128]{2,1,0:T(8,128)(2,1)S(1)}, u32[]{:S(2)}, u32[]{:S(2)}) async-start(bf16[32,112,128]{2,1,0:T(8,128)(2,1)} %pad_maximum_fusion.1), calls=%async_computation | async-start | bytes 1835008 | tf_op jit(solution)/shard_map/all_to_all | solution.py:146
  42.0 7.3 %collective-permute-start.1 = (bf16[256,128]{1,0:T(8,128)(2,1)S(1)}, bf16[256,128]{1,0:T(8,128)(2,1)S(1)}, u32[]{:S(2)}, u32[]{:S(2)}) collective-permute-start(bf16[256,128]{1,0:T(8,128)(2,1)S(1)} %get-tuple-element.16), channel_id=1, source_target_pairs={{0,1},{1,2},{2,3},{4,5},{5,6},{6,7},{8,9},{9,10},{10,11},{12,13},{... | collective-permute-start | bytes 196616 | tf_op jit(solution)/shard_map/ppermute | solution.py:26
  45.4 6.2 %collective-permute-start.2 = (bf16[256,128]{1,0:T(8,128)(2,1)S(1)}, bf16[256,128]{1,0:T(8,128)(2,1)S(1)}, u32[]{:S(2)}, u32[]{:S(2)}) collective-permute-start(bf16[256,128]{1,0:T(8,128)(2,1)S(1)} %get-tuple-element.17), channel_id=1, source_target_pairs={{1,0},{2,1},{3,2},{5,4},{6,5},{7,6},{9,8},{10,9},{11,10},{13,12},{... | collective-permute-start | bytes 196616 | tf_op jit(solution)/shard_map/ppermute | solution.py:31
  157.0 12.2 %copy-start.1 = (bf16[3072,64]{1,0:T(8,128)(2,1)S(1)}, bf16[3072,64]{1,0:T(8,128)(2,1)}, u32[]{:S(2)}) copy-start(bf16[3072,64]{1,0:T(8,128)(2,1)} %get-tuple-element.4) | copy-start | bytes 1179652
  158.0 6.9 %collective-permute-start.3 = (f32[256,128]{1,0:T(8,128)S(1)}, f32[256,128]{1,0:T(8,128)S(1)}, u32[]{:S(2)}, u32[]{:S(2)}) collective-permute-start(f32[256,128]{1,0:T(8,128)S(1)} %slice.73), channel_id=1, source_target_pairs={{0,1},{1,2},{2,3},{4,5},{5,6},{6,7},{8,9},{9,10},{10,11},{12,13},{... | collective-permute-start | bytes 393224 | tf_op jit(solution)/shard_map/ppermute | solution.py:26
  165.8 6.9 %collective-permute-start.4 = (f32[256,128]{1,0:T(8,128)S(1)}, f32[256,128]{1,0:T(8,128)S(1)}, u32[]{:S(2)}, u32[]{:S(2)}) collective-permute-start(f32[256,128]{1,0:T(8,128)S(1)} %get-tuple-element.13), channel_id=1, source_target_pairs={{1,0},{2,1},{3,2},{5,4},{6,5},{7,6},{9,8},{10,9},{11,10},{13,12},{... | collective-permute-start | bytes 393224 | tf_op jit(solution)/shard_map/ppermute | solution.py:31

commit v3 on v2

--- a/solution.py
+++ b/solution.py
@@ -58,7 +58,7 @@
         qg_ref[pl.ds(r, span), :] = (qg[:, :HD] * (HD ** -0.5)).astype(qg_ref.dtype)
         return carry
 
-    lax.fori_loop(0, steps, step, 0)
+    lax.fori_loop(0, steps, step, 0, unroll=2)
 
 
 def band_grads(rz, kv_pad, live, lse, dl):
@@ -124,20 +124,21 @@
 def body(upstream, queries, attention_out, keys_values, log_totals, neighbours):
     tokens_here = queries.shape[2]
     heads = lax.axis_size("seq")
+    lane = 128
+    part_rows = tokens_here * HD // lane
+    query_tok = queries.reshape(tokens_here, H, HD)
+    query_send = jnp.transpose(query_tok, (1, 0, 2)).reshape(H, part_rows, lane)
+    query_got = lax.all_to_all(query_send, "seq", split_axis=0, concat_axis=0, tiled=True)
     incoming = passed_along(upstream, "pipe", -1)
-    query_tok = queries.reshape(tokens_here, H, HD)
     grad_tok = incoming.reshape(tokens_here, H, HD)
     out_tok = attention_out.reshape(tokens_here, H, HD)
     delta_tok = jnp.sum(grad_tok.astype(jnp.float32) * out_tok.astype(jnp.float32), axis=2)
-    lane = 128
-    part_rows = tokens_here * HD // lane
     d_vals = 3 * tokens_here
     d_rows = -(-d_vals // (16 * lane)) * 16
     delta_parts = split3(jnp.transpose(delta_tok)).reshape(H, d_vals)
     delta_parts = jnp.pad(delta_parts, ((0, 0), (0, d_rows * lane - d_vals)))
     send = jnp.concatenate(
         [
-            jnp.transpose(query_tok, (1, 0, 2)).reshape(H, part_rows, lane),
             jnp.transpose(grad_tok, (1, 0, 2)).reshape(H, part_rows, lane),
             delta_parts.reshape(H, d_rows, lane),
         ],
@@ -146,9 +147,9 @@
     got = lax.all_to_all(send, "seq", split_axis=0, concat_axis=0, tiled=True)
     rows_here = heads * tokens_here
     blocks_here = rows_here // BLK
-    query_h = got[:, :part_rows].reshape(rows_here, HD)
-    grad_h = got[:, part_rows : 2 * part_rows].reshape(rows_here, HD)
-    d3 = got[:, 2 * part_rows :].reshape(heads, d_rows * lane)[:, :d_vals]
+    query_h = query_got.reshape(rows_here, HD)
+    grad_h = got[:, :part_rows].reshape(rows_here, HD)
+    d3 = got[:, part_rows:].reshape(heads, d_rows * lane)[:, :d_vals]
     d3 = d3.reshape(heads, 3, tokens_here).astype(jnp.float32)
     delta_h = ((d3[:, 0] + d3[:, 1]) + d3[:, 2]).reshape(rows_here)
     cache = keys_values.reshape(rows_here, 2 * HD)

time: 175 us -> 188 us (1.074)
  the two profiles are of different devices: /device:TPU:2 before, /device:TPU:28 now
where the time goes in v3:
time: 188 us; the launch traced here: 187 us
  waiting for transfers between devices  112 us (60%)
  starting transfers between devices  44 us (23%)
  Pallas kernels  13.4 us (7%)
  local copies, waits for them, and re-layouts  9.94 us (5%)
  other arithmetic  7.32 us (4%)
    all_to_all x1, waiting for transfers between devices, body(): got = lax.all_to_all(send, 'seq', split_axis=0, concat_axis=0, tiled=True)  52.7 us
    all_to_all x1, waiting for transfers between devices, body(): lax.all_to_all(query_send, 'seq', split_axis=0, concat_axis=0, tiled=True)  44.7 us
    all_to_all x1, starting transfers between devices, body(): lax.all_to_all(query_send, 'seq', split_axis=0, concat_axis=0, tiled=True)  28.7 us
    pallas_call x1, Pallas kernels, band_grads(): pl.pallas_call(band_kernel, out_shape=(jax.ShapeDtypeStruct((rows, HD), j...  13.4 us
    ppermute x1, waiting for transfers between devices, passed_along(): return lax.ppermute(value, axis, pairs)  6.4 us
    ppermute x2, starting transfers between devices, to_right(): return lax.ppermute(value, axis, [(i, i + 1) for i in range(count - 1)])  6.21 us
    ppermute x2, starting transfers between devices, to_left(): return lax.ppermute(value, axis, [(i + 1, i) for i in range(count - 1)])  5.18 us
    ppermute x2, waiting for transfers between devices, to_left(): return lax.ppermute(value, axis, [(i + 1, i) for i in range(count - 1)])  3.94 us
  transfers between devices with their start and end apart: 7, of which 6 were waited for; matrix products, arithmetic and copies ran while one was open for 4% of the time, Pallas kernels for 0%

profile of v3, /device:TPU:28, one launch (start us, length us, event | category | flops | bytes accessed | tf_op | source)
XLA Modules:
  0.0 187.2 jit_solution(8813268720521850259)
XLA Ops:
  0.6 1.3 copy.22
  1.9 0.4 copy.23
  2.3 1.1 reshape.115
  3.4 28.7 %all-to-all-start = ((bf16[32,48,128]{2,1,0:T(8,128)(2,1)}), bf16[32,48,128]{2,1,0:T(8,128)(2,1)S(1)}, u32[]{:S(2)}, u32[]{:S(2)}) async-start(bf16[32,48,128]{2,1,0:T(8,128)(2,1)} %reshape.115), calls=%async_computation | async-start | bytes 786432 | tf_op jit(solution)/shard_map/all_to_all | solution.py:131
  32.7 6.4 %collective-permute-done = bf16[1,1,96,2048]{2,3,1,0:T(8,128)(2,1)S(1)} collective-permute-done((bf16[1,1,96,2048]{2,3,1,0:T(8,128)(2,1)S(1)}, bf16[1,1,96,2048]{2,3,1,0:T(8,128)(2,1)S(1)}, u32[]{:S(2)}, u32[]{:S(2)}) %collective-permute-start) | collective-permute-done | bytes 393248 | tf_op jit(solution)/shard_map/ppermute | solution.py:21
  39.6 0.4 copy.25
  40.0 0.3 reshape.118
  40.3 0.9 pad_maximum_fusion.3
  41.2 44.7 %all-to-all-done = bf16[32,48,128]{2,1,0:T(8,128)(2,1)S(1)} async-done(((bf16[32,48,128]{2,1,0:T(8,128)(2,1)}), bf16[32,48,128]{2,1,0:T(8,128)(2,1)S(1)}, u32[]{:S(2)}, u32[]{:S(2)}) %all-to-all-start) | async-done | bytes 393248 | tf_op jit(solution)/shard_map/all_to_all | solution.py:131
  85.9 3.9 %all-to-all-start.1 = ((bf16[32,64,128]{2,1,0:T(8,128)(2,1)}), bf16[32,64,128]{2,1,0:T(8,128)(2,1)S(1)}, u32[]{:S(2)}, u32[]{:S(2)}) async-start(bf16[32,64,128]{2,1,0:T(8,128)(2,1)} %pad_maximum_fusion.3), calls=%async_computation.1 | async-start | bytes 1048576 | tf_op jit(solution)/shard_map/all_to_all | solution.py:147
  89.8 3.1 %collective-permute-start.1 = (bf16[256,128]{1,0:T(8,128)(2,1)S(1)}, bf16[256,128]{1,0:T(8,128)(2,1)S(1)}, u32[]{:S(2)}, u32[]{:S(2)}) collective-permute-start(bf16[256,128]{1,0:T(8,128)(2,1)S(1)} %get-tuple-element.14), channel_id=1, source_target_pairs={{0,1},{1,2},{2,3},{4,5},{5,6},{6,7},{8,9},{9,10},{10,11},{12,13},{... | collective-permute-start | bytes 196616 | tf_op jit(solution)/shard_map/ppermute | solution.py:26
  92.9 2.7 %collective-permute-start.2 = (bf16[256,128]{1,0:T(8,128)(2,1)S(1)}, bf16[256,128]{1,0:T(8,128)(2,1)S(1)}, u32[]{:S(2)}, u32[]{:S(2)}) collective-permute-start(bf16[256,128]{1,0:T(8,128)(2,1)S(1)} %get-tuple-element.15), channel_id=1, source_target_pairs={{1,0},{2,1},{3,2},{5,4},{6,5},{7,6},{9,8},{10,9},{11,10},{13,12},{... | collective-permute-start | bytes 196616 | tf_op jit(solution)/shard_map/ppermute | solution.py:31
  96.3 0.8 pad_add_fusion.live_ref
  97.1 1.9 %collective-permute-done.2 = bf16[256,128]{1,0:T(8,128)(2,1)S(1)} collective-permute-done((bf16[256,128]{1,0:T(8,128)(2,1)S(1)}, bf16[256,128]{1,0:T(8,128)(2,1)S(1)}, u32[]{:S(2)}, u32[]{:S(2)}) %collective-permute-start.2) | collective-permute-done | bytes 65568 | tf_op jit(solution)/shard_map/ppermute | solution.py:31
  99.1 1.0 pad_maximum_fusion.1.kv_ref
  100.1 0.3 mul.21
  100.6 52.7 %all-to-all-done.1 = bf16[32,64,128]{2,1,0:T(8,128)(2,1)S(1)} async-done(((bf16[32,64,128]{2,1,0:T(8,128)(2,1)}), bf16[32,64,128]{2,1,0:T(8,128)(2,1)S(1)}, u32[]{:S(2)}, u32[]{:S(2)}) %all-to-all-start.1) | async-done | bytes 524320 | tf_op jit(solution)/shard_map/all_to_all | solution.py:147
  153.6 0.7 add.54.dl_ref
  154.3 0.3 reshape.120
  154.7 0.3 concatenate.37
  155.0 1.2 pad_maximum_fusion.rz_ref
  156.2 13.4 %shard_map.77 = (bf16[3072,64]{1,0:T(8,128)(2,1)}, f32[3584,128]{1,0:T(8,128)}) custom-call(bf16[24,256,128]{2,1,0:T(8,128)(2,1)} %pad_maximum_fusion.rz_ref, bf16[3584,128]{1,0:T(8,128)(2,1)} %pad_maximum_fusion.1.kv_ref, s32[24,10,128]{2,1,0:T(8,128)} %pad_add_fusion.live_ref, f32[24,128]{1,0:T(8,128)} %bitcast.66, f32[24,128]{1,0:T(8,128)} %add.54.dl_ref), custom_call_target="tpu_custom_call" | custom-call | flops 3019898880 | bytes 6191104 | tf_op jit(solution)/shard_map/pallas_call | solution.py:71
  169.7 1.0 slice.69
  170.7 3.1 %collective-permute-start.3 = (f32[256,128]{1,0:T(8,128)S(1)}, f32[256,128]{1,0:T(8,128)S(1)}, u32[]{:S(2)}, u32[]{:S(2)}) collective-permute-start(f32[256,128]{1,0:T(8,128)S(1)} %slice.69), channel_id=1, source_target_pairs={{0,1},{1,2},{2,3},{4,5},{5,6},{6,7},{8,9},{9,10},{10,11},{12,13},{... | collective-permute-start | bytes 393224 | tf_op jit(solution)/shard_map/ppermute | solution.py:26
  173.8 3.7 %collective-permute-done.3 = f32[256,128]{1,0:T(8,128)S(1)} collective-permute-done((f32[256,128]{1,0:T(8,128)S(1)}, f32[256,128]{1,0:T(8,128)S(1)}, u32[]{:S(2)}, u32[]{:S(2)}) %collective-permute-start.3) | collective-permute-done | bytes 131104 | tf_op jit(solution)/shard_map/ppermute | solution.py:26
  177.5 1.0 fusion.2
  178.5 2.4 %collective-permute-start.4 = (f32[256,128]{1,0:T(8,128)S(1)}, f32[256,128]{1,0:T(8,128)S(1)}, u32[]{:S(2)}, u32[]{:S(2)}) collective-permute-start(f32[256,128]{1,0:T(8,128)S(1)} %get-tuple-element.13), channel_id=1, source_target_pairs={{1,0},{2,1},{3,2},{5,4},{6,5},{7,6},{9,8},{10,9},{11,10},{13,12},{... | collective-permute-start | bytes 393224 | tf_op jit(solution)/shard_map/ppermute | solution.py:31
  181.0 1.4 fusion.1
  182.4 1.0 copy.29
  183.4 2.0 %collective-permute-done.4 = f32[256,128]{1,0:T(8,128)S(1)} collective-permute-done((f32[256,128]{1,0:T(8,128)S(1)}, f32[256,128]{1,0:T(8,128)S(1)}, u32[]{:S(2)}, u32[]{:S(2)}) %collective-permute-start.4) | collective-permute-done | bytes 131104 | tf_op jit(solution)/shard_map/ppermute | solution.py:31
  185.4 0.9 fusion.3
  186.3 0.9 pad_maximum_fusion.2
  (41 shorter events, 2.1 us)
Async XLA Ops:
  1.9 30.2 %copy-start.2 = (bf16[1,1,96,2048]{3,2,1,0:T(8,128)(2,1)S(1)}, bf16[1,1,96,2048]{3,2,1,0:T(8,128)(2,1)}, u32[]{:S(2)}) copy-start(bf16[1,1,96,2048]{3,2,1,0:T(8,128)(2,1)} %param.6) | copy-start | bytes 1179652
  1.9 30.5 %copy-start.3 = (bf16[1,1,96,2048]{3,2,1,0:T(8,128)(2,1)S(1)}, bf16[1,1,96,2048]{3,2,1,0:T(8,128)(2,1)}, u32[]{:S(2)}) copy-start(bf16[1,1,96,2048]{3,2,1,0:T(8,128)(2,1)} %param.8) | copy-start | bytes 1179652
  3.4 82.5 %all-to-all-start = ((bf16[32,48,128]{2,1,0:T(8,128)(2,1)}), bf16[32,48,128]{2,1,0:T(8,128)(2,1)S(1)}, u32[]{:S(2)}, u32[]{:S(2)}) async-start(bf16[32,48,128]{2,1,0:T(8,128)(2,1)} %reshape.115), calls=%async_computation | async-start | bytes 786432 | tf_op jit(solution)/shard_map/all_to_all | solution.py:131
  32.4 6.7 %collective-permute-start = (bf16[1,1,96,2048]{2,3,1,0:T(8,128)(2,1)S(1)}, bf16[1,1,96,2048]{2,3,1,0:T(8,128)(2,1)S(1)}, u32[]{:S(2)}, u32[]{:S(2)}) collective-permute-start(bf16[1,1,96,2048]{2,3,1,0:T(8,128)(2,1)S(1)} %copy.24), channel_id=1, source_target_pairs={{0,896},{128,0},{256,128},{384,256},{512,384},{640,512},{768,640},... | collective-permute-start | bytes 1179656 | tf_op jit(solution)/shard_map/ppermute | solution.py:21
  39.9 49.8 %copy-start = (bf16[1,1,1,3072,128]{4,3,2,1,0:T(8,128)(2,1)S(1)}, bf16[1,1,1,3072,128]{4,3,2,1,0:T(8,128)(2,1)}, u32[]{:S(2)}) copy-start(bf16[1,1,1,3072,128]{4,3,2,1,0:T(8,128)(2,1)} %param.9) | copy-start | bytes 2359300
  40.0 55.7 %copy-start.4 = (s32[192,7]{0,1:T(8,128)S(1)}, s32[192,7]{0,1:T(8,128)}, u32[]{:S(2)}) copy-start(s32[192,7]{0,1:T(8,128)} %param.11) | copy-start | bytes 16132
  85.9 67.5 %all-to-all-start.1 = ((bf16[32,64,128]{2,1,0:T(8,128)(2,1)}), bf16[32,64,128]{2,1,0:T(8,128)(2,1)S(1)}, u32[]{:S(2)}, u32[]{:S(2)}) async-start(bf16[32,64,128]{2,1,0:T(8,128)(2,1)} %pad_maximum_fusion.3), calls=%async_computation.1 | async-start | bytes 1048576 | tf_op jit(solution)/shard_map/all_to_all | solution.py:147
  89.8 7.3 %collective-permute-start.1 = (bf16[256,128]{1,0:T(8,128)(2,1)S(1)}, bf16[256,128]{1,0:T(8,128)(2,1)S(1)}, u32[]{:S(2)}, u32[]{:S(2)}) collective-permute-start(bf16[256,128]{1,0:T(8,128)(2,1)S(1)} %get-tuple-element.14), channel_id=1, source_target_pairs={{0,1},{1,2},{2,3},{4,5},{5,6},{6,7},{8,9},{9,10},{10,11},{12,13},{... | collective-permute-start | bytes 196616 | tf_op jit(solution)/shard_map/ppermute | solution.py:26
  92.9 6.2 %collective-permute-start.2 = (bf16[256,128]{1,0:T(8,128)(2,1)S(1)}, bf16[256,128]{1,0:T(8,128)(2,1)S(1)}, u32[]{:S(2)}, u32[]{:S(2)}) collective-permute-start(bf16[256,128]{1,0:T(8,128)(2,1)S(1)} %get-tuple-element.15), channel_id=1, source_target_pairs={{1,0},{2,1},{3,2},{5,4},{6,5},{7,6},{9,8},{10,9},{11,10},{13,12},{... | collective-permute-start | bytes 196616 | tf_op jit(solution)/shard_map/ppermute | solution.py:31
  169.7 12.7 %copy-start.1 = (bf16[3072,64]{1,0:T(8,128)(2,1)S(1)}, bf16[3072,64]{1,0:T(8,128)(2,1)}, u32[]{:S(2)}) copy-start(bf16[3072,64]{1,0:T(8,128)(2,1)} %get-tuple-element.4) | copy-start | bytes 1179652
  170.7 6.9 %collective-permute-start.3 = (f32[256,128]{1,0:T(8,128)S(1)}, f32[256,128]{1,0:T(8,128)S(1)}, u32[]{:S(2)}, u32[]{:S(2)}) collective-permute-start(f32[256,128]{1,0:T(8,128)S(1)} %slice.69), channel_id=1, source_target_pairs={{0,1},{1,2},{2,3},{4,5},{5,6},{6,7},{8,9},{9,10},{10,11},{12,13},{... | collective-permute-start | bytes 393224 | tf_op jit(solution)/shard_map/ppermute | solution.py:26
  178.5 6.9 %collective-permute-start.4 = (f32[256,128]{1,0:T(8,128)S(1)}, f32[256,128]{1,0:T(8,128)S(1)}, u32[]{:S(2)}, u32[]{:S(2)}) collective-permute-start(f32[256,128]{1,0:T(8,128)S(1)} %get-tuple-element.13), channel_id=1, source_target_pairs={{1,0},{2,1},{3,2},{5,4},{6,5},{7,6},{9,8},{10,9},{11,10},{13,12},{... | collective-permute-start | bytes 393224 | tf_op jit(solution)/shard_map/ppermute | solution.py:31

commit v4 on v2

--- a/solution.py
+++ b/solution.py
@@ -31,7 +31,7 @@
     return lax.ppermute(value, axis, [(i + 1, i) for i in range(count - 1)])
 
 
-def band_kernel(rz_ref, kv_ref, live_ref, lse_ref, dl_ref, qg_ref, cache_ref):
+def band_kernel(rz_ref, kv_ref, live_ref, lse_ref, dl_ref, qg_ref, cache_ref, left_ref, right_ref):
     steps = rz_ref.shape[0]
     span = 2 * BLK
     win = (WIDTH + 1) * BLK
@@ -58,7 +58,10 @@
         qg_ref[pl.ds(r, span), :] = (qg[:, :HD] * (HD ** -0.5)).astype(qg_ref.dtype)
         return carry
 
-    lax.fori_loop(0, steps, step, 0)
+    lax.fori_loop(0, steps, step, 0, unroll=2)
+    rim = REACH * BLK
+    left_ref[...] = cache_ref[pl.ds(0, rim), :]
+    right_ref[...] = cache_ref[pl.ds(cache_ref.shape[0] - rim, rim), :]
 
 
 def band_grads(rz, kv_pad, live, lse, dl):
@@ -73,9 +76,11 @@
         out_shape=(
             jax.ShapeDtypeStruct((rows, HD), jnp.bfloat16),
             jax.ShapeDtypeStruct((pad_rows, 2 * HD), jnp.float32),
+            jax.ShapeDtypeStruct((REACH * BLK, 2 * HD), jnp.float32),
+            jax.ShapeDtypeStruct((REACH * BLK, 2 * HD), jnp.float32),
         ),
         in_specs=[vmem] * 5,
-        out_specs=(vmem, vmem),
+        out_specs=(vmem, vmem, vmem, vmem),
         cost_estimate=pl.CostEstimate(
             flops=flops,
             transcendentals=steps * win * 128,
@@ -158,11 +163,11 @@
     kv_pad = jnp.concatenate([left_halo, cache, right_halo], axis=0)
     first_block = lax.axis_index("tp") * blocks_here
     listed = lax.dynamic_slice_in_dim(neighbours, first_block, blocks_here, 0)
-    query_grad, cache_pad = local_grads(
+    query_grad, cache_pad, left_rim, right_rim = local_grads(
         query_h, grad_h, delta_h, log_totals.reshape(rows_here), kv_pad, listed, first_block
     )
-    from_right = to_left(cache_pad[:rim], "tp")
-    from_left = to_right(cache_pad[rim + rows_here :], "tp")
+    from_right = to_left(left_rim, "tp")
+    from_left = to_right(right_rim, "tp")
     own_part = cache_pad[rim : rim + rows_here]
     own_part = jnp.concatenate(
         [

time: 175 us -> 168 us (0.960)
  waiting for transfers between devices: 98 us -> 94.2 us
  Pallas kernels: 15.6 us -> 13.5 us
    ppermute x2, waiting for transfers between devices: 3.46 us -> 0.01 us  [to_right(): return lax.ppermute(value, axis, [(i, i + 1) for i in range(count - 1)])]
    pallas_call x1, Pallas kernels: 15.6 us -> 13.5 us  [band_grads(): pl.pallas_call(band_kernel, out_shape=(jax.ShapeDtypeStruct((rows, HD), j...]
  transfers between devices with their start and end apart: 6 -> 6, of which waited for: 5 -> 4; matrix products, arithmetic and copies ran while one was open for 4% -> 4% of each run, Pallas kernels for 0% -> 0%
where the time goes in v4:
time: 168 us; the launch traced here: 167 us
  waiting for transfers between devices  94.2 us (56%)
  starting transfers between devices  43 us (26%)
  Pallas kernels  13.5 us (8%)
  local copies, waits for them, and re-layouts  9.15 us (5%)
  other arithmetic  6.58 us (4%)
    all_to_all x1, waiting for transfers between devices, body(): got = lax.all_to_all(send, 'seq', split_axis=0, concat_axis=0, tiled=True)  85.4 us
    all_to_all x1, starting transfers between devices, body(): got = lax.all_to_all(send, 'seq', split_axis=0, concat_axis=0, tiled=True)  28.7 us
    pallas_call x1, Pallas kernels, band_grads(): pl.pallas_call(band_kernel, out_shape=(jax.ShapeDtypeStruct((rows, HD), j...  13.5 us
    ppermute x2, starting transfers between devices, to_right(): return lax.ppermute(value, axis, [(i, i + 1) for i in range(count - 1)])  6.92 us
    ppermute x2, starting transfers between devices, to_left(): return lax.ppermute(value, axis, [(i + 1, i) for i in range(count - 1)])  4.89 us
    ppermute x2, waiting for transfers between devices, to_left(): return lax.ppermute(value, axis, [(i + 1, i) for i in range(count - 1)])  4.44 us
    ppermute x1, waiting for transfers between devices, passed_along(): return lax.ppermute(value, axis, pairs)  4.41 us
    unnamed x15, local copies, waits for them, and re-layouts  3.91 us
  transfers between devices with their start and end apart: 6, of which 4 were waited for; matrix products, arithmetic and copies ran while one was open for 4% of the time, Pallas kernels for 0%

profile of v4, /device:TPU:2, one launch (start us, length us, event | category | flops | bytes accessed | tf_op | source)
XLA Modules:
  0.0 167.4 jit_solution(2149267327000855579)
XLA Ops:
  0.6 1.3 copy.24
  1.9 2.5 %collective-permute-start = (bf16[1,1,96,2048]{2,3,1,0:T(8,128)(2,1)S(1)}, bf16[1,1,96,2048]{2,3,1,0:T(8,128)(2,1)S(1)}, u32[]{:S(2)}, u32[]{:S(2)}) collective-permute-start(bf16[1,1,96,2048]{2,3,1,0:T(8,128)(2,1)S(1)} %copy.24), channel_id=1, source_target_pairs={{0,896},{128,0},{256,128},{384,256},{512,384},{640,512},{768,640},... | collective-permute-start | bytes 1179656 | tf_op jit(solution)/shard_map/ppermute | solution.py:21
  4.4 1.3 copy.22
  5.7 0.4 copy.23
  6.0 0.3 reshape.115
  6.4 0.3 copy.26
  6.7 4.4 %collective-permute-done = bf16[1,1,96,2048]{2,3,1,0:T(8,128)(2,1)S(1)} collective-permute-done((bf16[1,1,96,2048]{2,3,1,0:T(8,128)(2,1)S(1)}, bf16[1,1,96,2048]{2,3,1,0:T(8,128)(2,1)S(1)}, u32[]{:S(2)}, u32[]{:S(2)}) %collective-permute-start) | collective-permute-done | bytes 393248 | tf_op jit(solution)/shard_map/ppermute | solution.py:21
  11.1 0.2 fusion
  11.5 0.4 copy.25
  11.9 0.3 reshape.117
  12.3 1.0 pad_maximum_fusion.1
  13.3 28.7 %all-to-all-start = ((bf16[32,112,128]{2,1,0:T(8,128)(2,1)}), bf16[32,112,128]{2,1,0:T(8,128)(2,1)S(1)}, u32[]{:S(2)}, u32[]{:S(2)}) async-start(bf16[32,112,128]{2,1,0:T(8,128)(2,1)} %pad_maximum_fusion.1), calls=%async_computation | async-start | bytes 1835008 | tf_op jit(solution)/shard_map/all_to_all | solution.py:151
  42.0 3.4 %collective-permute-start.1 = (bf16[256,128]{1,0:T(8,128)(2,1)S(1)}, bf16[256,128]{1,0:T(8,128)(2,1)S(1)}, u32[]{:S(2)}, u32[]{:S(2)}) collective-permute-start(bf16[256,128]{1,0:T(8,128)(2,1)S(1)} %get-tuple-element.20), channel_id=1, source_target_pairs={{0,1},{1,2},{2,3},{4,5},{5,6},{6,7},{8,9},{9,10},{10,11},{12,13},{... | collective-permute-start | bytes 196616 | tf_op jit(solution)/shard_map/ppermute | solution.py:26
  45.4 2.4 %collective-permute-start.2 = (bf16[256,128]{1,0:T(8,128)(2,1)S(1)}, bf16[256,128]{1,0:T(8,128)(2,1)S(1)}, u32[]{:S(2)}, u32[]{:S(2)}) collective-permute-start(bf16[256,128]{1,0:T(8,128)(2,1)S(1)} %get-tuple-element.21), channel_id=1, source_target_pairs={{1,0},{2,1},{3,2},{5,4},{6,5},{7,6},{9,8},{10,9},{11,10},{13,12},{... | collective-permute-start | bytes 196616 | tf_op jit(solution)/shard_map/ppermute | solution.py:31
  48.6 0.8 pad_add_fusion.live_ref
  49.4 2.2 %collective-permute-done.2 = bf16[256,128]{1,0:T(8,128)(2,1)S(1)} collective-permute-done((bf16[256,128]{1,0:T(8,128)(2,1)S(1)}, bf16[256,128]{1,0:T(8,128)(2,1)S(1)}, u32[]{:S(2)}, u32[]{:S(2)}) %collective-permute-start.2) | collective-permute-done | bytes 65568 | tf_op jit(solution)/shard_map/ppermute | solution.py:31
  51.6 1.0 pad_maximum_fusion.2.kv_ref
  52.6 85.4 %all-to-all-done = bf16[32,112,128]{2,1,0:T(8,128)(2,1)S(1)} async-done(((bf16[32,112,128]{2,1,0:T(8,128)(2,1)}), bf16[32,112,128]{2,1,0:T(8,128)(2,1)S(1)}, u32[]{:S(2)}, u32[]{:S(2)}) %all-to-all-start) | async-done | bytes 917536 | tf_op jit(solution)/shard_map/all_to_all | solution.py:151
  138.2 0.7 add.54.dl_ref
  139.0 0.3 mul.22
  139.3 0.3 reshape.120
  139.7 0.2 concatenate.36
  139.8 0.3 concatenate.37
  140.1 1.3 pad_maximum_fusion.rz_ref
  141.4 13.5 %shard_map.77 = (bf16[3072,64]{1,0:T(8,128)(2,1)}, f32[3584,128]{1,0:T(8,128)}, f32[256,128]{1,0:T(8,128)}, f32[256,128]{1,0:T(8,128)}) custom-call(bf16[24,256,128]{2,1,0:T(8,128)(2,1)} %pad_maximum_fusion.rz_ref, bf16[3584,128]{1,0:T(8,128)(2,1)} %pad_maximum_fusion.2.kv_ref, s32[24,10,128]{2,1,0:T(8,128)} %pad_add_fusion.live_ref, f32[24,128]{1,0:T(8,128)} %bitcast.66, ...), custom_call_target="tpu_custom_call" | custom-call | flops 3019898880 | bytes 6191104 | tf_op jit(solution)/shard_map/pallas_call | solution.py:74
  154.9 3.5 %collective-permute-start.3 = (f32[256,128]{1,0:T(8,128)}, f32[256,128]{1,0:T(8,128)S(1)}, u32[]{:S(2)}, u32[]{:S(2)}) collective-permute-start(f32[256,128]{1,0:T(8,128)} %get-tuple-element.8), channel_id=1, source_target_pairs={{0,1},{1,2},{2,3},{4,5},{5,6},{6,7},{8,9},{9,10},{10,11},{12,13},{... | collective-permute-start | bytes 393224 | tf_op jit(solution)/shard_map/ppermute | solution.py:26
  158.4 2.4 %collective-permute-start.4 = (f32[256,128]{1,0:T(8,128)}, f32[256,128]{1,0:T(8,128)S(1)}, u32[]{:S(2)}, u32[]{:S(2)}) collective-permute-start(f32[256,128]{1,0:T(8,128)} %get-tuple-element.9), channel_id=1, source_target_pairs={{1,0},{2,1},{3,2},{5,4},{6,5},{7,6},{9,8},{10,9},{11,10},{13,12},{... | collective-permute-start | bytes 393224 | tf_op jit(solution)/shard_map/ppermute | solution.py:31
  160.9 1.4 fusion.1
  162.3 1.0 copy.29
  163.3 2.2 %collective-permute-done.4 = f32[256,128]{1,0:T(8,128)S(1)} collective-permute-done((f32[256,128]{1,0:T(8,128)}, f32[256,128]{1,0:T(8,128)S(1)}, u32[]{:S(2)}, u32[]{:S(2)}) %collective-permute-start.4) | collective-permute-done | bytes 131104 | tf_op jit(solution)/shard_map/ppermute | solution.py:31
  165.5 1.0 fusion.2
  166.5 0.9 pad_maximum_fusion.3
  (34 shorter events, 1.1 us)
Async XLA Ops:
  1.9 4.5 %copy-start.2 = (bf16[1,1,96,2048]{3,2,1,0:T(8,128)(2,1)S(1)}, bf16[1,1,96,2048]{3,2,1,0:T(8,128)(2,1)}, u32[]{:S(2)}) copy-start(bf16[1,1,96,2048]{3,2,1,0:T(8,128)(2,1)} %param.8) | copy-start | bytes 1179652
  1.9 9.2 %collective-permute-start = (bf16[1,1,96,2048]{2,3,1,0:T(8,128)(2,1)S(1)}, bf16[1,1,96,2048]{2,3,1,0:T(8,128)(2,1)S(1)}, u32[]{:S(2)}, u32[]{:S(2)}) collective-permute-start(bf16[1,1,96,2048]{2,3,1,0:T(8,128)(2,1)S(1)} %copy.24), channel_id=1, source_target_pairs={{0,896},{128,0},{256,128},{384,256},{512,384},{640,512},{768,640},... | collective-permute-start | bytes 1179656 | tf_op jit(solution)/shard_map/ppermute | solution.py:21
  12.2 29.8 %copy-start = (bf16[1,1,1,3072,128]{4,3,2,1,0:T(8,128)(2,1)S(1)}, bf16[1,1,1,3072,128]{4,3,2,1,0:T(8,128)(2,1)}, u32[]{:S(2)}) copy-start(bf16[1,1,1,3072,128]{4,3,2,1,0:T(8,128)(2,1)} %param.9) | copy-start | bytes 2359300
  12.2 35.7 %copy-start.3 = (s32[192,7]{0,1:T(8,128)S(1)}, s32[192,7]{0,1:T(8,128)}, u32[]{:S(2)}) copy-start(s32[192,7]{0,1:T(8,128)} %param.11) | copy-start | bytes 16132
  13.3 124.7 %all-to-all-start = ((bf16[32,112,128]{2,1,0:T(8,128)(2,1)}), bf16[32,112,128]{2,1,0:T(8,128)(2,1)S(1)}, u32[]{:S(2)}, u32[]{:S(2)}) async-start(bf16[32,112,128]{2,1,0:T(8,128)(2,1)} %pad_maximum_fusion.1), calls=%async_computation | async-start | bytes 1835008 | tf_op jit(solution)/shard_map/all_to_all | solution.py:151
  42.0 7.3 %collective-permute-start.1 = (bf16[256,128]{1,0:T(8,128)(2,1)S(1)}, bf16[256,128]{1,0:T(8,128)(2,1)S(1)}, u32[]{:S(2)}, u32[]{:S(2)}) collective-permute-start(bf16[256,128]{1,0:T(8,128)(2,1)S(1)} %get-tuple-element.20), channel_id=1, source_target_pairs={{0,1},{1,2},{2,3},{4,5},{5,6},{6,7},{8,9},{9,10},{10,11},{12,13},{... | collective-permute-start | bytes 196616 | tf_op jit(solution)/shard_map/ppermute | solution.py:26
  45.4 6.2 %collective-permute-start.2 = (bf16[256,128]{1,0:T(8,128)(2,1)S(1)}, bf16[256,128]{1,0:T(8,128)(2,1)S(1)}, u32[]{:S(2)}, u32[]{:S(2)}) collective-permute-start(bf16[256,128]{1,0:T(8,128)(2,1)S(1)} %get-tuple-element.21), channel_id=1, source_target_pairs={{1,0},{2,1},{3,2},{5,4},{6,5},{7,6},{9,8},{10,9},{11,10},{13,12},{... | collective-permute-start | bytes 196616 | tf_op jit(solution)/shard_map/ppermute | solution.py:31
  154.9 7.4 %copy-start.1 = (bf16[3072,64]{1,0:T(8,128)(2,1)S(1)}, bf16[3072,64]{1,0:T(8,128)(2,1)}, u32[]{:S(2)}) copy-start(bf16[3072,64]{1,0:T(8,128)(2,1)} %get-tuple-element.6) | copy-start | bytes 1179652
  154.9 8.4 %collective-permute-start.3 = (f32[256,128]{1,0:T(8,128)}, f32[256,128]{1,0:T(8,128)S(1)}, u32[]{:S(2)}, u32[]{:S(2)}) collective-permute-start(f32[256,128]{1,0:T(8,128)} %get-tuple-element.8), channel_id=1, source_target_pairs={{0,1},{1,2},{2,3},{4,5},{5,6},{6,7},{8,9},{9,10},{10,11},{12,13},{... | collective-permute-start | bytes 393224 | tf_op jit(solution)/shard_map/ppermute | solution.py:26
  158.4 7.1 %collective-permute-start.4 = (f32[256,128]{1,0:T(8,128)}, f32[256,128]{1,0:T(8,128)S(1)}, u32[]{:S(2)}, u32[]{:S(2)}) collective-permute-start(f32[256,128]{1,0:T(8,128)} %get-tuple-element.9), channel_id=1, source_target_pairs={{1,0},{2,1},{3,2},{5,4},{6,5},{7,6},{9,8},{10,9},{11,10},{13,12},{... | collective-permute-start | bytes 393224 | tf_op jit(solution)/shard_map/ppermute | solution.py:31

commit v5 on v4

--- a/solution.py
+++ b/solution.py
@@ -31,15 +31,18 @@
     return lax.ppermute(value, axis, [(i + 1, i) for i in range(count - 1)])
 
 
-def band_kernel(rz_ref, kv_ref, live_ref, lse_ref, dl_ref, qg_ref, cache_ref, left_ref, right_ref):
-    steps = rz_ref.shape[0]
+def band_kernel(pair_ref, kv_ref, live_ref, lse_ref, dl_ref, qg_ref, cache_ref, left_ref, right_ref):
+    steps = pair_ref.shape[0] // (2 * BLK)
     span = 2 * BLK
     win = (WIDTH + 1) * BLK
     cache_ref[...] = jnp.zeros_like(cache_ref)
 
     def step(i, carry):
         r = pl.multiple_of(i * span, span)
-        rz = rz_ref[i]
+        pair = pair_ref[pl.ds(r, span), :]
+        lane = lax.broadcasted_iota(jnp.int32, pair.shape, 1)
+        zero = jnp.zeros_like(pair)
+        rz = jnp.concatenate([jnp.where(lane < HD, pair, zero), jnp.where(lane < HD, zero, pair)], axis=0)
         kvw = kv_ref[pl.ds(r, win), :]
         nt = (((1,), (1,)), ((), ()))
         both = lax.dot_general(kvw, rz, nt, preferred_element_type=jnp.float32)
@@ -64,8 +67,8 @@
     right_ref[...] = cache_ref[pl.ds(cache_ref.shape[0] - rim, rim), :]
 
 
-def band_grads(rz, kv_pad, live, lse, dl):
-    steps = rz.shape[0]
+def band_grads(pair, kv_pad, live, lse, dl):
+    steps = pair.shape[0] // (2 * BLK)
     rows = steps * 2 * BLK
     pad_rows = kv_pad.shape[0]
     win = (WIDTH + 1) * BLK
@@ -84,9 +87,9 @@
         cost_estimate=pl.CostEstimate(
             flops=flops,
             transcendentals=steps * win * 128,
-            bytes_accessed=rz.size * 2 + pad_rows * 128 * 10 + rows * 10,
+            bytes_accessed=pair.size * 2 + pad_rows * 128 * 10 + rows * 10,
         ),
-    )(rz, kv_pad, live, lse, dl)
+    )(pair, kv_pad, live, lse, dl)
 
 
 def split3(x):
@@ -97,19 +100,13 @@
     return jnp.stack([hi, mid, lo], axis=1).astype(jnp.bfloat16)
 
 
-def local_grads(query_h, grad_h, delta_h, lse_h, kv_pad, listed, first_block):
-    rows_here = query_h.shape[0]
+def local_grads(pair, delta_h, lse_h, kv_pad, listed, first_block):
+    rows_here = pair.shape[0]
     blocks_here = rows_here // BLK
     steps = blocks_here // 2
     lane = 128
     delta_h = delta_h.reshape(steps, 2 * BLK)
     lse_h = lse_h.reshape(steps, 2 * BLK)
-    zeros = jnp.zeros((rows_here, HD), jnp.bfloat16)
-    top = jnp.concatenate([query_h * jnp.bfloat16(HD ** -0.5), zeros], axis=1)
-    bottom = jnp.concatenate([zeros, grad_h], axis=1)
-    rz = jnp.concatenate(
-        [top.reshape(steps, 2 * BLK, lane), bottom.reshape(steps, 2 * BLK, lane)], axis=1
-    )
     own = first_block + jnp.arange(blocks_here, dtype=jnp.int32)
     offset = listed - own[:, None] + REACH
     hit = (listed >= 0)[:, :, None] & (offset[:, :, None] == jnp.arange(WIDTH, dtype=jnp.int32)[None, None, :])
@@ -123,7 +120,7 @@
         ],
         axis=2,
     )
-    return band_grads(rz, kv_pad, live, lse_h, delta_h)
+    return band_grads(pair, kv_pad, live, lse_h, delta_h)
 
 
 def body(upstream, queries, attention_out, keys_values, log_totals, neighbours):
@@ -142,8 +139,7 @@
     delta_parts = jnp.pad(delta_parts, ((0, 0), (0, d_rows * lane - d_vals)))
     send = jnp.concatenate(
         [
-            jnp.transpose(query_tok, (1, 0, 2)).reshape(H, part_rows, lane),
-            jnp.transpose(grad_tok, (1, 0, 2)).reshape(H, part_rows, lane),
+            jnp.transpose(jnp.concatenate([query_tok * jnp.bfloat16(HD ** -0.5), grad_tok], axis=2), (1, 0, 2)),
             delta_parts.reshape(H, d_rows, lane),
         ],
         axis=1,
@@ -151,9 +147,8 @@
     got = lax.all_to_all(send, "seq", split_axis=0, concat_axis=0, tiled=True)
     rows_here = heads * tokens_here
     blocks_here = rows_here // BLK
-    query_h = got[:, :part_rows].reshape(rows_here, HD)
-    grad_h = got[:, part_rows : 2 * part_rows].reshape(rows_here, HD)
-    d3 = got[:, 2 * part_rows :].reshape(heads, d_rows * lane)[:, :d_vals]
+    pair = got[:, :tokens_here].reshape(rows_here, 2 * HD)
+    d3 = got[:, tokens_here:].reshape(heads, d_rows * lane)[:, :d_vals]
     d3 = d3.reshape(heads, 3, tokens_here).astype(jnp.float32)
     delta_h = ((d3[:, 0] + d3[:, 1]) + d3[:, 2]).reshape(rows_here)
     cache = keys_values.reshape(rows_here, 2 * HD)
@@ -164,7 +159,7 @@
     first_block = lax.axis_index("tp") * blocks_here
     listed = lax.dynamic_slice_in_dim(neighbours, first_block, blocks_here, 0)
     query_grad, cache_pad, left_rim, right_rim = local_grads(
-        query_h, grad_h, delta_h, log_totals.reshape(rows_here), kv_pad, listed, first_block
+        pair, delta_h, log_totals.reshape(rows_here), kv_pad, listed, first_block
     )
     from_right = to_left(left_rim, "tp")
     from_left = to_right(right_rim, "tp")

time: 168 us -> 167 us (level)
  no operation moved by 1% of the time
where the time goes in v5:
time: 167 us
  waiting for transfers between devices  94.9 us (57%)
  starting transfers between devices  43 us (26%)
  Pallas kernels  13.3 us (8%)
  local copies, waits for them, and re-layouts  9.34 us (6%)
  other arithmetic  5.18 us (3%)
    all_to_all x1, waiting for transfers between devices, body(): got = lax.all_to_all(send, 'seq', split_axis=0, concat_axis=0, tiled=True)  85.4 us
    all_to_all x1, starting transfers between devices, body(): got = lax.all_to_all(send, 'seq', split_axis=0, concat_axis=0, tiled=True)  28.7 us
    pallas_call x1, Pallas kernels, band_grads(): pl.pallas_call(band_kernel, out_shape=(jax.ShapeDtypeStruct((rows, HD), j...  13.3 us
    ppermute x2, starting transfers between devices, to_right(): return lax.ppermute(value, axis, [(i, i + 1) for i in range(count - 1)])  6.92 us
    ppermute x1, waiting for transfers between devices, passed_along(): return lax.ppermute(value, axis, pairs)  5.08 us
    ppermute x2, starting transfers between devices, to_left(): return lax.ppermute(value, axis, [(i + 1, i) for i in range(count - 1)])  4.89 us
    ppermute x2, waiting for transfers between devices, to_left(): return lax.ppermute(value, axis, [(i + 1, i) for i in range(count - 1)])  4.44 us
    unnamed x15, local copies, waits for them, and re-layouts  3.96 us
  transfers between devices with their start and end apart: 6, of which 4 were waited for; matrix products, arithmetic and copies ran while one was open for 4% of the time, Pallas kernels for 0%

profile of v5, /device:TPU:2, one launch (start us, length us, event | category | flops | bytes accessed | tf_op | source)
XLA Modules:
  0.0 166.6 jit_solution(9588791425410379011)
XLA Ops:
  0.6 1.3 copy.43
  2.0 2.5 %collective-permute-start = (bf16[1,1,96,2048]{2,3,1,0:T(8,128)(2,1)S(1)}, bf16[1,1,96,2048]{2,3,1,0:T(8,128)(2,1)S(1)}, u32[]{:S(2)}, u32[]{:S(2)}) collective-permute-start(bf16[1,1,96,2048]{2,3,1,0:T(8,128)(2,1)S(1)} %copy.43), channel_id=1, source_target_pairs={{0,896},{128,0},{256,128},{384,256},{512,384},{640,512},{768,640},... | collective-permute-start | bytes 1179656 | tf_op jit(solution)/shard_map/ppermute | solution.py:21
  4.4 1.3 copy.42
  5.7 0.3 copy.44
  6.0 5.1 %collective-permute-done = bf16[1,1,96,2048]{2,3,1,0:T(8,128)(2,1)S(1)} collective-permute-done((bf16[1,1,96,2048]{2,3,1,0:T(8,128)(2,1)S(1)}, bf16[1,1,96,2048]{2,3,1,0:T(8,128)(2,1)S(1)}, u32[]{:S(2)}, u32[]{:S(2)}) %collective-permute-start) | collective-permute-done | bytes 393248 | tf_op jit(solution)/shard_map/ppermute | solution.py:21
  11.1 0.2 fusion
  11.4 0.3 maximum_bitcast_fusion
  11.7 0.1 convert_element_type.48
  11.8 0.5 copy.46
  12.3 0.6 pad_maximum_fusion
  12.9 1.3 copy.47
  14.2 28.7 %all-to-all-start = ((bf16[32,112,128]{2,1,0:T(8,128)(2,1)}), bf16[32,112,128]{2,1,0:T(8,128)(2,1)S(1)}, u32[]{:S(2)}, u32[]{:S(2)}) async-start(bf16[32,112,128]{2,1,0:T(8,128)(2,1)} %copy.47), calls=%async_computation | async-start | bytes 1835008 | tf_op jit(solution)/shard_map/all_to_all | solution.py:147
  43.0 3.4 %collective-permute-start.1 = (bf16[256,128]{1,0:T(8,128)(2,1)S(1)}, bf16[256,128]{1,0:T(8,128)(2,1)S(1)}, u32[]{:S(2)}, u32[]{:S(2)}) collective-permute-start(bf16[256,128]{1,0:T(8,128)(2,1)S(1)} %get-tuple-element.22), channel_id=1, source_target_pairs={{0,1},{1,2},{2,3},{4,5},{5,6},{6,7},{8,9},{9,10},{10,11},{12,13},{... | collective-permute-start | bytes 196616 | tf_op jit(solution)/shard_map/ppermute | solution.py:26
  46.4 2.4 %collective-permute-start.2 = (bf16[256,128]{1,0:T(8,128)(2,1)S(1)}, bf16[256,128]{1,0:T(8,128)(2,1)S(1)}, u32[]{:S(2)}, u32[]{:S(2)}) collective-permute-start(bf16[256,128]{1,0:T(8,128)(2,1)S(1)} %get-tuple-element.23), channel_id=1, source_target_pairs={{1,0},{2,1},{3,2},{5,4},{6,5},{7,6},{9,8},{10,9},{11,10},{13,12},{... | collective-permute-start | bytes 196616 | tf_op jit(solution)/shard_map/ppermute | solution.py:31
  49.1 0.1 copy.48
  49.3 0.1 broadcast_in_dim.5
  49.4 0.1 broadcast_in_dim.4
  49.5 0.8 pad_add_fusion.live_ref
  50.3 2.2 %collective-permute-done.2 = bf16[256,128]{1,0:T(8,128)(2,1)S(1)} collective-permute-done((bf16[256,128]{1,0:T(8,128)(2,1)S(1)}, bf16[256,128]{1,0:T(8,128)(2,1)S(1)}, u32[]{:S(2)}, u32[]{:S(2)}) %collective-permute-start.2) | collective-permute-done | bytes 65568 | tf_op jit(solution)/shard_map/ppermute | solution.py:31
  52.6 1.0 pad_maximum_fusion.1.kv_ref
  53.6 85.4 %all-to-all-done = bf16[32,112,128]{2,1,0:T(8,128)(2,1)S(1)} async-done(((bf16[32,112,128]{2,1,0:T(8,128)(2,1)}), bf16[32,112,128]{2,1,0:T(8,128)(2,1)S(1)}, u32[]{:S(2)}, u32[]{:S(2)}) %all-to-all-start) | async-done | bytes 917536 | tf_op jit(solution)/shard_map/all_to_all | solution.py:147
  139.0 0.1 reshape.107
  139.2 0.7 add.50.dl_ref
  139.9 0.9 slice.65
  140.8 13.3 %shard_map.77 = (bf16[3072,64]{1,0:T(8,128)(2,1)}, f32[3584,128]{1,0:T(8,128)}, f32[256,128]{1,0:T(8,128)}, f32[256,128]{1,0:T(8,128)}) custom-call(bf16[3072,128]{1,0:T(8,128)(2,1)} %bitcast.55, bf16[3584,128]{1,0:T(8,128)(2,1)} %pad_maximum_fusion.1.kv_ref, s32[24,10,128]{2,1,0:T(8,128)} %pad_add_fusion.live_ref, f32[24,128]{1,0:T(8,128)} %bitcast.62, ...), custom_call_target="tpu_custom_call" | custom-call | flops 3019898880 | bytes 5404672 | tf_op jit(solution)/shard_map/pallas_call | solution.py:77
  154.1 3.5 %collective-permute-start.3 = (f32[256,128]{1,0:T(8,128)}, f32[256,128]{1,0:T(8,128)S(1)}, u32[]{:S(2)}, u32[]{:S(2)}) collective-permute-start(f32[256,128]{1,0:T(8,128)} %get-tuple-element.8), channel_id=1, source_target_pairs={{0,1},{1,2},{2,3},{4,5},{5,6},{6,7},{8,9},{9,10},{10,11},{12,13},{... | collective-permute-start | bytes 393224 | tf_op jit(solution)/shard_map/ppermute | solution.py:26
  157.6 2.4 %collective-permute-start.4 = (f32[256,128]{1,0:T(8,128)}, f32[256,128]{1,0:T(8,128)S(1)}, u32[]{:S(2)}, u32[]{:S(2)}) collective-permute-start(f32[256,128]{1,0:T(8,128)} %get-tuple-element.9), channel_id=1, source_target_pairs={{1,0},{2,1},{3,2},{5,4},{6,5},{7,6},{9,8},{10,9},{11,10},{13,12},{... | collective-permute-start | bytes 393224 | tf_op jit(solution)/shard_map/ppermute | solution.py:31
  160.1 1.4 fusion.1
  161.5 1.0 copy.49
  162.5 2.2 %collective-permute-done.4 = f32[256,128]{1,0:T(8,128)S(1)} collective-permute-done((f32[256,128]{1,0:T(8,128)}, f32[256,128]{1,0:T(8,128)S(1)}, u32[]{:S(2)}, u32[]{:S(2)}) %collective-permute-start.4) | collective-permute-done | bytes 131104 | tf_op jit(solution)/shard_map/ppermute | solution.py:31
  164.7 1.0 fusion.2
  165.7 0.9 pad_maximum_fusion.2
  (29 shorter events, 0.6 us)
Async XLA Ops:
  0.6 5.1 %copy-start.2 = (bf16[1,1,96,2048]{3,2,1,0:T(8,128)(2,1)S(1)}, bf16[1,1,96,2048]{3,2,1,0:T(8,128)(2,1)}, u32[]{:S(2)}) copy-start(bf16[1,1,96,2048]{3,2,1,0:T(8,128)(2,1)} %param.8) | copy-start | bytes 1179652
  2.0 9.2 %collective-permute-start = (bf16[1,1,96,2048]{2,3,1,0:T(8,128)(2,1)S(1)}, bf16[1,1,96,2048]{2,3,1,0:T(8,128)(2,1)S(1)}, u32[]{:S(2)}, u32[]{:S(2)}) collective-permute-start(bf16[1,1,96,2048]{2,3,1,0:T(8,128)(2,1)S(1)} %copy.43), channel_id=1, source_target_pairs={{0,896},{128,0},{256,128},{384,256},{512,384},{640,512},{768,640},... | collective-permute-start | bytes 1179656 | tf_op jit(solution)/shard_map/ppermute | solution.py:21
  12.9 30.0 %copy-start = (bf16[1,1,1,3072,128]{4,3,2,1,0:T(8,128)(2,1)S(1)}, bf16[1,1,1,3072,128]{4,3,2,1,0:T(8,128)(2,1)}, u32[]{:S(2)}) copy-start(bf16[1,1,1,3072,128]{4,3,2,1,0:T(8,128)(2,1)} %param.9) | copy-start | bytes 2359300
  12.9 35.9 %copy-start.3 = (s32[192,7]{0,1:T(8,128)S(1)}, s32[192,7]{0,1:T(8,128)}, u32[]{:S(2)}) copy-start(s32[192,7]{0,1:T(8,128)} %param.11) | copy-start | bytes 16132
  14.2 124.7 %all-to-all-start = ((bf16[32,112,128]{2,1,0:T(8,128)(2,1)}), bf16[32,112,128]{2,1,0:T(8,128)(2,1)S(1)}, u32[]{:S(2)}, u32[]{:S(2)}) async-start(bf16[32,112,128]{2,1,0:T(8,128)(2,1)} %copy.47), calls=%async_computation | async-start | bytes 1835008 | tf_op jit(solution)/shard_map/all_to_all | solution.py:147
  43.0 7.3 %collective-permute-start.1 = (bf16[256,128]{1,0:T(8,128)(2,1)S(1)}, bf16[256,128]{1,0:T(8,128)(2,1)S(1)}, u32[]{:S(2)}, u32[]{:S(2)}) collective-permute-start(bf16[256,128]{1,0:T(8,128)(2,1)S(1)} %get-tuple-element.22), channel_id=1, source_target_pairs={{0,1},{1,2},{2,3},{4,5},{5,6},{6,7},{8,9},{9,10},{10,11},{12,13},{... | collective-permute-start | bytes 196616 | tf_op jit(solution)/shard_map/ppermute | solution.py:26
  46.4 6.2 %collective-permute-start.2 = (bf16[256,128]{1,0:T(8,128)(2,1)S(1)}, bf16[256,128]{1,0:T(8,128)(2,1)S(1)}, u32[]{:S(2)}, u32[]{:S(2)}) collective-permute-start(bf16[256,128]{1,0:T(8,128)(2,1)S(1)} %get-tuple-element.23), channel_id=1, source_target_pairs={{1,0},{2,1},{3,2},{5,4},{6,5},{7,6},{9,8},{10,9},{11,10},{13,12},{... | collective-permute-start | bytes 196616 | tf_op jit(solution)/shard_map/ppermute | solution.py:31
  154.1 7.4 %copy-start.1 = (bf16[3072,64]{1,0:T(8,128)(2,1)S(1)}, bf16[3072,64]{1,0:T(8,128)(2,1)}, u32[]{:S(2)}) copy-start(bf16[3072,64]{1,0:T(8,128)(2,1)} %get-tuple-element.6) | copy-start | bytes 1179652
  154.1 8.4 %collective-permute-start.3 = (f32[256,128]{1,0:T(8,128)}, f32[256,128]{1,0:T(8,128)S(1)}, u32[]{:S(2)}, u32[]{:S(2)}) collective-permute-start(f32[256,128]{1,0:T(8,128)} %get-tuple-element.8), channel_id=1, source_target_pairs={{0,1},{1,2},{2,3},{4,5},{5,6},{6,7},{8,9},{9,10},{10,11},{12,13},{... | collective-permute-start | bytes 393224 | tf_op jit(solution)/shard_map/ppermute | solution.py:26
  157.6 7.1 %collective-permute-start.4 = (f32[256,128]{1,0:T(8,128)}, f32[256,128]{1,0:T(8,128)S(1)}, u32[]{:S(2)}, u32[]{:S(2)}) collective-permute-start(f32[256,128]{1,0:T(8,128)} %get-tuple-element.9), channel_id=1, source_target_pairs={{1,0},{2,1},{3,2},{5,4},{6,5},{7,6},{9,8},{10,9},{11,10},{13,12},{... | collective-permute-start | bytes 393224 | tf_op jit(solution)/shard_map/ppermute | solution.py:31

commit v6 on v5

--- a/solution.py
+++ b/solution.py
@@ -31,10 +31,12 @@
     return lax.ppermute(value, axis, [(i + 1, i) for i in range(count - 1)])
 
 
-def band_kernel(pair_ref, kv_ref, live_ref, lse_ref, dl_ref, qg_ref, cache_ref, left_ref, right_ref):
+def band_kernel(pair_ref, kv_ref, live_ref, lse_ref, dl_ref, qgt_ref, cache_out, ends_ref, rims_ref, cache_ref):
     steps = pair_ref.shape[0] // (2 * BLK)
     span = 2 * BLK
     win = (WIDTH + 1) * BLK
+    rim = REACH * BLK
+    rows = pair_ref.shape[0]
     cache_ref[...] = jnp.zeros_like(cache_ref)
 
     def step(i, carry):
@@ -57,37 +59,41 @@
         )
         cache_ref[pl.ds(r, win), :] += terms
         tn = (((0,), (0,)), ((), ()))
-        qg = lax.dot_general(gst, kvw, tn, preferred_element_type=jnp.float32)
-        qg_ref[pl.ds(r, span), :] = (qg[:, :HD] * (HD ** -0.5)).astype(qg_ref.dtype)
+        qgt = lax.dot_general(kvw, gst, tn, preferred_element_type=jnp.float32)
+        qgt_ref[:, pl.ds(r, span)] = (qgt[:HD] * (HD ** -0.5)).astype(qgt_ref.dtype)
         return carry
 
     lax.fori_loop(0, steps, step, 0, unroll=2)
-    rim = REACH * BLK
-    left_ref[...] = cache_ref[pl.ds(0, rim), :]
-    right_ref[...] = cache_ref[pl.ds(cache_ref.shape[0] - rim, rim), :]
+    cache_out[...] = cache_ref[pl.ds(rim, rows), :].astype(cache_out.dtype)
+    ends_ref[0] = cache_ref[pl.ds(rim, rim), :]
+    ends_ref[1] = cache_ref[pl.ds(rows, rim), :]
+    rims_ref[0] = cache_ref[pl.ds(0, rim), :]
+    rims_ref[1] = cache_ref[pl.ds(rows + rim, rim), :]
 
 
 def band_grads(pair, kv_pad, live, lse, dl):
-    steps = pair.shape[0] // (2 * BLK)
-    rows = steps * 2 * BLK
+    rows = pair.shape[0]
+    steps = rows // (2 * BLK)
     pad_rows = kv_pad.shape[0]
     win = (WIDTH + 1) * BLK
+    rim = REACH * BLK
     flops = steps * 3 * 2 * win * 256 * 128
     vmem = pl.BlockSpec(memory_space=pltpu.VMEM)
     return pl.pallas_call(
         band_kernel,
         out_shape=(
-            jax.ShapeDtypeStruct((rows, HD), jnp.bfloat16),
-            jax.ShapeDtypeStruct((pad_rows, 2 * HD), jnp.float32),
-            jax.ShapeDtypeStruct((REACH * BLK, 2 * HD), jnp.float32),
-            jax.ShapeDtypeStruct((REACH * BLK, 2 * HD), jnp.float32),
+            jax.ShapeDtypeStruct((HD, rows), jnp.bfloat16),
+            jax.ShapeDtypeStruct((rows, 2 * HD), jnp.bfloat16),
+            jax.ShapeDtypeStruct((2, rim, 2 * HD), jnp.float32),
+            jax.ShapeDtypeStruct((2, rim, 2 * HD), jnp.float32),
         ),
         in_specs=[vmem] * 5,
         out_specs=(vmem, vmem, vmem, vmem),
+        scratch_shapes=[pltpu.VMEM((pad_rows, 2 * HD), jnp.float32)],
         cost_estimate=pl.CostEstimate(
             flops=flops,
             transcendentals=steps * win * 128,
-            bytes_accessed=pair.size * 2 + pad_rows * 128 * 10 + rows * 10,
+            bytes_accessed=pair.size * 2 + pad_rows * 128 * 2 + rows * 8 + rows * 128 * 2 + rows * 64 * 2,
         ),
     )(pair, kv_pad, live, lse, dl)
 
@@ -158,22 +164,15 @@
     kv_pad = jnp.concatenate([left_halo, cache, right_halo], axis=0)
     first_block = lax.axis_index("tp") * blocks_here
     listed = lax.dynamic_slice_in_dim(neighbours, first_block, blocks_here, 0)
-    query_grad, cache_pad, left_rim, right_rim = local_grads(
+    query_grad_t, cache_own, ends, rims = local_grads(
         pair, delta_h, log_totals.reshape(rows_here), kv_pad, listed, first_block
     )
-    from_right = to_left(left_rim, "tp")
-    from_left = to_right(right_rim, "tp")
-    own_part = cache_pad[rim : rim + rows_here]
-    own_part = jnp.concatenate(
-        [
-            own_part[:rim] + from_left,
-            own_part[rim : rows_here - rim],
-            own_part[rows_here - rim :] + from_right,
-        ],
-        axis=0,
-    )
-    query_grad = query_grad.reshape(1, 1, 1, rows_here, HD)
-    cache_grad = own_part.astype(jnp.bfloat16).reshape(1, 1, 1, rows_here, 2 * HD)
+    from_right = to_left(rims[0], "tp")
+    from_left = to_right(rims[1], "tp")
+    cache_own = cache_own.at[:rim].set((ends[0] + from_left).astype(jnp.bfloat16))
+    cache_own = cache_own.at[rows_here - rim :].set((ends[1] + from_right).astype(jnp.bfloat16))
+    query_grad = jnp.transpose(query_grad_t).reshape(1, 1, 1, rows_here, HD)
+    cache_grad = cache_own.reshape(1, 1, 1, rows_here, 2 * HD)
     return (query_grad, cache_grad)
 
 

time: 167 us -> 167 us (level)
  local copies, waits for them, and re-layouts: 9.34 us -> 6.98 us
  waiting for transfers between devices: 94.9 us -> 96.6 us
    scatter x0 -> x2, other arithmetic: none -> 3.12 us  [the longest x1 1.56 us: body(): cache_own.at[:rim].set((ends[0] + from_left).astype(jnp.bfloat16))]
    unnamed x15 -> x14, local copies, waits for them, and re-layouts: 3.96 us -> 1.97 us
    concatenate x2 -> x0, other arithmetic: 1.93 us -> none  [body(): jnp.concatenate([own_part[:rim] + from_left, own_part[rim:rows_here - rim...]
  transfers between devices with their start and end apart: 6 -> 6, of which waited for: 4 -> 5; matrix products, arithmetic and copies ran while one was open for 4% -> 3% of each run, Pallas kernels for 0% -> 0%
where the time goes in v6:
time: 167 us
  waiting for transfers between devices  96.6 us (58%)
  starting transfers between devices  43 us (26%)
  Pallas kernels  12.7 us (8%)
  local copies, waits for them, and re-layouts  6.98 us (4%)
  other arithmetic  6.35 us (4%)
    all_to_all x1, waiting for transfers between devices, body(): got = lax.all_to_all(send, 'seq', split_axis=0, concat_axis=0, tiled=True)  85.4 us
    all_to_all x1, starting transfers between devices, body(): got = lax.all_to_all(send, 'seq', split_axis=0, concat_axis=0, tiled=True)  28.9 us
    pallas_call x1, Pallas kernels, band_grads(): pl.pallas_call(band_kernel, out_shape=(jax.ShapeDtypeStruct((HD, rows), j...  12.7 us
    ppermute x2, starting transfers between devices, to_right(): return lax.ppermute(value, axis, [(i, i + 1) for i in range(count - 1)])  6.8 us
    ppermute x1, waiting for transfers between devices, passed_along(): return lax.ppermute(value, axis, pairs)  6.07 us
    ppermute x2, starting transfers between devices, to_left(): return lax.ppermute(value, axis, [(i + 1, i) for i in range(count - 1)])  4.89 us
    ppermute x2, waiting for transfers between devices, to_left(): return lax.ppermute(value, axis, [(i + 1, i) for i in range(count - 1)])  4.1 us
  transfers between devices with their start and end apart: 6, of which 5 were waited for; matrix products, arithmetic and copies ran while one was open for 3% of the time, Pallas kernels for 0%

profile of v6, /device:TPU:2, one launch (start us, length us, event | category | flops | bytes accessed | tf_op | source)
XLA Modules:
  0.0 166.5 jit_solution(16758901271570529819)
XLA Ops:
  0.6 1.3 copy.39
  2.0 2.5 %collective-permute-start = (bf16[1,1,96,2048]{2,3,1,0:T(8,128)(2,1)S(1)}, bf16[1,1,96,2048]{2,3,1,0:T(8,128)(2,1)S(1)}, u32[]{:S(2)}, u32[]{:S(2)}) collective-permute-start(bf16[1,1,96,2048]{2,3,1,0:T(8,128)(2,1)S(1)} %copy.39), channel_id=1, source_target_pairs={{0,896},{128,0},{256,128},{384,256},{512,384},{640,512},{768,640},... | collective-permute-start | bytes 1179656 | tf_op jit(solution)/shard_map/ppermute | solution.py:21
  4.5 0.3 copy.40
  4.8 0.3 copy.38
  5.1 6.1 %collective-permute-done = bf16[1,1,96,2048]{2,3,1,0:T(8,128)(2,1)S(1)} collective-permute-done((bf16[1,1,96,2048]{2,3,1,0:T(8,128)(2,1)S(1)}, bf16[1,1,96,2048]{2,3,1,0:T(8,128)(2,1)S(1)}, u32[]{:S(2)}, u32[]{:S(2)}) %collective-permute-start) | collective-permute-done | bytes 393248 | tf_op jit(solution)/shard_map/ppermute | solution.py:21
  11.2 0.2 fusion
  11.5 0.1 convert_element_type.46
  11.6 0.5 copy.42
  12.1 0.3 maximum_bitcast_fusion
  12.4 0.6 pad_maximum_fusion
  13.0 1.3 copy.43
  14.2 28.9 %all-to-all-start = ((bf16[32,112,128]{2,1,0:T(8,128)(2,1)}), bf16[32,112,128]{2,1,0:T(8,128)(2,1)S(1)}, u32[]{:S(2)}, u32[]{:S(2)}) async-start(bf16[32,112,128]{2,1,0:T(8,128)(2,1)} %copy.43), calls=%async_computation | async-start | bytes 1835008 | tf_op jit(solution)/shard_map/all_to_all | solution.py:153
  43.1 3.4 %collective-permute-start.1 = (bf16[256,128]{1,0:T(8,128)(2,1)S(1)}, bf16[256,128]{1,0:T(8,128)(2,1)S(1)}, u32[]{:S(2)}, u32[]{:S(2)}) collective-permute-start(bf16[256,128]{1,0:T(8,128)(2,1)S(1)} %get-tuple-element.34), channel_id=1, source_target_pairs={{0,1},{1,2},{2,3},{4,5},{5,6},{6,7},{8,9},{9,10},{10,11},{12,13},{... | collective-permute-start | bytes 196616 | tf_op jit(solution)/shard_map/ppermute | solution.py:26
  46.5 2.4 %collective-permute-start.2 = (bf16[256,128]{1,0:T(8,128)(2,1)S(1)}, bf16[256,128]{1,0:T(8,128)(2,1)S(1)}, u32[]{:S(2)}, u32[]{:S(2)}) collective-permute-start(bf16[256,128]{1,0:T(8,128)(2,1)S(1)} %get-tuple-element.35), channel_id=1, source_target_pairs={{1,0},{2,1},{3,2},{5,4},{6,5},{7,6},{9,8},{10,9},{11,10},{13,12},{... | collective-permute-start | bytes 196616 | tf_op jit(solution)/shard_map/ppermute | solution.py:31
  49.2 0.1 copy.44
  49.4 0.1 broadcast_in_dim.4
  49.5 0.1 broadcast_in_dim.5
  49.7 0.8 pad_add_fusion.live_ref
  50.5 2.2 %collective-permute-done.2 = bf16[256,128]{1,0:T(8,128)(2,1)S(1)} collective-permute-done((bf16[256,128]{1,0:T(8,128)(2,1)S(1)}, bf16[256,128]{1,0:T(8,128)(2,1)S(1)}, u32[]{:S(2)}, u32[]{:S(2)}) %collective-permute-start.2) | collective-permute-done | bytes 65568 | tf_op jit(solution)/shard_map/ppermute | solution.py:31
  52.7 1.0 pad_maximum_fusion.1.kv_ref
  53.7 85.4 %all-to-all-done = bf16[32,112,128]{2,1,0:T(8,128)(2,1)S(1)} async-done(((bf16[32,112,128]{2,1,0:T(8,128)(2,1)}), bf16[32,112,128]{2,1,0:T(8,128)(2,1)S(1)}, u32[]{:S(2)}, u32[]{:S(2)}) %all-to-all-start) | async-done | bytes 917536 | tf_op jit(solution)/shard_map/all_to_all | solution.py:153
  139.2 0.1 reshape.124
  139.3 0.7 add.54.dl_ref
  140.0 1.0 slice.98
  141.0 12.7 %shard_map.77 = (bf16[64,3072]{1,0:T(8,128)(2,1)}, bf16[3072,128]{1,0:T(8,128)(2,1)}, f32[2,256,128]{2,1,0:T(8,128)}, f32[2,256,128]{2,1,0:T(8,128)}) custom-call(bf16[3072,128]{1,0:T(8,128)(2,1)} %bitcast.79, bf16[3584,128]{1,0:T(8,128)(2,1)} %pad_maximum_fusion.1.kv_ref, s32[24,10,128]{2,1,0:T(8,128)} %pad_add_fusion.live_ref, f32[24,128]{1,0:T(8,128)} %bitcast.87, ...), custom_call_target="tpu_custom_call" | custom-call | flops 3019898880 | bytes 2908160 | tf_op jit(solution)/shard_map/pallas_call | solution.py:82
  153.7 1.0 slice_bitcast_fusion
  154.7 3.4 %collective-permute-start.3 = (f32[256,128]{1,0:T(8,128)S(1)}, f32[256,128]{1,0:T(8,128)S(1)}, u32[]{:S(2)}, u32[]{:S(2)}) collective-permute-start(f32[256,128]{1,0:T(8,128)S(1)} %get-tuple-element.37), channel_id=1, source_target_pairs={{0,1},{1,2},{2,3},{4,5},{5,6},{6,7},{8,9},{9,10},{10,11},{12,13},{... | collective-permute-start | bytes 393224 | tf_op jit(solution)/shard_map/ppermute | solution.py:26
  158.1 2.4 %collective-permute-start.4 = (f32[256,128]{1,0:T(8,128)S(1)}, f32[256,128]{1,0:T(8,128)S(1)}, u32[]{:S(2)}, u32[]{:S(2)}) collective-permute-start(f32[256,128]{1,0:T(8,128)S(1)} %get-tuple-element.36), channel_id=1, source_target_pairs={{1,0},{2,1},{3,2},{5,4},{6,5},{7,6},{9,8},{10,9},{11,10},{13,12},{... | collective-permute-start | bytes 393224 | tf_op jit(solution)/shard_map/ppermute | solution.py:31
  160.5 1.0 collective-permute-done.3
  161.5 1.6 fusion.4
  163.1 1.8 %collective-permute-done.4 = f32[256,128]{1,0:T(8,128)S(1)} collective-permute-done((f32[256,128]{1,0:T(8,128)S(1)}, f32[256,128]{1,0:T(8,128)S(1)}, u32[]{:S(2)}, u32[]{:S(2)}) %collective-permute-start.4) | collective-permute-done | bytes 131104 | tf_op jit(solution)/shard_map/ppermute | solution.py:31
  165.0 1.6 fusion.6
  (28 shorter events, 0.6 us)
Async XLA Ops:
  0.6 3.8 %copy-start.1 = (bf16[1,1,96,2048]{3,2,1,0:T(8,128)(2,1)S(1)}, bf16[1,1,96,2048]{3,2,1,0:T(8,128)(2,1)}, u32[]{:S(2)}) copy-start(bf16[1,1,96,2048]{3,2,1,0:T(8,128)(2,1)} %param.12) | copy-start | bytes 1179652
  0.6 4.1 %copy-start.2 = (bf16[1,1,96,2048]{3,2,1,0:T(8,128)(2,1)S(1)}, bf16[1,1,96,2048]{3,2,1,0:T(8,128)(2,1)}, u32[]{:S(2)}) copy-start(bf16[1,1,96,2048]{3,2,1,0:T(8,128)(2,1)} %param.11) | copy-start | bytes 1179652
  2.0 9.2 %collective-permute-start = (bf16[1,1,96,2048]{2,3,1,0:T(8,128)(2,1)S(1)}, bf16[1,1,96,2048]{2,3,1,0:T(8,128)(2,1)S(1)}, u32[]{:S(2)}, u32[]{:S(2)}) collective-permute-start(bf16[1,1,96,2048]{2,3,1,0:T(8,128)(2,1)S(1)} %copy.39), channel_id=1, source_target_pairs={{0,896},{128,0},{256,128},{384,256},{512,384},{640,512},{768,640},... | collective-permute-start | bytes 1179656 | tf_op jit(solution)/shard_map/ppermute | solution.py:21
  14.2 28.9 %copy-start = (bf16[1,1,1,3072,128]{4,3,2,1,0:T(8,128)(2,1)S(1)}, bf16[1,1,1,3072,128]{4,3,2,1,0:T(8,128)(2,1)}, u32[]{:S(2)}) copy-start(bf16[1,1,1,3072,128]{4,3,2,1,0:T(8,128)(2,1)} %param.13) | copy-start | bytes 2359300
  14.2 34.8 %copy-start.3 = (s32[192,7]{0,1:T(8,128)S(1)}, s32[192,7]{0,1:T(8,128)}, u32[]{:S(2)}) copy-start(s32[192,7]{0,1:T(8,128)} %param.15) | copy-start | bytes 16132
  14.2 124.9 %all-to-all-start = ((bf16[32,112,128]{2,1,0:T(8,128)(2,1)}), bf16[32,112,128]{2,1,0:T(8,128)(2,1)S(1)}, u32[]{:S(2)}, u32[]{:S(2)}) async-start(bf16[32,112,128]{2,1,0:T(8,128)(2,1)} %copy.43), calls=%async_computation | async-start | bytes 1835008 | tf_op jit(solution)/shard_map/all_to_all | solution.py:153
  43.1 7.3 %collective-permute-start.1 = (bf16[256,128]{1,0:T(8,128)(2,1)S(1)}, bf16[256,128]{1,0:T(8,128)(2,1)S(1)}, u32[]{:S(2)}, u32[]{:S(2)}) collective-permute-start(bf16[256,128]{1,0:T(8,128)(2,1)S(1)} %get-tuple-element.34), channel_id=1, source_target_pairs={{0,1},{1,2},{2,3},{4,5},{5,6},{6,7},{8,9},{9,10},{10,11},{12,13},{... | collective-permute-start | bytes 196616 | tf_op jit(solution)/shard_map/ppermute | solution.py:26
  46.5 6.2 %collective-permute-start.2 = (bf16[256,128]{1,0:T(8,128)(2,1)S(1)}, bf16[256,128]{1,0:T(8,128)(2,1)S(1)}, u32[]{:S(2)}, u32[]{:S(2)}) collective-permute-start(bf16[256,128]{1,0:T(8,128)(2,1)S(1)} %get-tuple-element.35), channel_id=1, source_target_pairs={{1,0},{2,1},{3,2},{5,4},{6,5},{7,6},{9,8},{10,9},{11,10},{13,12},{... | collective-permute-start | bytes 196616 | tf_op jit(solution)/shard_map/ppermute | solution.py:31
  154.7 6.9 %collective-permute-start.3 = (f32[256,128]{1,0:T(8,128)S(1)}, f32[256,128]{1,0:T(8,128)S(1)}, u32[]{:S(2)}, u32[]{:S(2)}) collective-permute-start(f32[256,128]{1,0:T(8,128)S(1)} %get-tuple-element.37), channel_id=1, source_target_pairs={{0,1},{1,2},{2,3},{4,5},{5,6},{6,7},{8,9},{9,10},{10,11},{12,13},{... | collective-permute-start | bytes 393224 | tf_op jit(solution)/shard_map/ppermute | solution.py:26
  158.1 6.9 %collective-permute-start.4 = (f32[256,128]{1,0:T(8,128)S(1)}, f32[256,128]{1,0:T(8,128)S(1)}, u32[]{:S(2)}, u32[]{:S(2)}) collective-permute-start(f32[256,128]{1,0:T(8,128)S(1)} %get-tuple-element.36), channel_id=1, source_target_pairs={{1,0},{2,1},{3,2},{5,4},{6,5},{7,6},{9,8},{10,9},{11,10},{13,12},{... | collective-permute-start | bytes 393224 | tf_op jit(solution)/shard_map/ppermute | solution.py:31

commit v7 on v6

--- a/solution.py
+++ b/solution.py
@@ -140,17 +140,18 @@
     lane = 128
     part_rows = tokens_here * HD // lane
     d_vals = 3 * tokens_here
-    d_rows = -(-d_vals // (16 * lane)) * 16
+    d_rows = -(-d_vals // lane)
     delta_parts = split3(jnp.transpose(delta_tok)).reshape(H, d_vals)
     delta_parts = jnp.pad(delta_parts, ((0, 0), (0, d_rows * lane - d_vals)))
     send = jnp.concatenate(
         [
-            jnp.transpose(jnp.concatenate([query_tok * jnp.bfloat16(HD ** -0.5), grad_tok], axis=2), (1, 0, 2)),
-            delta_parts.reshape(H, d_rows, lane),
+            jnp.transpose(jnp.concatenate([query_tok * jnp.bfloat16(HD ** -0.5), grad_tok], axis=2), (1, 0, 2)).reshape(H, tokens_here * lane),
+            delta_parts,
         ],
         axis=1,
-    )
+    ).reshape(H, 1, (tokens_here + d_rows) * lane)
     got = lax.all_to_all(send, "seq", split_axis=0, concat_axis=0, tiled=True)
+    got = got.reshape(heads, tokens_here + d_rows, lane)
     rows_here = heads * tokens_here
     blocks_here = rows_here // BLK
     pair = got[:, :tokens_here].reshape(rows_here, 2 * HD)

time: 167 us -> 168 us (level)
  waiting for transfers between devices: 96.6 us -> 88.2 us
  other arithmetic: 6.35 us -> 12 us
  local copies, waits for them, and re-layouts: 6.98 us -> 11 us
    all_to_all x1, waiting for transfers between devices: 85.4 us -> 78 us  [body(): got = lax.all_to_all(send, 'seq', split_axis=0, concat_axis=0, tiled=True)]
    all_to_all x0 -> x1, other arithmetic: none -> 4.89 us  [body(): got = lax.all_to_all(send, 'seq', split_axis=0, concat_axis=0, tiled=True)]
    unnamed x14 -> x13, local copies, waits for them, and re-layouts: 1.97 us -> 6.24 us
where the time goes in v7:
time: 168 us
  waiting for transfers between devices  88.2 us (52%)
  starting transfers between devices  42.9 us (26%)
  Pallas kernels  12.7 us (8%)
  other arithmetic  12 us (7%)
  local copies, waits for them, and re-layouts  11 us (7%)
    all_to_all x1, waiting for transfers between devices, body(): got = lax.all_to_all(send, 'seq', split_axis=0, concat_axis=0, tiled=True)  78 us
    all_to_all x1, starting transfers between devices, body(): got = lax.all_to_all(send, 'seq', split_axis=0, concat_axis=0, tiled=True)  28.7 us
    pallas_call x1, Pallas kernels, band_grads(): pl.pallas_call(band_kernel, out_shape=(jax.ShapeDtypeStruct((HD, rows), j...  12.7 us
    ppermute x2, starting transfers between devices, to_right(): return lax.ppermute(value, axis, [(i, i + 1) for i in range(count - 1)])  6.8 us
    unnamed x13, local copies, waits for them, and re-layouts  6.24 us
    ppermute x1, waiting for transfers between devices, passed_along(): return lax.ppermute(value, axis, pairs)  5.08 us
    all_to_all x1, other arithmetic, body(): got = lax.all_to_all(send, 'seq', split_axis=0, concat_axis=0, tiled=True)  4.89 us
    ppermute x2, starting transfers between devices, to_left(): return lax.ppermute(value, axis, [(i + 1, i) for i in range(count - 1)])  4.89 us
  transfers between devices with their start and end apart: 6, of which 5 were waited for; matrix products, arithmetic and copies ran while one was open for 3% of the time, Pallas kernels for 0%

profile of v7, /device:TPU:2, one launch (start us, length us, event | category | flops | bytes accessed | tf_op | source)
XLA Modules:
  0.0 167.6 jit_solution(1362430736626722987)
XLA Ops:
  0.6 1.3 copy.28
  2.0 2.5 %collective-permute-start = (bf16[1,1,96,2048]{2,3,1,0:T(8,128)(2,1)S(1)}, bf16[1,1,96,2048]{2,3,1,0:T(8,128)(2,1)S(1)}, u32[]{:S(2)}, u32[]{:S(2)}) collective-permute-start(bf16[1,1,96,2048]{2,3,1,0:T(8,128)(2,1)S(1)} %copy.28), channel_id=1, source_target_pairs={{0,896},{128,0},{256,128},{384,256},{512,384},{640,512},{768,640},... | collective-permute-start | bytes 1179656 | tf_op jit(solution)/shard_map/ppermute | solution.py:21
  4.4 1.3 copy.27
  5.7 0.3 copy.30
  6.0 5.1 %collective-permute-done = bf16[1,1,96,2048]{2,3,1,0:T(8,128)(2,1)S(1)} collective-permute-done((bf16[1,1,96,2048]{2,3,1,0:T(8,128)(2,1)S(1)}, bf16[1,1,96,2048]{2,3,1,0:T(8,128)(2,1)S(1)}, u32[]{:S(2)}, u32[]{:S(2)}) %collective-permute-start) | collective-permute-done | bytes 393248 | tf_op jit(solution)/shard_map/ppermute | solution.py:21
  11.1 0.2 fusion.1
  11.4 0.3 maximum_bitcast_fusion
  11.6 0.6 copy.29
  12.2 0.3 copy.38
  12.8 0.5 broadcast.50
  13.3 1.2 reduce.9
  14.6 1.8 %reshape.141 = bf16[32,2,6336]{2,1,0:T(2,128)(2,1)} reshape(bf16[32,12672]{1,0:T(8,128)(2,1)S(1)} %reduce.9) | data formatting | bytes 1622016
  16.3 28.7 %all-to-all-start = ((bf16[32,2,6336]{2,1,0:T(2,128)(2,1)}), bf16[32,2,6336]{2,1,0:T(2,128)(2,1)S(1)}, u32[]{:S(2)}, u32[]{:S(2)}) async-start(bf16[32,2,6336]{2,1,0:T(2,128)(2,1)} %reshape.141), calls=%async_computation | async-start | bytes 1638400 | tf_op jit(solution)/shard_map/all_to_all | solution.py:153
  45.1 3.4 %collective-permute-start.1 = (bf16[256,128]{1,0:T(8,128)(2,1)S(1)}, bf16[256,128]{1,0:T(8,128)(2,1)S(1)}, u32[]{:S(2)}, u32[]{:S(2)}) collective-permute-start(bf16[256,128]{1,0:T(8,128)(2,1)S(1)} %get-tuple-element.34), channel_id=1, source_target_pairs={{0,1},{1,2},{2,3},{4,5},{5,6},{6,7},{8,9},{9,10},{10,11},{12,13},{... | collective-permute-start | bytes 196616 | tf_op jit(solution)/shard_map/ppermute | solution.py:26
  48.5 2.4 %collective-permute-start.2 = (bf16[256,128]{1,0:T(8,128)(2,1)S(1)}, bf16[256,128]{1,0:T(8,128)(2,1)S(1)}, u32[]{:S(2)}, u32[]{:S(2)}) collective-permute-start(bf16[256,128]{1,0:T(8,128)(2,1)S(1)} %get-tuple-element.35), channel_id=1, source_target_pairs={{1,0},{2,1},{3,2},{5,4},{6,5},{7,6},{9,8},{10,9},{11,10},{13,12},{... | collective-permute-start | bytes 196616 | tf_op jit(solution)/shard_map/ppermute | solution.py:31
  51.6 0.8 pad_add_fusion.live_ref
  52.4 2.2 %collective-permute-done.2 = bf16[256,128]{1,0:T(8,128)(2,1)S(1)} collective-permute-done((bf16[256,128]{1,0:T(8,128)(2,1)S(1)}, bf16[256,128]{1,0:T(8,128)(2,1)S(1)}, u32[]{:S(2)}, u32[]{:S(2)}) %collective-permute-start.2) | collective-permute-done | bytes 65568 | tf_op jit(solution)/shard_map/ppermute | solution.py:31
  54.7 1.0 pad_maximum_fusion.kv_ref
  55.7 78.0 %all-to-all-done = bf16[32,2,6336]{2,1,0:T(2,128)(2,1)S(1)} async-done(((bf16[32,2,6336]{2,1,0:T(2,128)(2,1)}), bf16[32,2,6336]{2,1,0:T(2,128)(2,1)S(1)}, u32[]{:S(2)}, u32[]{:S(2)}) %all-to-all-start) | async-done | bytes 811040 | tf_op jit(solution)/shard_map/all_to_all | solution.py:153
  133.7 1.3 reshape.142
  135.0 4.9 %reduce.4 = bf16[32,12672]{1,0:T(8,128)(2,1)S(1)} reduce(bf16[32,1,12672]{2,1,0:T(2,128)(2,1)S(1)} %reshape.142, bf16[]{:T(256)} %constant.89), dimensions={1}, to_apply=%all_to_all.3.reduce_sub_computation | reduce | bytes 1622018 | tf_op jit(solution)/shard_map/all_to_all | solution.py:153
  139.9 0.4 reshape.122
  140.3 1.0 slice.98
  141.5 0.7 add.54.dl_ref
  142.1 12.7 %shard_map.77 = (bf16[64,3072]{1,0:T(8,128)(2,1)}, bf16[3072,128]{1,0:T(8,128)(2,1)}, f32[2,256,128]{2,1,0:T(8,128)}, f32[2,256,128]{2,1,0:T(8,128)}) custom-call(bf16[3072,128]{1,0:T(8,128)(2,1)} %bitcast.84, bf16[3584,128]{1,0:T(8,128)(2,1)} %pad_maximum_fusion.kv_ref, s32[24,10,128]{2,1,0:T(8,128)} %pad_add_fusion.live_ref, f32[24,128]{1,0:T(8,128)} %bitcast.91, ...), custom_call_target="tpu_custom_call" | custom-call | flops 3019898880 | bytes 2908160 | tf_op jit(solution)/shard_map/pallas_call | solution.py:82
  154.8 1.0 slice_bitcast_fusion
  155.8 3.4 %collective-permute-start.3 = (f32[256,128]{1,0:T(8,128)S(1)}, f32[256,128]{1,0:T(8,128)S(1)}, u32[]{:S(2)}, u32[]{:S(2)}) collective-permute-start(f32[256,128]{1,0:T(8,128)S(1)} %get-tuple-element.37), channel_id=1, source_target_pairs={{0,1},{1,2},{2,3},{4,5},{5,6},{6,7},{8,9},{9,10},{10,11},{12,13},{... | collective-permute-start | bytes 393224 | tf_op jit(solution)/shard_map/ppermute | solution.py:26
  159.2 2.4 %collective-permute-start.4 = (f32[256,128]{1,0:T(8,128)S(1)}, f32[256,128]{1,0:T(8,128)S(1)}, u32[]{:S(2)}, u32[]{:S(2)}) collective-permute-start(f32[256,128]{1,0:T(8,128)S(1)} %get-tuple-element.36), channel_id=1, source_target_pairs={{1,0},{2,1},{3,2},{5,4},{6,5},{7,6},{9,8},{10,9},{11,10},{13,12},{... | collective-permute-start | bytes 393224 | tf_op jit(solution)/shard_map/ppermute | solution.py:31
  161.7 1.0 collective-permute-done.3
  162.7 1.6 fusion.7
  164.2 1.8 %collective-permute-done.4 = f32[256,128]{1,0:T(8,128)S(1)} collective-permute-done((f32[256,128]{1,0:T(8,128)S(1)}, f32[256,128]{1,0:T(8,128)S(1)}, u32[]{:S(2)}, u32[]{:S(2)}) %collective-permute-start.4) | collective-permute-done | bytes 131104 | tf_op jit(solution)/shard_map/ppermute | solution.py:31
  166.1 1.6 fusion.9
  (30 shorter events, 1.1 us)
Async XLA Ops:
  0.6 5.1 %copy-start.1 = (bf16[1,1,96,2048]{3,2,1,0:T(8,128)(2,1)S(1)}, bf16[1,1,96,2048]{3,2,1,0:T(8,128)(2,1)}, u32[]{:S(2)}) copy-start(bf16[1,1,96,2048]{3,2,1,0:T(8,128)(2,1)} %param.12) | copy-start | bytes 1179652
  2.0 9.2 %collective-permute-start = (bf16[1,1,96,2048]{2,3,1,0:T(8,128)(2,1)S(1)}, bf16[1,1,96,2048]{2,3,1,0:T(8,128)(2,1)S(1)}, u32[]{:S(2)}, u32[]{:S(2)}) collective-permute-start(bf16[1,1,96,2048]{2,3,1,0:T(8,128)(2,1)S(1)} %copy.28), channel_id=1, source_target_pairs={{0,896},{128,0},{256,128},{384,256},{512,384},{640,512},{768,640},... | collective-permute-start | bytes 1179656 | tf_op jit(solution)/shard_map/ppermute | solution.py:21
  14.5 30.5 %copy-start = (bf16[1,1,1,3072,128]{4,3,2,1,0:T(8,128)(2,1)S(1)}, bf16[1,1,1,3072,128]{4,3,2,1,0:T(8,128)(2,1)}, u32[]{:S(2)}) copy-start(bf16[1,1,1,3072,128]{4,3,2,1,0:T(8,128)(2,1)} %param.13) | copy-start | bytes 2359300
  14.5 36.4 %copy-start.2 = (s32[192,7]{0,1:T(8,128)S(1)}, s32[192,7]{0,1:T(8,128)}, u32[]{:S(2)}) copy-start(s32[192,7]{0,1:T(8,128)} %param.15) | copy-start | bytes 16132
  16.3 117.4 %all-to-all-start = ((bf16[32,2,6336]{2,1,0:T(2,128)(2,1)}), bf16[32,2,6336]{2,1,0:T(2,128)(2,1)S(1)}, u32[]{:S(2)}, u32[]{:S(2)}) async-start(bf16[32,2,6336]{2,1,0:T(2,128)(2,1)} %reshape.141), calls=%async_computation | async-start | bytes 1638400 | tf_op jit(solution)/shard_map/all_to_all | solution.py:153
  45.1 7.3 %collective-permute-start.1 = (bf16[256,128]{1,0:T(8,128)(2,1)S(1)}, bf16[256,128]{1,0:T(8,128)(2,1)S(1)}, u32[]{:S(2)}, u32[]{:S(2)}) collective-permute-start(bf16[256,128]{1,0:T(8,128)(2,1)S(1)} %get-tuple-element.34), channel_id=1, source_target_pairs={{0,1},{1,2},{2,3},{4,5},{5,6},{6,7},{8,9},{9,10},{10,11},{12,13},{... | collective-permute-start | bytes 196616 | tf_op jit(solution)/shard_map/ppermute | solution.py:26
  48.5 6.2 %collective-permute-start.2 = (bf16[256,128]{1,0:T(8,128)(2,1)S(1)}, bf16[256,128]{1,0:T(8,128)(2,1)S(1)}, u32[]{:S(2)}, u32[]{:S(2)}) collective-permute-start(bf16[256,128]{1,0:T(8,128)(2,1)S(1)} %get-tuple-element.35), channel_id=1, source_target_pairs={{1,0},{2,1},{3,2},{5,4},{6,5},{7,6},{9,8},{10,9},{11,10},{13,12},{... | collective-permute-start | bytes 196616 | tf_op jit(solution)/shard_map/ppermute | solution.py:31
  155.8 6.9 %collective-permute-start.3 = (f32[256,128]{1,0:T(8,128)S(1)}, f32[256,128]{1,0:T(8,128)S(1)}, u32[]{:S(2)}, u32[]{:S(2)}) collective-permute-start(f32[256,128]{1,0:T(8,128)S(1)} %get-tuple-element.37), channel_id=1, source_target_pairs={{0,1},{1,2},{2,3},{4,5},{5,6},{6,7},{8,9},{9,10},{10,11},{12,13},{... | collective-permute-start | bytes 393224 | tf_op jit(solution)/shard_map/ppermute | solution.py:26
  159.2 6.9 %collective-permute-start.4 = (f32[256,128]{1,0:T(8,128)S(1)}, f32[256,128]{1,0:T(8,128)S(1)}, u32[]{:S(2)}, u32[]{:S(2)}) collective-permute-start(f32[256,128]{1,0:T(8,128)S(1)} %get-tuple-element.36), channel_id=1, source_target_pairs={{1,0},{2,1},{3,2},{5,4},{6,5},{7,6},{9,8},{10,9},{11,10},{13,12},{... | collective-permute-start | bytes 393224 | tf_op jit(solution)/shard_map/ppermute | solution.py:31

commit v8 on v6

--- a/solution.py
+++ b/solution.py
@@ -31,7 +31,7 @@
     return lax.ppermute(value, axis, [(i + 1, i) for i in range(count - 1)])
 
 
-def band_kernel(pair_ref, kv_ref, live_ref, lse_ref, dl_ref, qgt_ref, cache_out, ends_ref, rims_ref, cache_ref):
+def band_kernel(pair_ref, kv_ref, bias_ref, dl_ref, qgt_ref, cache_out, head_ref, tail_ref, left_ref, right_ref, cache_ref):
     steps = pair_ref.shape[0] // (2 * BLK)
     span = 2 * BLK
     win = (WIDTH + 1) * BLK
@@ -48,10 +48,9 @@
         kvw = kv_ref[pl.ds(r, win), :]
         nt = (((1,), (1,)), ((), ()))
         both = lax.dot_general(kvw, rz, nt, preferred_element_type=jnp.float32)
-        live = jnp.broadcast_to(live_ref[i][:, None, :], (WIDTH + 1, BLK, span)).reshape(win, span)
-        lse = lse_ref[pl.ds(i, 1), :]
+        bias = jnp.broadcast_to(bias_ref[i][:, None, :], (WIDTH + 1, BLK, span)).reshape(win, span)
         dl = dl_ref[pl.ds(i, 1), :]
-        wt = jnp.where(live != 0, jnp.exp(both[:, :span] - lse), 0.0)
+        wt = jnp.exp(both[:, :span] - bias)
         gst = (wt * (both[:, span:] - dl)).astype(jnp.bfloat16)
         wht = wt.astype(jnp.bfloat16)
         terms = jnp.dot(
@@ -65,13 +64,13 @@
 
     lax.fori_loop(0, steps, step, 0, unroll=2)
     cache_out[...] = cache_ref[pl.ds(rim, rows), :].astype(cache_out.dtype)
-    ends_ref[0] = cache_ref[pl.ds(rim, rim), :]
-    ends_ref[1] = cache_ref[pl.ds(rows, rim), :]
-    rims_ref[0] = cache_ref[pl.ds(0, rim), :]
-    rims_ref[1] = cache_ref[pl.ds(rows + rim, rim), :]
+    head_ref[...] = cache_ref[pl.ds(rim, rim), :]
+    tail_ref[...] = cache_ref[pl.ds(rows, rim), :]
+    left_ref[...] = cache_ref[pl.ds(0, rim), :]
+    right_ref[...] = cache_ref[pl.ds(rows + rim, rim), :]
 
 
-def band_grads(pair, kv_pad, live, lse, dl):
+def band_grads(pair, kv_pad, bias, dl):
     rows = pair.shape[0]
     steps = rows // (2 * BLK)
     pad_rows = kv_pad.shape[0]
@@ -84,18 +83,16 @@
         out_shape=(
             jax.ShapeDtypeStruct((HD, rows), jnp.bfloat16),
             jax.ShapeDtypeStruct((rows, 2 * HD), jnp.bfloat16),
-            jax.ShapeDtypeStruct((2, rim, 2 * HD), jnp.float32),
-            jax.ShapeDtypeStruct((2, rim, 2 * HD), jnp.float32),
-        ),
-        in_specs=[vmem] * 5,
-        out_specs=(vmem, vmem, vmem, vmem),
+        ) + (jax.ShapeDtypeStruct((rim, 2 * HD), jnp.float32),) * 4,
+        in_specs=[vmem] * 4,
+        out_specs=(vmem,) * 6,
         scratch_shapes=[pltpu.VMEM((pad_rows, 2 * HD), jnp.float32)],
         cost_estimate=pl.CostEstimate(
             flops=flops,
             transcendentals=steps * win * 128,
             bytes_accessed=pair.size * 2 + pad_rows * 128 * 2 + rows * 8 + rows * 128 * 2 + rows * 64 * 2,
         ),
-    )(pair, kv_pad, live, lse, dl)
+    )(pair, kv_pad, bias, dl)
 
 
 def split3(x):
@@ -126,7 +123,8 @@
         ],
         axis=2,
     )
-    return band_grads(pair, kv_pad, live, lse_h, delta_h)
+    bias = jnp.where(live != 0, lse_h[:, None, :], jnp.inf)
+    return band_grads(pair, kv_pad, bias, delta_h)
 
 
 def body(upstream, queries, attention_out, keys_values, log_totals, neighbours):
@@ -164,13 +162,19 @@
     kv_pad = jnp.concatenate([left_halo, cache, right_halo], axis=0)
     first_block = lax.axis_index("tp") * blocks_here
     listed = lax.dynamic_slice_in_dim(neighbours, first_block, blocks_here, 0)
-    query_grad_t, cache_own, ends, rims = local_grads(
+    query_grad_t, cache_own, head_part, tail_part, left_rim, right_rim = local_grads(
         pair, delta_h, log_totals.reshape(rows_here), kv_pad, listed, first_block
     )
-    from_right = to_left(rims[0], "tp")
-    from_left = to_right(rims[1], "tp")
-    cache_own = cache_own.at[:rim].set((ends[0] + from_left).astype(jnp.bfloat16))
-    cache_own = cache_own.at[rows_here - rim :].set((ends[1] + from_right).astype(jnp.bfloat16))
+    from_right = to_left(left_rim, "tp")
+    from_left = to_right(right_rim, "tp")
+    cache_own = jnp.concatenate(
+        [
+            (head_part + from_left).astype(jnp.bfloat16),
+            cache_own[rim : rows_here - rim],
+            (tail_part + from_right).astype(jnp.bfloat16),
+        ],
+        axis=0,
+    )
     query_grad = jnp.transpose(query_grad_t).reshape(1, 1, 1, rows_here, HD)
     cache_grad = cache_own.reshape(1, 1, 1, rows_here, 2 * HD)
     return (query_grad, cache_grad)

time: 167 us -> 166 us (level)
  other arithmetic: 6.35 us -> 4.19 us
    scatter x2 -> x0, other arithmetic: 3.12 us -> none  [the longest x1 1.56 us: body(): cache_own.at[:rim].set((ends[0] + from_left).astype(jnp.bfloat16))]
where the time goes in v8:
time: 166 us; the launch traced here: 165 us
  waiting for transfers between devices  97.2 us (59%)
  starting transfers between devices  43.1 us (26%)
  Pallas kernels  12.7 us (8%)
  local copies, waits for them, and re-layouts  7.1 us (4%)
  other arithmetic  4.19 us (3%)
    all_to_all x1, waiting for transfers between devices, body(): got = lax.all_to_all(send, 'seq', split_axis=0, concat_axis=0, tiled=True)  85.4 us
    all_to_all x1, starting transfers between devices, body(): got = lax.all_to_all(send, 'seq', split_axis=0, concat_axis=0, tiled=True)  28.9 us
    pallas_call x1, Pallas kernels, band_grads(): pl.pallas_call(band_kernel, out_shape=(jax.ShapeDtypeStruct((HD, rows), j...  12.7 us
    ppermute x2, starting transfers between devices, to_right(): return lax.ppermute(value, axis, [(i, i + 1) for i in range(count - 1)])  6.92 us
    ppermute x1, waiting for transfers between devices, passed_along(): return lax.ppermute(value, axis, pairs)  6.07 us
    ppermute x2, waiting for transfers between devices, to_left(): return lax.ppermute(value, axis, [(i + 1, i) for i in range(count - 1)])  5.62 us
    ppermute x2, starting transfers between devices, to_left(): return lax.ppermute(value, axis, [(i + 1, i) for i in range(count - 1)])  4.89 us
  transfers between devices with their start and end apart: 6, of which 5 were waited for; matrix products, arithmetic and copies ran while one was open for 3% of the time, Pallas kernels for 0%

profile of v8, /device:TPU:2, one launch (start us, length us, event | category | flops | bytes accessed | tf_op | source)
XLA Modules:
  0.0 165.2 jit_solution(11738380249571515616)
XLA Ops:
  0.6 1.3 copy.39
  2.0 2.5 %collective-permute-start = (bf16[1,1,96,2048]{2,3,1,0:T(8,128)(2,1)S(1)}, bf16[1,1,96,2048]{2,3,1,0:T(8,128)(2,1)S(1)}, u32[]{:S(2)}, u32[]{:S(2)}) collective-permute-start(bf16[1,1,96,2048]{2,3,1,0:T(8,128)(2,1)S(1)} %copy.39), channel_id=1, source_target_pairs={{0,896},{128,0},{256,128},{384,256},{512,384},{640,512},{768,640},... | collective-permute-start | bytes 1179656 | tf_op jit(solution)/shard_map/ppermute | solution.py:21
  4.5 0.3 copy.40
  4.8 0.3 copy.38
  5.1 6.1 %collective-permute-done = bf16[1,1,96,2048]{2,3,1,0:T(8,128)(2,1)S(1)} collective-permute-done((bf16[1,1,96,2048]{2,3,1,0:T(8,128)(2,1)S(1)}, bf16[1,1,96,2048]{2,3,1,0:T(8,128)(2,1)S(1)}, u32[]{:S(2)}, u32[]{:S(2)}) %collective-permute-start) | collective-permute-done | bytes 393248 | tf_op jit(solution)/shard_map/ppermute | solution.py:21
  11.2 0.2 fusion
  11.5 0.1 convert_element_type.46
  11.6 0.5 copy.42
  12.1 0.3 maximum_bitcast_fusion
  12.4 0.6 pad_maximum_fusion
  13.0 1.3 copy.43
  14.2 28.9 %all-to-all-start = ((bf16[32,112,128]{2,1,0:T(8,128)(2,1)}), bf16[32,112,128]{2,1,0:T(8,128)(2,1)S(1)}, u32[]{:S(2)}, u32[]{:S(2)}) async-start(bf16[32,112,128]{2,1,0:T(8,128)(2,1)} %copy.43), calls=%async_computation | async-start | bytes 1835008 | tf_op jit(solution)/shard_map/all_to_all | solution.py:151
  43.1 3.4 %collective-permute-start.1 = (bf16[256,128]{1,0:T(8,128)(2,1)S(1)}, bf16[256,128]{1,0:T(8,128)(2,1)S(1)}, u32[]{:S(2)}, u32[]{:S(2)}) collective-permute-start(bf16[256,128]{1,0:T(8,128)(2,1)S(1)} %get-tuple-element.14), channel_id=1, source_target_pairs={{0,1},{1,2},{2,3},{4,5},{5,6},{6,7},{8,9},{9,10},{10,11},{12,13},{... | collective-permute-start | bytes 196616 | tf_op jit(solution)/shard_map/ppermute | solution.py:26
  46.5 2.4 %collective-permute-start.2 = (bf16[256,128]{1,0:T(8,128)(2,1)S(1)}, bf16[256,128]{1,0:T(8,128)(2,1)S(1)}, u32[]{:S(2)}, u32[]{:S(2)}) collective-permute-start(bf16[256,128]{1,0:T(8,128)(2,1)S(1)} %get-tuple-element.15), channel_id=1, source_target_pairs={{1,0},{2,1},{3,2},{5,4},{6,5},{7,6},{9,8},{10,9},{11,10},{13,12},{... | collective-permute-start | bytes 196616 | tf_op jit(solution)/shard_map/ppermute | solution.py:31
  49.0 0.1 dynamic-slice_compare_fusion
  49.2 0.1 copy.44
  49.4 0.1 broadcast_in_dim.14
  49.5 0.1 broadcast_in_dim.15
  49.7 0.8 fusion.1.bias_ref
  50.5 2.2 %collective-permute-done.2 = bf16[256,128]{1,0:T(8,128)(2,1)S(1)} collective-permute-done((bf16[256,128]{1,0:T(8,128)(2,1)S(1)}, bf16[256,128]{1,0:T(8,128)(2,1)S(1)}, u32[]{:S(2)}, u32[]{:S(2)}) %collective-permute-start.2) | collective-permute-done | bytes 65568 | tf_op jit(solution)/shard_map/ppermute | solution.py:31
  52.7 1.0 pad_maximum_fusion.1.kv_ref
  53.7 85.4 %all-to-all-done = bf16[32,112,128]{2,1,0:T(8,128)(2,1)S(1)} async-done(((bf16[32,112,128]{2,1,0:T(8,128)(2,1)}), bf16[32,112,128]{2,1,0:T(8,128)(2,1)S(1)}, u32[]{:S(2)}, u32[]{:S(2)}) %all-to-all-start) | async-done | bytes 917536 | tf_op jit(solution)/shard_map/all_to_all | solution.py:151
  139.2 0.1 reshape.66
  139.3 0.7 add.50.dl_ref
  140.0 0.9 slice.52
  140.9 12.7 %shard_map.77 = (bf16[64,3072]{1,0:T(8,128)(2,1)}, bf16[3072,128]{1,0:T(8,128)(2,1)}, f32[256,128]{1,0:T(8,128)}, f32[256,128]{1,0:T(8,128)}, f32[256,128]{1,0:T(8,128)}, /*index=5*/f32[256,128]{1,0:T(8,128)}) custom-call(bf16[3072,128]{1,0:T(8,128)(2,1)} %bitcast.52, bf16[3584,128]{1,0:T(8,128)(2,1)} %pad_maximum_fusion.1.kv_ref, ...), custom_call_target="tpu_custom_call" | custom-call | flops 3019898880 | bytes 2908160 | tf_op jit(solution)/shard_map/pallas_call | solution.py:81
  153.6 3.5 %collective-permute-start.3 = (f32[256,128]{1,0:T(8,128)}, f32[256,128]{1,0:T(8,128)S(1)}, u32[]{:S(2)}, u32[]{:S(2)}) collective-permute-start(f32[256,128]{1,0:T(8,128)} %get-tuple-element.10), channel_id=1, source_target_pairs={{0,1},{1,2},{2,3},{4,5},{5,6},{6,7},{8,9},{9,10},{10,11},{12,13},{... | collective-permute-start | bytes 393224 | tf_op jit(solution)/shard_map/ppermute | solution.py:26
  157.1 2.4 %collective-permute-start.4 = (f32[256,128]{1,0:T(8,128)}, f32[256,128]{1,0:T(8,128)S(1)}, u32[]{:S(2)}, u32[]{:S(2)}) collective-permute-start(f32[256,128]{1,0:T(8,128)} %get-tuple-element.13), channel_id=1, source_target_pairs={{1,0},{2,1},{3,2},{5,4},{6,5},{7,6},{9,8},{10,9},{11,10},{13,12},{... | collective-permute-start | bytes 393224 | tf_op jit(solution)/shard_map/ppermute | solution.py:31
  159.6 1.1 slice.51
  160.7 0.1 collective-permute-done.3
  160.8 3.4 %collective-permute-done.4 = f32[256,128]{1,0:T(8,128)S(1)} collective-permute-done((f32[256,128]{1,0:T(8,128)}, f32[256,128]{1,0:T(8,128)S(1)}, u32[]{:S(2)}, u32[]{:S(2)}) %collective-permute-start.4) | collective-permute-done | bytes 131104 | tf_op jit(solution)/shard_map/ppermute | solution.py:31
  164.2 0.9 maximum_bitcast_fusion.1
  (35 shorter events, 0.5 us)
Async XLA Ops:
  0.6 3.8 %copy-start.1 = (bf16[1,1,96,2048]{3,2,1,0:T(8,128)(2,1)S(1)}, bf16[1,1,96,2048]{3,2,1,0:T(8,128)(2,1)}, u32[]{:S(2)}) copy-start(bf16[1,1,96,2048]{3,2,1,0:T(8,128)(2,1)} %param.8) | copy-start | bytes 1179652
  0.6 4.1 %copy-start.2 = (bf16[1,1,96,2048]{3,2,1,0:T(8,128)(2,1)S(1)}, bf16[1,1,96,2048]{3,2,1,0:T(8,128)(2,1)}, u32[]{:S(2)}) copy-start(bf16[1,1,96,2048]{3,2,1,0:T(8,128)(2,1)} %param.7) | copy-start | bytes 1179652
  2.0 9.2 %collective-permute-start = (bf16[1,1,96,2048]{2,3,1,0:T(8,128)(2,1)S(1)}, bf16[1,1,96,2048]{2,3,1,0:T(8,128)(2,1)S(1)}, u32[]{:S(2)}, u32[]{:S(2)}) collective-permute-start(bf16[1,1,96,2048]{2,3,1,0:T(8,128)(2,1)S(1)} %copy.39), channel_id=1, source_target_pairs={{0,896},{128,0},{256,128},{384,256},{512,384},{640,512},{768,640},... | collective-permute-start | bytes 1179656 | tf_op jit(solution)/shard_map/ppermute | solution.py:21
  14.2 28.9 %copy-start = (bf16[1,1,1,3072,128]{4,3,2,1,0:T(8,128)(2,1)S(1)}, bf16[1,1,1,3072,128]{4,3,2,1,0:T(8,128)(2,1)}, u32[]{:S(2)}) copy-start(bf16[1,1,1,3072,128]{4,3,2,1,0:T(8,128)(2,1)} %param.9) | copy-start | bytes 2359300
  14.2 34.8 %copy-start.6 = (s32[192,7]{0,1:T(8,128)S(1)}, s32[192,7]{0,1:T(8,128)}, u32[]{:S(2)}) copy-start(s32[192,7]{0,1:T(8,128)} %param.11) | copy-start | bytes 16132
  14.2 35.4 %copy-start.5 = (f32[1,1,1,3072]{3,2,1,0:T(1,128)S(1)}, f32[1,1,1,3072]{3,2,1,0:T(1,128)}, u32[]{:S(2)}) copy-start(f32[1,1,1,3072]{3,2,1,0:T(1,128)} %param.10) | copy-start | bytes 36868
  14.2 124.9 %all-to-all-start = ((bf16[32,112,128]{2,1,0:T(8,128)(2,1)}), bf16[32,112,128]{2,1,0:T(8,128)(2,1)S(1)}, u32[]{:S(2)}, u32[]{:S(2)}) async-start(bf16[32,112,128]{2,1,0:T(8,128)(2,1)} %copy.43), calls=%async_computation | async-start | bytes 1835008 | tf_op jit(solution)/shard_map/all_to_all | solution.py:151
  43.1 7.3 %collective-permute-start.1 = (bf16[256,128]{1,0:T(8,128)(2,1)S(1)}, bf16[256,128]{1,0:T(8,128)(2,1)S(1)}, u32[]{:S(2)}, u32[]{:S(2)}) collective-permute-start(bf16[256,128]{1,0:T(8,128)(2,1)S(1)} %get-tuple-element.14), channel_id=1, source_target_pairs={{0,1},{1,2},{2,3},{4,5},{5,6},{6,7},{8,9},{9,10},{10,11},{12,13},{... | collective-permute-start | bytes 196616 | tf_op jit(solution)/shard_map/ppermute | solution.py:26
  46.5 6.2 %collective-permute-start.2 = (bf16[256,128]{1,0:T(8,128)(2,1)S(1)}, bf16[256,128]{1,0:T(8,128)(2,1)S(1)}, u32[]{:S(2)}, u32[]{:S(2)}) collective-permute-start(bf16[256,128]{1,0:T(8,128)(2,1)S(1)} %get-tuple-element.15), channel_id=1, source_target_pairs={{1,0},{2,1},{3,2},{5,4},{6,5},{7,6},{9,8},{10,9},{11,10},{13,12},{... | collective-permute-start | bytes 196616 | tf_op jit(solution)/shard_map/ppermute | solution.py:31
  153.6 7.2 %copy-start.4 = (f32[256,128]{1,0:T(8,128)S(1)}, f32[256,128]{1,0:T(8,128)}, u32[]{:S(2)}) copy-start(f32[256,128]{1,0:T(8,128)} %get-tuple-element.9) | copy-start | bytes 393220
  153.6 10.6 %copy-start.3 = (f32[256,128]{1,0:T(8,128)S(1)}, f32[256,128]{1,0:T(8,128)}, u32[]{:S(2)}) copy-start(f32[256,128]{1,0:T(8,128)} %get-tuple-element.12) | copy-start | bytes 393220
  153.6 7.2 %collective-permute-start.3 = (f32[256,128]{1,0:T(8,128)}, f32[256,128]{1,0:T(8,128)S(1)}, u32[]{:S(2)}, u32[]{:S(2)}) collective-permute-start(f32[256,128]{1,0:T(8,128)} %get-tuple-element.10), channel_id=1, source_target_pairs={{0,1},{1,2},{2,3},{4,5},{5,6},{6,7},{8,9},{9,10},{10,11},{12,13},{... | collective-permute-start | bytes 393224 | tf_op jit(solution)/shard_map/ppermute | solution.py:26
  157.1 7.1 %collective-permute-start.4 = (f32[256,128]{1,0:T(8,128)}, f32[256,128]{1,0:T(8,128)S(1)}, u32[]{:S(2)}, u32[]{:S(2)}) collective-permute-start(f32[256,128]{1,0:T(8,128)} %get-tuple-element.13), channel_id=1, source_target_pairs={{1,0},{2,1},{3,2},{5,4},{6,5},{7,6},{9,8},{10,9},{11,10},{13,12},{... | collective-permute-start | bytes 393224 | tf_op jit(solution)/shard_map/ppermute | solution.py:31

commit v9 on v8

--- a/solution.py
+++ b/solution.py
@@ -63,7 +63,7 @@
         return carry
 
     lax.fori_loop(0, steps, step, 0, unroll=2)
-    cache_out[...] = cache_ref[pl.ds(rim, rows), :].astype(cache_out.dtype)
+    cache_out[...] = cache_ref[pl.ds(2 * rim, rows - 2 * rim), :].astype(cache_out.dtype)
     head_ref[...] = cache_ref[pl.ds(rim, rim), :]
     tail_ref[...] = cache_ref[pl.ds(rows, rim), :]
     left_ref[...] = cache_ref[pl.ds(0, rim), :]
@@ -82,7 +82,7 @@
         band_kernel,
         out_shape=(
             jax.ShapeDtypeStruct((HD, rows), jnp.bfloat16),
-            jax.ShapeDtypeStruct((rows, 2 * HD), jnp.bfloat16),
+            jax.ShapeDtypeStruct((rows - 2 * rim, 2 * HD), jnp.bfloat16),
         ) + (jax.ShapeDtypeStruct((rim, 2 * HD), jnp.float32),) * 4,
         in_specs=[vmem] * 4,
         out_specs=(vmem,) * 6,
@@ -170,7 +170,7 @@
     cache_own = jnp.concatenate(
         [
             (head_part + from_left).astype(jnp.bfloat16),
-            cache_own[rim : rows_here - rim],
+            cache_own,
             (tail_part + from_right).astype(jnp.bfloat16),
         ],
         axis=0,

time: 166 us -> 166 us (level)
  other arithmetic: 4.19 us -> 6.02 us
  transfers between devices with their start and end apart: 6 -> 6, of which waited for: 5 -> 5; matrix products, arithmetic and copies ran while one was open for 3% -> 2% of each run, Pallas kernels for 0% -> 0%
where the time goes in v9:
time: 166 us
  waiting for transfers between devices  97.4 us (59%)
  starting transfers between devices  43.1 us (26%)
  Pallas kernels  12.6 us (8%)
  other arithmetic  6.02 us (4%)
  local copies, waits for them, and re-layouts  5.95 us (4%)
    all_to_all x1, waiting for transfers between devices, body(): got = lax.all_to_all(send, 'seq', split_axis=0, concat_axis=0, tiled=True)  85.4 us
    all_to_all x1, starting transfers between devices, body(): got = lax.all_to_all(send, 'seq', split_axis=0, concat_axis=0, tiled=True)  28.9 us
    pallas_call x1, Pallas kernels, band_grads(): pl.pallas_call(band_kernel, out_shape=(jax.ShapeDtypeStruct((HD, rows), j...  12.6 us
    ppermute x2, starting transfers between devices, to_right(): return lax.ppermute(value, axis, [(i, i + 1) for i in range(count - 1)])  6.92 us
    ppermute x1, waiting for transfers between devices, passed_along(): return lax.ppermute(value, axis, pairs)  6.07 us
    ppermute x2, starting transfers between devices, to_left(): return lax.ppermute(value, axis, [(i + 1, i) for i in range(count - 1)])  4.89 us
    ppermute x2, waiting for transfers between devices, to_left(): return lax.ppermute(value, axis, [(i + 1, i) for i in range(count - 1)])  4.71 us
  transfers between devices with their start and end apart: 6, of which 5 were waited for; matrix products, arithmetic and copies ran while one was open for 2% of the time, Pallas kernels for 0%

profile of v9, /device:TPU:2, one launch (start us, length us, event | category | flops | bytes accessed | tf_op | source)
XLA Modules:
  0.0 166.0 jit_solution(6537743891143255845)
XLA Ops:
  0.6 1.3 copy.39
  2.0 2.5 %collective-permute-start = (bf16[1,1,96,2048]{2,3,1,0:T(8,128)(2,1)S(1)}, bf16[1,1,96,2048]{2,3,1,0:T(8,128)(2,1)S(1)}, u32[]{:S(2)}, u32[]{:S(2)}) collective-permute-start(bf16[1,1,96,2048]{2,3,1,0:T(8,128)(2,1)S(1)} %copy.39), channel_id=1, source_target_pairs={{0,896},{128,0},{256,128},{384,256},{512,384},{640,512},{768,640},... | collective-permute-start | bytes 1179656 | tf_op jit(solution)/shard_map/ppermute | solution.py:21
  4.5 0.3 copy.40
  4.8 0.3 copy.38
  5.1 6.1 %collective-permute-done = bf16[1,1,96,2048]{2,3,1,0:T(8,128)(2,1)S(1)} collective-permute-done((bf16[1,1,96,2048]{2,3,1,0:T(8,128)(2,1)S(1)}, bf16[1,1,96,2048]{2,3,1,0:T(8,128)(2,1)S(1)}, u32[]{:S(2)}, u32[]{:S(2)}) %collective-permute-start) | collective-permute-done | bytes 393248 | tf_op jit(solution)/shard_map/ppermute | solution.py:21
  11.2 0.2 fusion
  11.5 0.1 convert_element_type.46
  11.6 0.5 copy.42
  12.1 0.3 maximum_bitcast_fusion
  12.4 0.6 pad_maximum_fusion
  13.0 1.3 copy.43
  14.2 28.9 %all-to-all-start = ((bf16[32,112,128]{2,1,0:T(8,128)(2,1)}), bf16[32,112,128]{2,1,0:T(8,128)(2,1)S(1)}, u32[]{:S(2)}, u32[]{:S(2)}) async-start(bf16[32,112,128]{2,1,0:T(8,128)(2,1)} %copy.43), calls=%async_computation | async-start | bytes 1835008 | tf_op jit(solution)/shard_map/all_to_all | solution.py:151
  43.1 3.4 %collective-permute-start.1 = (bf16[256,128]{1,0:T(8,128)(2,1)S(1)}, bf16[256,128]{1,0:T(8,128)(2,1)S(1)}, u32[]{:S(2)}, u32[]{:S(2)}) collective-permute-start(bf16[256,128]{1,0:T(8,128)(2,1)S(1)} %get-tuple-element.14), channel_id=1, source_target_pairs={{0,1},{1,2},{2,3},{4,5},{5,6},{6,7},{8,9},{9,10},{10,11},{12,13},{... | collective-permute-start | bytes 196616 | tf_op jit(solution)/shard_map/ppermute | solution.py:26
  46.5 2.4 %collective-permute-start.2 = (bf16[256,128]{1,0:T(8,128)(2,1)S(1)}, bf16[256,128]{1,0:T(8,128)(2,1)S(1)}, u32[]{:S(2)}, u32[]{:S(2)}) collective-permute-start(bf16[256,128]{1,0:T(8,128)(2,1)S(1)} %get-tuple-element.15), channel_id=1, source_target_pairs={{1,0},{2,1},{3,2},{5,4},{6,5},{7,6},{9,8},{10,9},{11,10},{13,12},{... | collective-permute-start | bytes 196616 | tf_op jit(solution)/shard_map/ppermute | solution.py:31
  49.2 0.1 copy.44
  49.4 0.1 broadcast_in_dim.14
  49.5 0.1 broadcast_in_dim.15
  49.7 0.8 fusion.1.bias_ref
  50.5 2.2 %collective-permute-done.2 = bf16[256,128]{1,0:T(8,128)(2,1)S(1)} collective-permute-done((bf16[256,128]{1,0:T(8,128)(2,1)S(1)}, bf16[256,128]{1,0:T(8,128)(2,1)S(1)}, u32[]{:S(2)}, u32[]{:S(2)}) %collective-permute-start.2) | collective-permute-done | bytes 65568 | tf_op jit(solution)/shard_map/ppermute | solution.py:31
  52.7 1.0 pad_maximum_fusion.1.kv_ref
  53.7 85.4 %all-to-all-done = bf16[32,112,128]{2,1,0:T(8,128)(2,1)S(1)} async-done(((bf16[32,112,128]{2,1,0:T(8,128)(2,1)}), bf16[32,112,128]{2,1,0:T(8,128)(2,1)S(1)}, u32[]{:S(2)}, u32[]{:S(2)}) %all-to-all-start) | async-done | bytes 917536 | tf_op jit(solution)/shard_map/all_to_all | solution.py:151
  139.2 0.1 reshape.66
  139.3 0.7 add.50.dl_ref
  140.0 0.9 slice.48
  140.9 12.6 %shard_map.77 = (bf16[64,3072]{1,0:T(8,128)(2,1)}, bf16[2560,128]{1,0:T(8,128)(2,1)}, f32[256,128]{1,0:T(8,128)}, f32[256,128]{1,0:T(8,128)}, f32[256,128]{1,0:T(8,128)}, /*index=5*/f32[256,128]{1,0:T(8,128)}) custom-call(bf16[3072,128]{1,0:T(8,128)(2,1)} %bitcast.52, bf16[3584,128]{1,0:T(8,128)(2,1)} %pad_maximum_fusion.1.kv_ref, ...), custom_call_target="tpu_custom_call" | custom-call | flops 3019898880 | bytes 2908160 | tf_op jit(solution)/shard_map/pallas_call | solution.py:81
  153.6 3.5 %collective-permute-start.3 = (f32[256,128]{1,0:T(8,128)}, f32[256,128]{1,0:T(8,128)S(1)}, u32[]{:S(2)}, u32[]{:S(2)}) collective-permute-start(f32[256,128]{1,0:T(8,128)} %get-tuple-element.10), channel_id=1, source_target_pairs={{0,1},{1,2},{2,3},{4,5},{5,6},{6,7},{8,9},{9,10},{10,11},{12,13},{... | collective-permute-start | bytes 393224 | tf_op jit(solution)/shard_map/ppermute | solution.py:26
  157.1 2.4 %collective-permute-start.4 = (f32[256,128]{1,0:T(8,128)}, f32[256,128]{1,0:T(8,128)S(1)}, u32[]{:S(2)}, u32[]{:S(2)}) collective-permute-start(f32[256,128]{1,0:T(8,128)} %get-tuple-element.13), channel_id=1, source_target_pairs={{1,0},{2,1},{3,2},{5,4},{6,5},{7,6},{9,8},{10,9},{11,10},{13,12},{... | collective-permute-start | bytes 393224 | tf_op jit(solution)/shard_map/ppermute | solution.py:31
  159.5 1.2 collective-permute-done.3
  160.7 0.9 add_convert_fusion.1
  161.7 2.5 %collective-permute-done.4 = f32[256,128]{1,0:T(8,128)S(1)} collective-permute-done((f32[256,128]{1,0:T(8,128)}, f32[256,128]{1,0:T(8,128)S(1)}, u32[]{:S(2)}, u32[]{:S(2)}) %collective-permute-start.4) | collective-permute-done | bytes 131104 | tf_op jit(solution)/shard_map/ppermute | solution.py:31
  164.2 0.9 add_convert_fusion
  165.1 0.9 maximum_bitcast_fusion.1
  (32 shorter events, 0.6 us)
Async XLA Ops:
  0.6 3.8 %copy-start.2 = (bf16[1,1,96,2048]{3,2,1,0:T(8,128)(2,1)S(1)}, bf16[1,1,96,2048]{3,2,1,0:T(8,128)(2,1)}, u32[]{:S(2)}) copy-start(bf16[1,1,96,2048]{3,2,1,0:T(8,128)(2,1)} %param.8) | copy-start | bytes 1179652
  0.6 4.1 %copy-start.3 = (bf16[1,1,96,2048]{3,2,1,0:T(8,128)(2,1)S(1)}, bf16[1,1,96,2048]{3,2,1,0:T(8,128)(2,1)}, u32[]{:S(2)}) copy-start(bf16[1,1,96,2048]{3,2,1,0:T(8,128)(2,1)} %param.7) | copy-start | bytes 1179652
  2.0 9.2 %collective-permute-start = (bf16[1,1,96,2048]{2,3,1,0:T(8,128)(2,1)S(1)}, bf16[1,1,96,2048]{2,3,1,0:T(8,128)(2,1)S(1)}, u32[]{:S(2)}, u32[]{:S(2)}) collective-permute-start(bf16[1,1,96,2048]{2,3,1,0:T(8,128)(2,1)S(1)} %copy.39), channel_id=1, source_target_pairs={{0,896},{128,0},{256,128},{384,256},{512,384},{640,512},{768,640},... | collective-permute-start | bytes 1179656 | tf_op jit(solution)/shard_map/ppermute | solution.py:21
  14.2 28.9 %copy-start = (bf16[1,1,1,3072,128]{4,3,2,1,0:T(8,128)(2,1)S(1)}, bf16[1,1,1,3072,128]{4,3,2,1,0:T(8,128)(2,1)}, u32[]{:S(2)}) copy-start(bf16[1,1,1,3072,128]{4,3,2,1,0:T(8,128)(2,1)} %param.9) | copy-start | bytes 2359300
  14.2 34.8 %copy-start.5 = (s32[192,7]{0,1:T(8,128)S(1)}, s32[192,7]{0,1:T(8,128)}, u32[]{:S(2)}) copy-start(s32[192,7]{0,1:T(8,128)} %param.11) | copy-start | bytes 16132
  14.2 35.4 %copy-start.4 = (f32[1,1,1,3072]{3,2,1,0:T(1,128)S(1)}, f32[1,1,1,3072]{3,2,1,0:T(1,128)}, u32[]{:S(2)}) copy-start(f32[1,1,1,3072]{3,2,1,0:T(1,128)} %param.10) | copy-start | bytes 36868
  14.2 124.9 %all-to-all-start = ((bf16[32,112,128]{2,1,0:T(8,128)(2,1)}), bf16[32,112,128]{2,1,0:T(8,128)(2,1)S(1)}, u32[]{:S(2)}, u32[]{:S(2)}) async-start(bf16[32,112,128]{2,1,0:T(8,128)(2,1)} %copy.43), calls=%async_computation | async-start | bytes 1835008 | tf_op jit(solution)/shard_map/all_to_all | solution.py:151
  43.1 7.3 %collective-permute-start.1 = (bf16[256,128]{1,0:T(8,128)(2,1)S(1)}, bf16[256,128]{1,0:T(8,128)(2,1)S(1)}, u32[]{:S(2)}, u32[]{:S(2)}) collective-permute-start(bf16[256,128]{1,0:T(8,128)(2,1)S(1)} %get-tuple-element.14), channel_id=1, source_target_pairs={{0,1},{1,2},{2,3},{4,5},{5,6},{6,7},{8,9},{9,10},{10,11},{12,13},{... | collective-permute-start | bytes 196616 | tf_op jit(solution)/shard_map/ppermute | solution.py:26
  46.5 6.2 %collective-permute-start.2 = (bf16[256,128]{1,0:T(8,128)(2,1)S(1)}, bf16[256,128]{1,0:T(8,128)(2,1)S(1)}, u32[]{:S(2)}, u32[]{:S(2)}) collective-permute-start(bf16[256,128]{1,0:T(8,128)(2,1)S(1)} %get-tuple-element.15), channel_id=1, source_target_pairs={{1,0},{2,1},{3,2},{5,4},{6,5},{7,6},{9,8},{10,9},{11,10},{13,12},{... | collective-permute-start | bytes 196616 | tf_op jit(solution)/shard_map/ppermute | solution.py:31
  153.6 11.5 %copy-start.1 = (bf16[2560,128]{1,0:T(8,128)(2,1)S(1)}, bf16[2560,128]{1,0:T(8,128)(2,1)}, u32[]{:S(2)}) copy-start(bf16[2560,128]{1,0:T(8,128)(2,1)} %get-tuple-element.11) | copy-start | bytes 1966084
  153.6 7.2 %collective-permute-start.3 = (f32[256,128]{1,0:T(8,128)}, f32[256,128]{1,0:T(8,128)S(1)}, u32[]{:S(2)}, u32[]{:S(2)}) collective-permute-start(f32[256,128]{1,0:T(8,128)} %get-tuple-element.10), channel_id=1, source_target_pairs={{0,1},{1,2},{2,3},{4,5},{5,6},{6,7},{8,9},{9,10},{10,11},{12,13},{... | collective-permute-start | bytes 393224 | tf_op jit(solution)/shard_map/ppermute | solution.py:26
  157.1 7.1 %collective-permute-start.4 = (f32[256,128]{1,0:T(8,128)}, f32[256,128]{1,0:T(8,128)S(1)}, u32[]{:S(2)}, u32[]{:S(2)}) collective-permute-start(f32[256,128]{1,0:T(8,128)} %get-tuple-element.13), channel_id=1, source_target_pairs={{1,0},{2,1},{3,2},{5,4},{6,5},{7,6},{9,8},{10,9},{11,10},{13,12},{... | collective-permute-start | bytes 393224 | tf_op jit(solution)/shard_map/ppermute | solution.py:31

commit v10 on v8

--- a/solution.py
+++ b/solution.py
@@ -130,7 +130,8 @@
 def body(upstream, queries, attention_out, keys_values, log_totals, neighbours):
     tokens_here = queries.shape[2]
     heads = lax.axis_size("seq")
-    incoming = passed_along(upstream, "pipe", -1)
+    pieces = jnp.split(upstream, 4, axis=2)
+    incoming = jnp.concatenate([passed_along(piece, "pipe", -1) for piece in pieces], axis=2)
     query_tok = queries.reshape(tokens_here, H, HD)
     grad_tok = incoming.reshape(tokens_here, H, HD)
     out_tok = attention_out.reshape(tokens_here, H, HD)

time: 166 us -> 186 us (1.12)
  waiting for transfers between devices: 97.2 us -> 111 us
  local copies, waits for them, and re-layouts: 7.1 us -> 10.9 us
    ppermute x1 -> x4, waiting for transfers between devices: 6.07 us -> 18.6 us  [passed_along(): return lax.ppermute(value, axis, pairs)]
    unnamed x20 -> x25, local copies, waits for them, and re-layouts: 1.98 us -> 4.71 us
    ppermute x1 -> x4, starting transfers between devices: 2.47 us -> 3.99 us  [passed_along(): return lax.ppermute(value, axis, pairs)]
  transfers between devices with their start and end apart: 6 -> 9, of which waited for: 5 -> 8; matrix products, arithmetic and copies ran while one was open for 3% -> 4% of each run, Pallas kernels for 0% -> 0%
where the time goes in v10:
time: 186 us
  waiting for transfers between devices  111 us (60%)
  starting transfers between devices  44.7 us (24%)
  Pallas kernels  12.7 us (7%)
  local copies, waits for them, and re-layouts  10.9 us (6%)
  other arithmetic  5.94 us (3%)
    all_to_all x1, waiting for transfers between devices, body(): got = lax.all_to_all(send, 'seq', split_axis=0, concat_axis=0, tiled=True)  85.4 us
    all_to_all x1, starting transfers between devices, body(): got = lax.all_to_all(send, 'seq', split_axis=0, concat_axis=0, tiled=True)  28.9 us
    ppermute x4, waiting for transfers between devices, passed_along(): return lax.ppermute(value, axis, pairs)  18.6 us
    pallas_call x1, Pallas kernels, band_grads(): pl.pallas_call(band_kernel, out_shape=(jax.ShapeDtypeStruct((HD, rows), j...  12.7 us
    ppermute x2, starting transfers between devices, to_right(): return lax.ppermute(value, axis, [(i, i + 1) for i in range(count - 1)])  6.93 us
    ppermute x2, waiting for transfers between devices, to_left(): return lax.ppermute(value, axis, [(i + 1, i) for i in range(count - 1)])  6.52 us
    ppermute x2, starting transfers between devices, to_left(): return lax.ppermute(value, axis, [(i + 1, i) for i in range(count - 1)])  4.89 us
    unnamed x25, local copies, waits for them, and re-layouts  4.71 us
  transfers between devices with their start and end apart: 9, of which 8 were waited for; matrix products, arithmetic and copies ran while one was open for 4% of the time, Pallas kernels for 0%

profile of v10, /device:TPU:2, one launch (start us, length us, event | category | flops | bytes accessed | tf_op | source)
XLA Modules:
  0.0 185.8 jit_solution(6089766967809530202)
XLA Ops:
  0.6 1.1 fusion.9
  1.7 1.0 copy.57
  2.7 2.5 %collective-permute-start = (bf16[1,1,24,2048]{2,3,1,0:T(8,128)(2,1)}, bf16[1,1,24,2048]{2,3,1,0:T(8,128)(2,1)S(1)}, u32[]{:S(2)}, u32[]{:S(2)}) collective-permute-start(bf16[1,1,24,2048]{2,3,1,0:T(8,128)(2,1)} %copy.57), channel_id=1, source_target_pairs={{0,896},{128,0},{256,128},{384,256},{512,384},{640,512},{768,640},... | collective-permute-start | bytes 294920 | tf_op jit(solution)/shard_map/ppermute | solution.py:21
  5.2 1.0 copy.58
  6.2 0.7 collective-permute-start.1
  6.9 1.0 copy.59
  8.1 1.0 copy.60
  9.1 0.7 collective-permute-start.3
  10.1 0.3 copy.52
  10.4 1.8 collective-permute-done
  12.2 5.6 %collective-permute-done.1 = bf16[1,1,24,2048]{2,3,1,0:T(8,128)(2,1)S(1)} collective-permute-done((bf16[1,1,24,2048]{2,3,1,0:T(8,128)(2,1)}, bf16[1,1,24,2048]{2,3,1,0:T(8,128)(2,1)S(1)}, u32[]{:S(2)}, u32[]{:S(2)}) %collective-permute-start.1) | collective-permute-done | bytes 98336 | tf_op jit(solution)/shard_map/ppermute | solution.py:21
  17.8 5.6 %collective-permute-done.2 = bf16[1,1,24,2048]{2,3,1,0:T(8,128)(2,1)S(1)} collective-permute-done((bf16[1,1,24,2048]{2,3,1,0:T(8,128)(2,1)}, bf16[1,1,24,2048]{2,3,1,0:T(8,128)(2,1)S(1)}, u32[]{:S(2)}, u32[]{:S(2)}) %collective-permute-start.2) | collective-permute-done | bytes 98336 | tf_op jit(solution)/shard_map/ppermute | solution.py:21
  23.4 5.6 %collective-permute-done.3 = bf16[1,1,24,2048]{2,3,1,0:T(8,128)(2,1)} collective-permute-done((bf16[1,1,24,2048]{2,3,1,0:T(8,128)(2,1)}, bf16[1,1,24,2048]{2,3,1,0:T(8,128)(2,1)}, u32[]{:S(2)}, u32[]{:S(2)}) %collective-permute-start.3) | collective-permute-done | bytes 98336 | tf_op jit(solution)/shard_map/ppermute | solution.py:21
  29.0 1.7 pad_maximum_fusion.2
  31.2 0.5 copy.54
  32.0 0.6 pad_maximum_fusion
  32.6 1.3 copy.55
  33.9 28.9 %all-to-all-start = ((bf16[32,112,128]{2,1,0:T(8,128)(2,1)}), bf16[32,112,128]{2,1,0:T(8,128)(2,1)S(1)}, u32[]{:S(2)}, u32[]{:S(2)}) async-start(bf16[32,112,128]{2,1,0:T(8,128)(2,1)} %copy.55), calls=%async_computation | async-start | bytes 1835008 | tf_op jit(solution)/shard_map/all_to_all | solution.py:152
  62.8 3.4 %collective-permute-start.4 = (bf16[256,128]{1,0:T(8,128)(2,1)S(1)}, bf16[256,128]{1,0:T(8,128)(2,1)S(1)}, u32[]{:S(2)}, u32[]{:S(2)}) collective-permute-start(bf16[256,128]{1,0:T(8,128)(2,1)S(1)} %get-tuple-element.14), channel_id=1, source_target_pairs={{0,1},{1,2},{2,3},{4,5},{5,6},{6,7},{8,9},{9,10},{10,11},{12,13},{... | collective-permute-start | bytes 196616 | tf_op jit(solution)/shard_map/ppermute | solution.py:26
  66.2 2.4 %collective-permute-start.5 = (bf16[256,128]{1,0:T(8,128)(2,1)S(1)}, bf16[256,128]{1,0:T(8,128)(2,1)S(1)}, u32[]{:S(2)}, u32[]{:S(2)}) collective-permute-start(bf16[256,128]{1,0:T(8,128)(2,1)S(1)} %get-tuple-element.15), channel_id=1, source_target_pairs={{1,0},{2,1},{3,2},{5,4},{6,5},{7,6},{9,8},{10,9},{11,10},{13,12},{... | collective-permute-start | bytes 196616 | tf_op jit(solution)/shard_map/ppermute | solution.py:31
  69.3 0.8 fusion.1.bias_ref
  70.1 2.2 %collective-permute-done.5 = bf16[256,128]{1,0:T(8,128)(2,1)S(1)} collective-permute-done((bf16[256,128]{1,0:T(8,128)(2,1)S(1)}, bf16[256,128]{1,0:T(8,128)(2,1)S(1)}, u32[]{:S(2)}, u32[]{:S(2)}) %collective-permute-start.5) | collective-permute-done | bytes 65568 | tf_op jit(solution)/shard_map/ppermute | solution.py:31
  72.3 1.0 pad_maximum_fusion.1.kv_ref
  73.3 85.4 %all-to-all-done = bf16[32,112,128]{2,1,0:T(8,128)(2,1)S(1)} async-done(((bf16[32,112,128]{2,1,0:T(8,128)(2,1)}), bf16[32,112,128]{2,1,0:T(8,128)(2,1)S(1)}, u32[]{:S(2)}, u32[]{:S(2)}) %all-to-all-start) | async-done | bytes 917536 | tf_op jit(solution)/shard_map/all_to_all | solution.py:152
  159.0 0.7 add.50.dl_ref
  159.6 0.9 slice.52
  160.6 12.7 %shard_map.77 = (bf16[64,3072]{1,0:T(8,128)(2,1)}, bf16[3072,128]{1,0:T(8,128)(2,1)}, f32[256,128]{1,0:T(8,128)}, f32[256,128]{1,0:T(8,128)}, f32[256,128]{1,0:T(8,128)}, /*index=5*/f32[256,128]{1,0:T(8,128)}) custom-call(bf16[3072,128]{1,0:T(8,128)(2,1)} %bitcast.52, bf16[3584,128]{1,0:T(8,128)(2,1)} %pad_maximum_fusion.1.kv_ref, ...), custom_call_target="tpu_custom_call" | custom-call | flops 3019898880 | bytes 2908160 | tf_op jit(solution)/shard_map/pallas_call | solution.py:81
  173.3 3.5 %collective-permute-start.6 = (f32[256,128]{1,0:T(8,128)}, f32[256,128]{1,0:T(8,128)S(1)}, u32[]{:S(2)}, u32[]{:S(2)}) collective-permute-start(f32[256,128]{1,0:T(8,128)} %get-tuple-element.10), channel_id=1, source_target_pairs={{0,1},{1,2},{2,3},{4,5},{5,6},{6,7},{8,9},{9,10},{10,11},{12,13},{... | collective-permute-start | bytes 393224 | tf_op jit(solution)/shard_map/ppermute | solution.py:26
  176.8 1.1 slice.51
  177.9 2.4 %collective-permute-start.7 = (f32[256,128]{1,0:T(8,128)S(1)}, f32[256,128]{1,0:T(8,128)S(1)}, u32[]{:S(2)}, u32[]{:S(2)}) collective-permute-start(f32[256,128]{1,0:T(8,128)S(1)} %copy-done.7), channel_id=1, source_target_pairs={{1,0},{2,1},{3,2},{5,4},{6,5},{7,6},{9,8},{10,9},{11,10},{13,12},{... | collective-permute-start | bytes 393224 | tf_op jit(solution)/shard_map/ppermute | solution.py:31
  180.5 4.3 %collective-permute-done.7 = f32[256,128]{1,0:T(8,128)S(1)} collective-permute-done((f32[256,128]{1,0:T(8,128)S(1)}, f32[256,128]{1,0:T(8,128)S(1)}, u32[]{:S(2)}, u32[]{:S(2)}) %collective-permute-start.7) | collective-permute-done | bytes 131104 | tf_op jit(solution)/shard_map/ppermute | solution.py:31
  184.8 0.9 maximum_bitcast_fusion.1
  (48 shorter events, 2.1 us)
Async XLA Ops:
  2.7 7.1 %copy-start.1 = (bf16[1,1,96,2048]{3,2,1,0:T(8,128)(2,1)S(1)}, bf16[1,1,96,2048]{3,2,1,0:T(8,128)(2,1)}, u32[]{:S(2)}) copy-start(bf16[1,1,96,2048]{3,2,1,0:T(8,128)(2,1)} %param.7) | copy-start | bytes 1179652
  2.7 9.5 %collective-permute-start = (bf16[1,1,24,2048]{2,3,1,0:T(8,128)(2,1)}, bf16[1,1,24,2048]{2,3,1,0:T(8,128)(2,1)S(1)}, u32[]{:S(2)}, u32[]{:S(2)}) collective-permute-start(bf16[1,1,24,2048]{2,3,1,0:T(8,128)(2,1)} %copy.57), channel_id=1, source_target_pairs={{0,896},{128,0},{256,128},{384,256},{512,384},{640,512},{768,640},... | collective-permute-start | bytes 294920 | tf_op jit(solution)/shard_map/ppermute | solution.py:21
  6.2 11.6 %collective-permute-start.1 = (bf16[1,1,24,2048]{2,3,1,0:T(8,128)(2,1)}, bf16[1,1,24,2048]{2,3,1,0:T(8,128)(2,1)S(1)}, u32[]{:S(2)}, u32[]{:S(2)}) collective-permute-start(bf16[1,1,24,2048]{2,3,1,0:T(8,128)(2,1)} %copy.58), channel_id=1, source_target_pairs={{0,896},{128,0},{256,128},{384,256},{512,384},{640,512},{768,640},... | collective-permute-start | bytes 294920 | tf_op jit(solution)/shard_map/ppermute | solution.py:21
  7.9 15.5 %collective-permute-start.2 = (bf16[1,1,24,2048]{2,3,1,0:T(8,128)(2,1)}, bf16[1,1,24,2048]{2,3,1,0:T(8,128)(2,1)S(1)}, u32[]{:S(2)}, u32[]{:S(2)}) collective-permute-start(bf16[1,1,24,2048]{2,3,1,0:T(8,128)(2,1)} %copy.59), channel_id=1, source_target_pairs={{0,896},{128,0},{256,128},{384,256},{512,384},{640,512},{768,640},... | collective-permute-start | bytes 294920 | tf_op jit(solution)/shard_map/ppermute | solution.py:21
  9.1 1.0 copy-start.2
  9.1 19.9 %collective-permute-start.3 = (bf16[1,1,24,2048]{2,3,1,0:T(8,128)(2,1)}, bf16[1,1,24,2048]{2,3,1,0:T(8,128)(2,1)}, u32[]{:S(2)}, u32[]{:S(2)}) collective-permute-start(bf16[1,1,24,2048]{2,3,1,0:T(8,128)(2,1)} %copy.60), channel_id=1, source_target_pairs={{0,896},{128,0},{256,128},{384,256},{512,384},{640,512},{768,640},... | collective-permute-start | bytes 294920 | tf_op jit(solution)/shard_map/ppermute | solution.py:21
  33.9 28.9 %copy-start = (bf16[1,1,1,3072,128]{4,3,2,1,0:T(8,128)(2,1)S(1)}, bf16[1,1,1,3072,128]{4,3,2,1,0:T(8,128)(2,1)}, u32[]{:S(2)}) copy-start(bf16[1,1,1,3072,128]{4,3,2,1,0:T(8,128)(2,1)} %param.9) | copy-start | bytes 2359300
  33.9 34.8 %copy-start.6 = (s32[192,7]{0,1:T(8,128)S(1)}, s32[192,7]{0,1:T(8,128)}, u32[]{:S(2)}) copy-start(s32[192,7]{0,1:T(8,128)} %param.11) | copy-start | bytes 16132
  33.9 35.4 %copy-start.5 = (f32[1,1,1,3072]{3,2,1,0:T(1,128)S(1)}, f32[1,1,1,3072]{3,2,1,0:T(1,128)}, u32[]{:S(2)}) copy-start(f32[1,1,1,3072]{3,2,1,0:T(1,128)} %param.10) | copy-start | bytes 36868
  33.9 124.9 %all-to-all-start = ((bf16[32,112,128]{2,1,0:T(8,128)(2,1)}), bf16[32,112,128]{2,1,0:T(8,128)(2,1)S(1)}, u32[]{:S(2)}, u32[]{:S(2)}) async-start(bf16[32,112,128]{2,1,0:T(8,128)(2,1)} %copy.55), calls=%async_computation | async-start | bytes 1835008 | tf_op jit(solution)/shard_map/all_to_all | solution.py:152
  62.8 7.4 %collective-permute-start.4 = (bf16[256,128]{1,0:T(8,128)(2,1)S(1)}, bf16[256,128]{1,0:T(8,128)(2,1)S(1)}, u32[]{:S(2)}, u32[]{:S(2)}) collective-permute-start(bf16[256,128]{1,0:T(8,128)(2,1)S(1)} %get-tuple-element.14), channel_id=1, source_target_pairs={{0,1},{1,2},{2,3},{4,5},{5,6},{6,7},{8,9},{9,10},{10,11},{12,13},{... | collective-permute-start | bytes 196616 | tf_op jit(solution)/shard_map/ppermute | solution.py:26
  66.2 6.2 %collective-permute-start.5 = (bf16[256,128]{1,0:T(8,128)(2,1)S(1)}, bf16[256,128]{1,0:T(8,128)(2,1)S(1)}, u32[]{:S(2)}, u32[]{:S(2)}) collective-permute-start(bf16[256,128]{1,0:T(8,128)(2,1)S(1)} %get-tuple-element.15), channel_id=1, source_target_pairs={{1,0},{2,1},{3,2},{5,4},{6,5},{7,6},{9,8},{10,9},{11,10},{13,12},{... | collective-permute-start | bytes 196616 | tf_op jit(solution)/shard_map/ppermute | solution.py:31
  173.2 4.7 %copy-start.7 = (f32[256,128]{1,0:T(8,128)S(1)}, f32[256,128]{1,0:T(8,128)}, u32[]{:S(2)}) copy-start(f32[256,128]{1,0:T(8,128)} %get-tuple-element.13) | copy-start | bytes 393220
  173.2 7.2 %copy-start.4 = (f32[256,128]{1,0:T(8,128)S(1)}, f32[256,128]{1,0:T(8,128)}, u32[]{:S(2)}) copy-start(f32[256,128]{1,0:T(8,128)} %get-tuple-element.9) | copy-start | bytes 393220
  173.2 11.6 %copy-start.3 = (f32[256,128]{1,0:T(8,128)S(1)}, f32[256,128]{1,0:T(8,128)}, u32[]{:S(2)}) copy-start(f32[256,128]{1,0:T(8,128)} %get-tuple-element.12) | copy-start | bytes 393220
  173.3 7.2 %collective-permute-start.6 = (f32[256,128]{1,0:T(8,128)}, f32[256,128]{1,0:T(8,128)S(1)}, u32[]{:S(2)}, u32[]{:S(2)}) collective-permute-start(f32[256,128]{1,0:T(8,128)} %get-tuple-element.10), channel_id=1, source_target_pairs={{0,1},{1,2},{2,3},{4,5},{5,6},{6,7},{8,9},{9,10},{10,11},{12,13},{... | collective-permute-start | bytes 393224 | tf_op jit(solution)/shard_map/ppermute | solution.py:26
  177.9 6.9 %collective-permute-start.7 = (f32[256,128]{1,0:T(8,128)S(1)}, f32[256,128]{1,0:T(8,128)S(1)}, u32[]{:S(2)}, u32[]{:S(2)}) collective-permute-start(f32[256,128]{1,0:T(8,128)S(1)} %copy-done.7), channel_id=1, source_target_pairs={{1,0},{2,1},{3,2},{5,4},{6,5},{7,6},{9,8},{10,9},{11,10},{13,12},{... | collective-permute-start | bytes 393224 | tf_op jit(solution)/shard_map/ppermute | solution.py:31

commit v11 on v8

--- a/solution.py
+++ b/solution.py
@@ -66,8 +66,8 @@
     cache_out[...] = cache_ref[pl.ds(rim, rows), :].astype(cache_out.dtype)
     head_ref[...] = cache_ref[pl.ds(rim, rim), :]
     tail_ref[...] = cache_ref[pl.ds(rows, rim), :]
-    left_ref[...] = cache_ref[pl.ds(0, rim), :]
-    right_ref[...] = cache_ref[pl.ds(rows + rim, rim), :]
+    left_ref[...] = cache_ref[pl.ds(0, rim), :].astype(left_ref.dtype)
+    right_ref[...] = cache_ref[pl.ds(rows + rim, rim), :].astype(right_ref.dtype)
 
 
 def band_grads(pair, kv_pad, bias, dl):
@@ -83,7 +83,8 @@
         out_shape=(
             jax.ShapeDtypeStruct((HD, rows), jnp.bfloat16),
             jax.ShapeDtypeStruct((rows, 2 * HD), jnp.bfloat16),
-        ) + (jax.ShapeDtypeStruct((rim, 2 * HD), jnp.float32),) * 4,
+        ) + (jax.ShapeDtypeStruct((rim, 2 * HD), jnp.float32),) * 2
+        + (jax.ShapeDtypeStruct((rim, 2 * HD), jnp.bfloat16),) * 2,
         in_specs=[vmem] * 4,
         out_specs=(vmem,) * 6,
         scratch_shapes=[pltpu.VMEM((pad_rows, 2 * HD), jnp.float32)],
@@ -169,9 +170,9 @@
     from_left = to_right(right_rim, "tp")
     cache_own = jnp.concatenate(
         [
-            (head_part + from_left).astype(jnp.bfloat16),
+            (head_part + from_left.astype(jnp.float32)).astype(jnp.bfloat16),
             cache_own[rim : rows_here - rim],
-            (tail_part + from_right).astype(jnp.bfloat16),
+            (tail_part + from_right.astype(jnp.float32)).astype(jnp.bfloat16),
         ],
         axis=0,
     )

time: 166 us -> 165 us (level)
  transfers between devices with their start and end apart: 6 -> 6, of which waited for: 5 -> 4; matrix products, arithmetic and copies ran while one was open for 3% -> 3% of each run, Pallas kernels for 0% -> 0%
where the time goes in v11:
time: 165 us; the launch traced here: 164 us
  waiting for transfers between devices  96.4 us (58%)
  starting transfers between devices  43.1 us (26%)
  Pallas kernels  12.6 us (8%)
  local copies, waits for them, and re-layouts  7.1 us (4%)
  other arithmetic  4.19 us (3%)
    all_to_all x1, waiting for transfers between devices, body(): got = lax.all_to_all(send, 'seq', split_axis=0, concat_axis=0, tiled=True)  85.4 us
    all_to_all x1, starting transfers between devices, body(): got = lax.all_to_all(send, 'seq', split_axis=0, concat_axis=0, tiled=True)  28.9 us
    pallas_call x1, Pallas kernels, band_grads(): pl.pallas_call(band_kernel, out_shape=(jax.ShapeDtypeStruct((HD, rows), j...  12.6 us
    ppermute x2, starting transfers between devices, to_right(): return lax.ppermute(value, axis, [(i, i + 1) for i in range(count - 1)])  6.92 us
    ppermute x1, waiting for transfers between devices, passed_along(): return lax.ppermute(value, axis, pairs)  6.07 us
    ppermute x2, waiting for transfers between devices, to_left(): return lax.ppermute(value, axis, [(i + 1, i) for i in range(count - 1)])  4.98 us
    ppermute x2, starting transfers between devices, to_left(): return lax.ppermute(value, axis, [(i + 1, i) for i in range(count - 1)])  4.88 us
  transfers between devices with their start and end apart: 6, of which 4 were waited for; matrix products, arithmetic and copies ran while one was open for 3% of the time, Pallas kernels for 0%

profile of v11, /device:TPU:2, one launch (start us, length us, event | category | flops | bytes accessed | tf_op | source)
XLA Modules:
  0.0 164.4 jit_solution(770426172793081325)
XLA Ops:
  0.6 1.3 copy.39
  2.0 2.5 %collective-permute-start = (bf16[1,1,96,2048]{2,3,1,0:T(8,128)(2,1)S(1)}, bf16[1,1,96,2048]{2,3,1,0:T(8,128)(2,1)S(1)}, u32[]{:S(2)}, u32[]{:S(2)}) collective-permute-start(bf16[1,1,96,2048]{2,3,1,0:T(8,128)(2,1)S(1)} %copy.39), channel_id=1, source_target_pairs={{0,896},{128,0},{256,128},{384,256},{512,384},{640,512},{768,640},... | collective-permute-start | bytes 1179656 | tf_op jit(solution)/shard_map/ppermute | solution.py:21
  4.5 0.3 copy.40
  4.8 0.3 copy.38
  5.1 6.1 %collective-permute-done = bf16[1,1,96,2048]{2,3,1,0:T(8,128)(2,1)S(1)} collective-permute-done((bf16[1,1,96,2048]{2,3,1,0:T(8,128)(2,1)S(1)}, bf16[1,1,96,2048]{2,3,1,0:T(8,128)(2,1)S(1)}, u32[]{:S(2)}, u32[]{:S(2)}) %collective-permute-start) | collective-permute-done | bytes 393248 | tf_op jit(solution)/shard_map/ppermute | solution.py:21
  11.2 0.2 fusion
  11.5 0.1 convert_element_type.52
  11.6 0.5 copy.42
  12.1 0.3 maximum_bitcast_fusion
  12.4 0.6 pad_maximum_fusion
  13.0 1.3 copy.43
  14.2 28.9 %all-to-all-start = ((bf16[32,112,128]{2,1,0:T(8,128)(2,1)}), bf16[32,112,128]{2,1,0:T(8,128)(2,1)S(1)}, u32[]{:S(2)}, u32[]{:S(2)}) async-start(bf16[32,112,128]{2,1,0:T(8,128)(2,1)} %copy.43), calls=%async_computation | async-start | bytes 1835008 | tf_op jit(solution)/shard_map/all_to_all | solution.py:152
  43.1 3.4 %collective-permute-start.1 = (bf16[256,128]{1,0:T(8,128)(2,1)S(1)}, bf16[256,128]{1,0:T(8,128)(2,1)S(1)}, u32[]{:S(2)}, u32[]{:S(2)}) collective-permute-start(bf16[256,128]{1,0:T(8,128)(2,1)S(1)} %get-tuple-element.14), channel_id=1, source_target_pairs={{0,1},{1,2},{2,3},{4,5},{5,6},{6,7},{8,9},{9,10},{10,11},{12,13},{... | collective-permute-start | bytes 196616 | tf_op jit(solution)/shard_map/ppermute | solution.py:26
  46.5 2.4 %collective-permute-start.2 = (bf16[256,128]{1,0:T(8,128)(2,1)S(1)}, bf16[256,128]{1,0:T(8,128)(2,1)S(1)}, u32[]{:S(2)}, u32[]{:S(2)}) collective-permute-start(bf16[256,128]{1,0:T(8,128)(2,1)S(1)} %get-tuple-element.15), channel_id=1, source_target_pairs={{1,0},{2,1},{3,2},{5,4},{6,5},{7,6},{9,8},{10,9},{11,10},{13,12},{... | collective-permute-start | bytes 196616 | tf_op jit(solution)/shard_map/ppermute | solution.py:31
  49.0 0.1 dynamic-slice_compare_fusion
  49.1 0.1 subtract_add_fusion
  49.2 0.1 copy.44
  49.4 0.1 broadcast_in_dim.14
  49.5 0.1 broadcast_in_dim.15
  49.7 0.8 fusion.1.bias_ref
  50.5 2.2 %collective-permute-done.2 = bf16[256,128]{1,0:T(8,128)(2,1)S(1)} collective-permute-done((bf16[256,128]{1,0:T(8,128)(2,1)S(1)}, bf16[256,128]{1,0:T(8,128)(2,1)S(1)}, u32[]{:S(2)}, u32[]{:S(2)}) %collective-permute-start.2) | collective-permute-done | bytes 65568 | tf_op jit(solution)/shard_map/ppermute | solution.py:31
  52.7 1.0 pad_maximum_fusion.1.kv_ref
  53.7 85.4 %all-to-all-done = bf16[32,112,128]{2,1,0:T(8,128)(2,1)S(1)} async-done(((bf16[32,112,128]{2,1,0:T(8,128)(2,1)}), bf16[32,112,128]{2,1,0:T(8,128)(2,1)S(1)}, u32[]{:S(2)}, u32[]{:S(2)}) %all-to-all-start) | async-done | bytes 917536 | tf_op jit(solution)/shard_map/all_to_all | solution.py:152
  139.2 0.1 reshape.66
  139.3 0.7 add.50.dl_ref
  140.0 0.9 slice.52
  140.9 12.6 %shard_map.77 = (bf16[64,3072]{1,0:T(8,128)(2,1)}, bf16[3072,128]{1,0:T(8,128)(2,1)}, f32[256,128]{1,0:T(8,128)}, f32[256,128]{1,0:T(8,128)}, bf16[256,128]{1,0:T(8,128)(2,1)}, /*index=5*/bf16[256,128]{1,0:T(8,128)(2,1)}) custom-call(bf16[3072,128]{1,0:T(8,128)(2,1)} %bitcast.52, bf16[3584,128]{1,0:T(8,128)(2,1)} %pad_maximum_fusion.1.kv_ref, ...), custom_call_target="tpu_custom_call" | custom-call | flops 3019898880 | bytes 2908160 | tf_op jit(solution)/shard_map/pallas_call | solution.py:81
  153.6 3.5 %collective-permute-start.3 = (bf16[256,128]{1,0:T(8,128)(2,1)}, bf16[256,128]{1,0:T(8,128)(2,1)S(1)}, u32[]{:S(2)}, u32[]{:S(2)}) collective-permute-start(bf16[256,128]{1,0:T(8,128)(2,1)} %get-tuple-element.10), channel_id=1, source_target_pairs={{0,1},{1,2},{2,3},{4,5},{5,6},{6,7},{8,9},{9,10},{10,11},{12,13},{... | collective-permute-start | bytes 196616 | tf_op jit(solution)/shard_map/ppermute | solution.py:26
  157.1 2.4 %collective-permute-start.4 = (bf16[256,128]{1,0:T(8,128)(2,1)}, bf16[256,128]{1,0:T(8,128)(2,1)S(1)}, u32[]{:S(2)}, u32[]{:S(2)}) collective-permute-start(bf16[256,128]{1,0:T(8,128)(2,1)} %get-tuple-element.13), channel_id=1, source_target_pairs={{1,0},{2,1},{3,2},{5,4},{6,5},{7,6},{9,8},{10,9},{11,10},{13,12},{... | collective-permute-start | bytes 196616 | tf_op jit(solution)/shard_map/ppermute | solution.py:31
  159.6 1.1 slice.51
  160.7 2.7 %collective-permute-done.4 = bf16[256,128]{1,0:T(8,128)(2,1)S(1)} collective-permute-done((bf16[256,128]{1,0:T(8,128)(2,1)}, bf16[256,128]{1,0:T(8,128)(2,1)S(1)}, u32[]{:S(2)}, u32[]{:S(2)}) %collective-permute-start.4) | collective-permute-done | bytes 65568 | tf_op jit(solution)/shard_map/ppermute | solution.py:31
  163.5 0.9 maximum_bitcast_fusion.1
  (35 shorter events, 0.5 us)
Async XLA Ops:
  0.6 3.8 %copy-start.1 = (bf16[1,1,96,2048]{3,2,1,0:T(8,128)(2,1)S(1)}, bf16[1,1,96,2048]{3,2,1,0:T(8,128)(2,1)}, u32[]{:S(2)}) copy-start(bf16[1,1,96,2048]{3,2,1,0:T(8,128)(2,1)} %param.8) | copy-start | bytes 1179652
  0.6 4.1 %copy-start.2 = (bf16[1,1,96,2048]{3,2,1,0:T(8,128)(2,1)S(1)}, bf16[1,1,96,2048]{3,2,1,0:T(8,128)(2,1)}, u32[]{:S(2)}) copy-start(bf16[1,1,96,2048]{3,2,1,0:T(8,128)(2,1)} %param.7) | copy-start | bytes 1179652
  2.0 9.2 %collective-permute-start = (bf16[1,1,96,2048]{2,3,1,0:T(8,128)(2,1)S(1)}, bf16[1,1,96,2048]{2,3,1,0:T(8,128)(2,1)S(1)}, u32[]{:S(2)}, u32[]{:S(2)}) collective-permute-start(bf16[1,1,96,2048]{2,3,1,0:T(8,128)(2,1)S(1)} %copy.39), channel_id=1, source_target_pairs={{0,896},{128,0},{256,128},{384,256},{512,384},{640,512},{768,640},... | collective-permute-start | bytes 1179656 | tf_op jit(solution)/shard_map/ppermute | solution.py:21
  14.2 28.9 %copy-start = (bf16[1,1,1,3072,128]{4,3,2,1,0:T(8,128)(2,1)S(1)}, bf16[1,1,1,3072,128]{4,3,2,1,0:T(8,128)(2,1)}, u32[]{:S(2)}) copy-start(bf16[1,1,1,3072,128]{4,3,2,1,0:T(8,128)(2,1)} %param.9) | copy-start | bytes 2359300
  14.2 34.8 %copy-start.6 = (s32[192,7]{0,1:T(8,128)S(1)}, s32[192,7]{0,1:T(8,128)}, u32[]{:S(2)}) copy-start(s32[192,7]{0,1:T(8,128)} %param.11) | copy-start | bytes 16132
  14.2 35.4 %copy-start.5 = (f32[1,1,1,3072]{3,2,1,0:T(1,128)S(1)}, f32[1,1,1,3072]{3,2,1,0:T(1,128)}, u32[]{:S(2)}) copy-start(f32[1,1,1,3072]{3,2,1,0:T(1,128)} %param.10) | copy-start | bytes 36868
  14.2 124.9 %all-to-all-start = ((bf16[32,112,128]{2,1,0:T(8,128)(2,1)}), bf16[32,112,128]{2,1,0:T(8,128)(2,1)S(1)}, u32[]{:S(2)}, u32[]{:S(2)}) async-start(bf16[32,112,128]{2,1,0:T(8,128)(2,1)} %copy.43), calls=%async_computation | async-start | bytes 1835008 | tf_op jit(solution)/shard_map/all_to_all | solution.py:152
  43.1 7.3 %collective-permute-start.1 = (bf16[256,128]{1,0:T(8,128)(2,1)S(1)}, bf16[256,128]{1,0:T(8,128)(2,1)S(1)}, u32[]{:S(2)}, u32[]{:S(2)}) collective-permute-start(bf16[256,128]{1,0:T(8,128)(2,1)S(1)} %get-tuple-element.14), channel_id=1, source_target_pairs={{0,1},{1,2},{2,3},{4,5},{5,6},{6,7},{8,9},{9,10},{10,11},{12,13},{... | collective-permute-start | bytes 196616 | tf_op jit(solution)/shard_map/ppermute | solution.py:26
  46.5 6.2 %collective-permute-start.2 = (bf16[256,128]{1,0:T(8,128)(2,1)S(1)}, bf16[256,128]{1,0:T(8,128)(2,1)S(1)}, u32[]{:S(2)}, u32[]{:S(2)}) collective-permute-start(bf16[256,128]{1,0:T(8,128)(2,1)S(1)} %get-tuple-element.15), channel_id=1, source_target_pairs={{1,0},{2,1},{3,2},{5,4},{6,5},{7,6},{9,8},{10,9},{11,10},{13,12},{... | collective-permute-start | bytes 196616 | tf_op jit(solution)/shard_map/ppermute | solution.py:31
  153.6 7.1 %copy-start.4 = (f32[256,128]{1,0:T(8,128)S(1)}, f32[256,128]{1,0:T(8,128)}, u32[]{:S(2)}) copy-start(f32[256,128]{1,0:T(8,128)} %get-tuple-element.9) | copy-start | bytes 393220
  153.6 9.9 %copy-start.3 = (f32[256,128]{1,0:T(8,128)S(1)}, f32[256,128]{1,0:T(8,128)}, u32[]{:S(2)}) copy-start(f32[256,128]{1,0:T(8,128)} %get-tuple-element.12) | copy-start | bytes 393220
  153.6 7.1 %collective-permute-start.3 = (bf16[256,128]{1,0:T(8,128)(2,1)}, bf16[256,128]{1,0:T(8,128)(2,1)S(1)}, u32[]{:S(2)}, u32[]{:S(2)}) collective-permute-start(bf16[256,128]{1,0:T(8,128)(2,1)} %get-tuple-element.10), channel_id=1, source_target_pairs={{0,1},{1,2},{2,3},{4,5},{5,6},{6,7},{8,9},{9,10},{10,11},{12,13},{... | collective-permute-start | bytes 196616 | tf_op jit(solution)/shard_map/ppermute | solution.py:26
  157.1 6.4 %collective-permute-start.4 = (bf16[256,128]{1,0:T(8,128)(2,1)}, bf16[256,128]{1,0:T(8,128)(2,1)S(1)}, u32[]{:S(2)}, u32[]{:S(2)}) collective-permute-start(bf16[256,128]{1,0:T(8,128)(2,1)} %get-tuple-element.13), channel_id=1, source_target_pairs={{1,0},{2,1},{3,2},{5,4},{6,5},{7,6},{9,8},{10,9},{11,10},{13,12},{... | collective-permute-start | bytes 196616 | tf_op jit(solution)/shard_map/ppermute | solution.py:31

commit v12 on v8

--- a/solution.py
+++ b/solution.py
@@ -32,16 +32,16 @@
 
 
 def band_kernel(pair_ref, kv_ref, bias_ref, dl_ref, qgt_ref, cache_out, head_ref, tail_ref, left_ref, right_ref, cache_ref):
-    steps = pair_ref.shape[0] // (2 * BLK)
+    rows = qgt_ref.shape[1]
+    chunk = pair_ref.shape[0] // H
+    tokens = rows // H
     span = 2 * BLK
     win = (WIDTH + 1) * BLK
     rim = REACH * BLK
-    rows = pair_ref.shape[0]
     cache_ref[...] = jnp.zeros_like(cache_ref)
 
-    def step(i, carry):
+    def step(i, pair):
         r = pl.multiple_of(i * span, span)
-        pair = pair_ref[pl.ds(r, span), :]
         lane = lax.broadcasted_iota(jnp.int32, pair.shape, 1)
         zero = jnp.zeros_like(pair)
         rz = jnp.concatenate([jnp.where(lane < HD, pair, zero), jnp.where(lane < HD, zero, pair)], axis=0)
@@ -60,9 +60,22 @@
         tn = (((0,), (0,)), ((), ()))
         qgt = lax.dot_general(kvw, gst, tn, preferred_element_type=jnp.float32)
         qgt_ref[:, pl.ds(r, span)] = (qgt[:HD] * (HD ** -0.5)).astype(qgt_ref.dtype)
+
+    per = tokens // (span - tokens)
+    group = per + 1
+
+    def grouped(g, carry):
+        for c in range(per):
+            first = c * span
+            src0, off0 = divmod(first, tokens)
+            take0 = tokens - off0
+            base = g * group
+            a = pair_ref[pl.ds(pl.multiple_of((base + src0) * chunk + off0, 16), take0), :]
+            b = pair_ref[pl.ds(pl.multiple_of((base + src0 + 1) * chunk, 16), span - take0), :]
+            step(g * per + c, jnp.concatenate([a, b], axis=0))
         return carry
 
-    lax.fori_loop(0, steps, step, 0, unroll=2)
+    lax.fori_loop(0, rows // (span * per), grouped, 0)
     cache_out[...] = cache_ref[pl.ds(rim, rows), :].astype(cache_out.dtype)
     head_ref[...] = cache_ref[pl.ds(rim, rim), :]
     tail_ref[...] = cache_ref[pl.ds(rows, rim), :]
@@ -71,7 +84,7 @@
 
 
 def band_grads(pair, kv_pad, bias, dl):
-    rows = pair.shape[0]
+    rows = dl.size
     steps = rows // (2 * BLK)
     pad_rows = kv_pad.shape[0]
     win = (WIDTH + 1) * BLK
@@ -104,7 +117,7 @@
 
 
 def local_grads(pair, delta_h, lse_h, kv_pad, listed, first_block):
-    rows_here = pair.shape[0]
+    rows_here = delta_h.shape[0]
     blocks_here = rows_here // BLK
     steps = blocks_here // 2
     lane = 128
@@ -151,7 +164,7 @@
     got = lax.all_to_all(send, "seq", split_axis=0, concat_axis=0, tiled=True)
     rows_here = heads * tokens_here
     blocks_here = rows_here // BLK
-    pair = got[:, :tokens_here].reshape(rows_here, 2 * HD)
+    pair = got.reshape(heads * (tokens_here + d_rows), 2 * HD)
     d3 = got[:, tokens_here:].reshape(heads, d_rows * lane)[:, :d_vals]
     d3 = d3.reshape(heads, 3, tokens_here).astype(jnp.float32)
     delta_h = ((d3[:, 0] + d3[:, 1]) + d3[:, 2]).reshape(rows_here)

time: 166 us -> 164 us (0.988)
  no operation moved by 1% of the time
where the time goes in v12:
time: 164 us
  waiting for transfers between devices  97.2 us (59%)
  starting transfers between devices  43.1 us (26%)
  Pallas kernels  11.9 us (7%)
  local copies, waits for them, and re-layouts  6.26 us (4%)
  other arithmetic  4.2 us (3%)
    all_to_all x1, waiting for transfers between devices, body(): got = lax.all_to_all(send, 'seq', split_axis=0, concat_axis=0, tiled=True)  85.4 us
    all_to_all x1, starting transfers between devices, body(): got = lax.all_to_all(send, 'seq', split_axis=0, concat_axis=0, tiled=True)  28.9 us
    pallas_call x1, Pallas kernels, band_grads(): pl.pallas_call(band_kernel, out_shape=(jax.ShapeDtypeStruct((HD, rows), j...  11.9 us
    ppermute x2, starting transfers between devices, to_right(): return lax.ppermute(value, axis, [(i, i + 1) for i in range(count - 1)])  6.92 us
    ppermute x1, waiting for transfers between devices, passed_along(): return lax.ppermute(value, axis, pairs)  6.07 us
    ppermute x2, waiting for transfers between devices, to_left(): return lax.ppermute(value, axis, [(i + 1, i) for i in range(count - 1)])  5.61 us
    ppermute x2, starting transfers between devices, to_left(): return lax.ppermute(value, axis, [(i + 1, i) for i in range(count - 1)])  4.89 us
  transfers between devices with their start and end apart: 6, of which 5 were waited for; matrix products, arithmetic and copies ran while one was open for 3% of the time, Pallas kernels for 0%

profile of v12, /device:TPU:2, one launch (start us, length us, event | category | flops | bytes accessed | tf_op | source)
XLA Modules:
  0.0 163.5 jit_solution(15992656130112896195)
XLA Ops:
  0.6 1.3 copy.39
  2.0 2.5 %collective-permute-start = (bf16[1,1,96,2048]{2,3,1,0:T(8,128)(2,1)S(1)}, bf16[1,1,96,2048]{2,3,1,0:T(8,128)(2,1)S(1)}, u32[]{:S(2)}, u32[]{:S(2)}) collective-permute-start(bf16[1,1,96,2048]{2,3,1,0:T(8,128)(2,1)S(1)} %copy.39), channel_id=1, source_target_pairs={{0,896},{128,0},{256,128},{384,256},{512,384},{640,512},{768,640},... | collective-permute-start | bytes 1179656 | tf_op jit(solution)/shard_map/ppermute | solution.py:21
  4.5 0.3 copy.40
  4.8 0.3 copy.38
  5.1 6.1 %collective-permute-done = bf16[1,1,96,2048]{2,3,1,0:T(8,128)(2,1)S(1)} collective-permute-done((bf16[1,1,96,2048]{2,3,1,0:T(8,128)(2,1)S(1)}, bf16[1,1,96,2048]{2,3,1,0:T(8,128)(2,1)S(1)}, u32[]{:S(2)}, u32[]{:S(2)}) %collective-permute-start) | collective-permute-done | bytes 393248 | tf_op jit(solution)/shard_map/ppermute | solution.py:21
  11.2 0.2 fusion
  11.5 0.1 convert_element_type.46
  11.6 0.5 copy.42
  12.1 0.3 maximum_bitcast_fusion
  12.4 0.6 pad_maximum_fusion
  13.0 1.3 copy.43
  14.3 28.9 %all-to-all-start = ((bf16[32,112,128]{2,1,0:T(8,128)(2,1)}), bf16[32,112,128]{2,1,0:T(8,128)(2,1)S(1)}, u32[]{:S(2)}, u32[]{:S(2)}) async-start(bf16[32,112,128]{2,1,0:T(8,128)(2,1)} %copy.43), calls=%async_computation | async-start | bytes 1835008 | tf_op jit(solution)/shard_map/all_to_all | solution.py:164
  43.2 3.4 %collective-permute-start.1 = (bf16[256,128]{1,0:T(8,128)(2,1)S(1)}, bf16[256,128]{1,0:T(8,128)(2,1)S(1)}, u32[]{:S(2)}, u32[]{:S(2)}) collective-permute-start(bf16[256,128]{1,0:T(8,128)(2,1)S(1)} %get-tuple-element.14), channel_id=1, source_target_pairs={{0,1},{1,2},{2,3},{4,5},{5,6},{6,7},{8,9},{9,10},{10,11},{12,13},{... | collective-permute-start | bytes 196616 | tf_op jit(solution)/shard_map/ppermute | solution.py:26
  46.6 2.4 %collective-permute-start.2 = (bf16[256,128]{1,0:T(8,128)(2,1)S(1)}, bf16[256,128]{1,0:T(8,128)(2,1)S(1)}, u32[]{:S(2)}, u32[]{:S(2)}) collective-permute-start(bf16[256,128]{1,0:T(8,128)(2,1)S(1)} %get-tuple-element.15), channel_id=1, source_target_pairs={{1,0},{2,1},{3,2},{5,4},{6,5},{7,6},{9,8},{10,9},{11,10},{13,12},{... | collective-permute-start | bytes 196616 | tf_op jit(solution)/shard_map/ppermute | solution.py:31
  49.0 0.1 dynamic-slice_compare_fusion
  49.1 0.1 subtract_add_fusion
  49.2 0.1 copy.44
  49.4 0.1 pad.14
  49.4 0.1 broadcast_in_dim.14
  49.6 0.1 broadcast_in_dim.15
  49.7 0.8 fusion.1.bias_ref
  50.5 2.2 %collective-permute-done.2 = bf16[256,128]{1,0:T(8,128)(2,1)S(1)} collective-permute-done((bf16[256,128]{1,0:T(8,128)(2,1)S(1)}, bf16[256,128]{1,0:T(8,128)(2,1)S(1)}, u32[]{:S(2)}, u32[]{:S(2)}) %collective-permute-start.2) | collective-permute-done | bytes 65568 | tf_op jit(solution)/shard_map/ppermute | solution.py:31
  52.7 1.0 pad_maximum_fusion.1.kv_ref
  53.7 85.4 %all-to-all-done = bf16[32,112,128]{2,1,0:T(8,128)(2,1)S(1)} async-done(((bf16[32,112,128]{2,1,0:T(8,128)(2,1)}), bf16[32,112,128]{2,1,0:T(8,128)(2,1)S(1)}, u32[]{:S(2)}, u32[]{:S(2)}) %all-to-all-start) | async-done | bytes 917536 | tf_op jit(solution)/shard_map/all_to_all | solution.py:164
  139.2 0.1 reshape.66
  139.4 0.7 add.50.dl_ref
  140.1 11.9 %shard_map.77 = (bf16[64,3072]{1,0:T(8,128)(2,1)}, bf16[3072,128]{1,0:T(8,128)(2,1)}, f32[256,128]{1,0:T(8,128)}, f32[256,128]{1,0:T(8,128)}, f32[256,128]{1,0:T(8,128)}, /*index=5*/f32[256,128]{1,0:T(8,128)}) custom-call(bf16[3584,128]{1,0:T(8,128)(2,1)} %bitcast.51, bf16[3584,128]{1,0:T(8,128)(2,1)} %pad_maximum_fusion.1.kv_ref, ...), custom_call_target="tpu_custom_call" | custom-call | flops 3019898880 | bytes 3039232 | tf_op jit(solution)/shard_map/pallas_call | solution.py:94
  152.0 3.5 %collective-permute-start.3 = (f32[256,128]{1,0:T(8,128)}, f32[256,128]{1,0:T(8,128)S(1)}, u32[]{:S(2)}, u32[]{:S(2)}) collective-permute-start(f32[256,128]{1,0:T(8,128)} %get-tuple-element.10), channel_id=1, source_target_pairs={{0,1},{1,2},{2,3},{4,5},{5,6},{6,7},{8,9},{9,10},{10,11},{12,13},{... | collective-permute-start | bytes 393224 | tf_op jit(solution)/shard_map/ppermute | solution.py:26
  155.5 2.4 %collective-permute-start.4 = (f32[256,128]{1,0:T(8,128)}, f32[256,128]{1,0:T(8,128)S(1)}, u32[]{:S(2)}, u32[]{:S(2)}) collective-permute-start(f32[256,128]{1,0:T(8,128)} %get-tuple-element.13), channel_id=1, source_target_pairs={{1,0},{2,1},{3,2},{5,4},{6,5},{7,6},{9,8},{10,9},{11,10},{13,12},{... | collective-permute-start | bytes 393224 | tf_op jit(solution)/shard_map/ppermute | solution.py:31
  158.0 1.1 slice.47
  159.2 3.4 %collective-permute-done.4 = f32[256,128]{1,0:T(8,128)S(1)} collective-permute-done((f32[256,128]{1,0:T(8,128)}, f32[256,128]{1,0:T(8,128)S(1)}, u32[]{:S(2)}, u32[]{:S(2)}) %collective-permute-start.4) | collective-permute-done | bytes 131104 | tf_op jit(solution)/shard_map/ppermute | solution.py:31
  162.6 0.9 maximum_bitcast_fusion.1
  (36 shorter events, 0.5 us)
Async XLA Ops:
  0.6 3.8 %copy-start.2 = (bf16[1,1,96,2048]{3,2,1,0:T(8,128)(2,1)S(1)}, bf16[1,1,96,2048]{3,2,1,0:T(8,128)(2,1)}, u32[]{:S(2)}) copy-start(bf16[1,1,96,2048]{3,2,1,0:T(8,128)(2,1)} %param.8) | copy-start | bytes 1179652
  0.6 4.1 %copy-start.3 = (bf16[1,1,96,2048]{3,2,1,0:T(8,128)(2,1)S(1)}, bf16[1,1,96,2048]{3,2,1,0:T(8,128)(2,1)}, u32[]{:S(2)}) copy-start(bf16[1,1,96,2048]{3,2,1,0:T(8,128)(2,1)} %param.7) | copy-start | bytes 1179652
  2.0 9.2 %collective-permute-start = (bf16[1,1,96,2048]{2,3,1,0:T(8,128)(2,1)S(1)}, bf16[1,1,96,2048]{2,3,1,0:T(8,128)(2,1)S(1)}, u32[]{:S(2)}, u32[]{:S(2)}) collective-permute-start(bf16[1,1,96,2048]{2,3,1,0:T(8,128)(2,1)S(1)} %copy.39), channel_id=1, source_target_pairs={{0,896},{128,0},{256,128},{384,256},{512,384},{640,512},{768,640},... | collective-permute-start | bytes 1179656 | tf_op jit(solution)/shard_map/ppermute | solution.py:21
  14.3 28.9 %copy-start.1 = (bf16[1,1,1,3072,128]{4,3,2,1,0:T(8,128)(2,1)S(1)}, bf16[1,1,1,3072,128]{4,3,2,1,0:T(8,128)(2,1)}, u32[]{:S(2)}) copy-start(bf16[1,1,1,3072,128]{4,3,2,1,0:T(8,128)(2,1)} %param.9) | copy-start | bytes 2359300
  14.3 34.8 %copy-start.7 = (s32[192,7]{0,1:T(8,128)S(1)}, s32[192,7]{0,1:T(8,128)}, u32[]{:S(2)}) copy-start(s32[192,7]{0,1:T(8,128)} %param.11) | copy-start | bytes 16132
  14.3 35.4 %copy-start.6 = (f32[1,1,1,3072]{3,2,1,0:T(1,128)S(1)}, f32[1,1,1,3072]{3,2,1,0:T(1,128)}, u32[]{:S(2)}) copy-start(f32[1,1,1,3072]{3,2,1,0:T(1,128)} %param.10) | copy-start | bytes 36868
  14.3 124.9 %all-to-all-start = ((bf16[32,112,128]{2,1,0:T(8,128)(2,1)}), bf16[32,112,128]{2,1,0:T(8,128)(2,1)S(1)}, u32[]{:S(2)}, u32[]{:S(2)}) async-start(bf16[32,112,128]{2,1,0:T(8,128)(2,1)} %copy.43), calls=%async_computation | async-start | bytes 1835008 | tf_op jit(solution)/shard_map/all_to_all | solution.py:164
  43.2 7.3 %collective-permute-start.1 = (bf16[256,128]{1,0:T(8,128)(2,1)S(1)}, bf16[256,128]{1,0:T(8,128)(2,1)S(1)}, u32[]{:S(2)}, u32[]{:S(2)}) collective-permute-start(bf16[256,128]{1,0:T(8,128)(2,1)S(1)} %get-tuple-element.14), channel_id=1, source_target_pairs={{0,1},{1,2},{2,3},{4,5},{5,6},{6,7},{8,9},{9,10},{10,11},{12,13},{... | collective-permute-start | bytes 196616 | tf_op jit(solution)/shard_map/ppermute | solution.py:26
  46.6 6.2 %collective-permute-start.2 = (bf16[256,128]{1,0:T(8,128)(2,1)S(1)}, bf16[256,128]{1,0:T(8,128)(2,1)S(1)}, u32[]{:S(2)}, u32[]{:S(2)}) collective-permute-start(bf16[256,128]{1,0:T(8,128)(2,1)S(1)} %get-tuple-element.15), channel_id=1, source_target_pairs={{1,0},{2,1},{3,2},{5,4},{6,5},{7,6},{9,8},{10,9},{11,10},{13,12},{... | collective-permute-start | bytes 196616 | tf_op jit(solution)/shard_map/ppermute | solution.py:31
  139.1 1.0 copy-start
  152.0 7.2 %copy-start.5 = (f32[256,128]{1,0:T(8,128)S(1)}, f32[256,128]{1,0:T(8,128)}, u32[]{:S(2)}) copy-start(f32[256,128]{1,0:T(8,128)} %get-tuple-element.9) | copy-start | bytes 393220
  152.0 10.6 %copy-start.4 = (f32[256,128]{1,0:T(8,128)S(1)}, f32[256,128]{1,0:T(8,128)}, u32[]{:S(2)}) copy-start(f32[256,128]{1,0:T(8,128)} %get-tuple-element.12) | copy-start | bytes 393220
  152.0 7.2 %collective-permute-start.3 = (f32[256,128]{1,0:T(8,128)}, f32[256,128]{1,0:T(8,128)S(1)}, u32[]{:S(2)}, u32[]{:S(2)}) collective-permute-start(f32[256,128]{1,0:T(8,128)} %get-tuple-element.10), channel_id=1, source_target_pairs={{0,1},{1,2},{2,3},{4,5},{5,6},{6,7},{8,9},{9,10},{10,11},{12,13},{... | collective-permute-start | bytes 393224 | tf_op jit(solution)/shard_map/ppermute | solution.py:26
  155.5 7.1 %collective-permute-start.4 = (f32[256,128]{1,0:T(8,128)}, f32[256,128]{1,0:T(8,128)S(1)}, u32[]{:S(2)}, u32[]{:S(2)}) collective-permute-start(f32[256,128]{1,0:T(8,128)} %get-tuple-element.13), channel_id=1, source_target_pairs={{1,0},{2,1},{3,2},{5,4},{6,5},{7,6},{9,8},{10,9},{11,10},{13,12},{... | collective-permute-start | bytes 393224 | tf_op jit(solution)/shard_map/ppermute | solution.py:31

commit v13 on v12

--- a/solution.py
+++ b/solution.py
@@ -75,7 +75,7 @@
             step(g * per + c, jnp.concatenate([a, b], axis=0))
         return carry
 
-    lax.fori_loop(0, rows // (span * per), grouped, 0)
+    lax.fori_loop(0, rows // (span * per), grouped, 0, unroll=2)
     cache_out[...] = cache_ref[pl.ds(rim, rows), :].astype(cache_out.dtype)
     head_ref[...] = cache_ref[pl.ds(rim, rim), :]
     tail_ref[...] = cache_ref[pl.ds(rows, rim), :]

time: 164 us -> 164 us (level)
  no operation moved by 1% of the time
where the time goes in v13:
time: 164 us; the launch traced here: 163 us
  waiting for transfers between devices  97.2 us (59%)
  starting transfers between devices  43.1 us (26%)
  Pallas kernels  11.5 us (7%)
  local copies, waits for them, and re-layouts  6.26 us (4%)
  other arithmetic  4.2 us (3%)
    all_to_all x1, waiting for transfers between devices, body(): got = lax.all_to_all(send, 'seq', split_axis=0, concat_axis=0, tiled=True)  85.4 us
    all_to_all x1, starting transfers between devices, body(): got = lax.all_to_all(send, 'seq', split_axis=0, concat_axis=0, tiled=True)  28.9 us
    pallas_call x1, Pallas kernels, band_grads(): pl.pallas_call(band_kernel, out_shape=(jax.ShapeDtypeStruct((HD, rows), j...  11.5 us
    ppermute x2, starting transfers between devices, to_right(): return lax.ppermute(value, axis, [(i, i + 1) for i in range(count - 1)])  6.92 us
    ppermute x1, waiting for transfers between devices, passed_along(): return lax.ppermute(value, axis, pairs)  6.07 us
    ppermute x2, waiting for transfers between devices, to_left(): return lax.ppermute(value, axis, [(i + 1, i) for i in range(count - 1)])  5.61 us
    ppermute x2, starting transfers between devices, to_left(): return lax.ppermute(value, axis, [(i + 1, i) for i in range(count - 1)])  4.89 us
  transfers between devices with their start and end apart: 6, of which 5 were waited for; matrix products, arithmetic and copies ran while one was open for 3% of the time, Pallas kernels for 0%

profile of v13, /device:TPU:2, one launch (start us, length us, event | category | flops | bytes accessed | tf_op | source)
XLA Modules:
  0.0 163.2 jit_solution(14342574220249846248)
XLA Ops:
  0.6 1.3 copy.39
  2.0 2.5 %collective-permute-start = (bf16[1,1,96,2048]{2,3,1,0:T(8,128)(2,1)S(1)}, bf16[1,1,96,2048]{2,3,1,0:T(8,128)(2,1)S(1)}, u32[]{:S(2)}, u32[]{:S(2)}) collective-permute-start(bf16[1,1,96,2048]{2,3,1,0:T(8,128)(2,1)S(1)} %copy.39), channel_id=1, source_target_pairs={{0,896},{128,0},{256,128},{384,256},{512,384},{640,512},{768,640},... | collective-permute-start | bytes 1179656 | tf_op jit(solution)/shard_map/ppermute | solution.py:21
  4.5 0.3 copy.40
  4.8 0.3 copy.38
  5.1 6.1 %collective-permute-done = bf16[1,1,96,2048]{2,3,1,0:T(8,128)(2,1)S(1)} collective-permute-done((bf16[1,1,96,2048]{2,3,1,0:T(8,128)(2,1)S(1)}, bf16[1,1,96,2048]{2,3,1,0:T(8,128)(2,1)S(1)}, u32[]{:S(2)}, u32[]{:S(2)}) %collective-permute-start) | collective-permute-done | bytes 393248 | tf_op jit(solution)/shard_map/ppermute | solution.py:21
  11.2 0.2 fusion
  11.5 0.1 convert_element_type.46
  11.6 0.5 copy.42
  12.1 0.3 maximum_bitcast_fusion
  12.4 0.6 pad_maximum_fusion
  13.0 1.3 copy.43
  14.3 28.9 %all-to-all-start = ((bf16[32,112,128]{2,1,0:T(8,128)(2,1)}), bf16[32,112,128]{2,1,0:T(8,128)(2,1)S(1)}, u32[]{:S(2)}, u32[]{:S(2)}) async-start(bf16[32,112,128]{2,1,0:T(8,128)(2,1)} %copy.43), calls=%async_computation | async-start | bytes 1835008 | tf_op jit(solution)/shard_map/all_to_all | solution.py:164
  43.2 3.4 %collective-permute-start.1 = (bf16[256,128]{1,0:T(8,128)(2,1)S(1)}, bf16[256,128]{1,0:T(8,128)(2,1)S(1)}, u32[]{:S(2)}, u32[]{:S(2)}) collective-permute-start(bf16[256,128]{1,0:T(8,128)(2,1)S(1)} %get-tuple-element.14), channel_id=1, source_target_pairs={{0,1},{1,2},{2,3},{4,5},{5,6},{6,7},{8,9},{9,10},{10,11},{12,13},{... | collective-permute-start | bytes 196616 | tf_op jit(solution)/shard_map/ppermute | solution.py:26
  46.6 2.4 %collective-permute-start.2 = (bf16[256,128]{1,0:T(8,128)(2,1)S(1)}, bf16[256,128]{1,0:T(8,128)(2,1)S(1)}, u32[]{:S(2)}, u32[]{:S(2)}) collective-permute-start(bf16[256,128]{1,0:T(8,128)(2,1)S(1)} %get-tuple-element.15), channel_id=1, source_target_pairs={{1,0},{2,1},{3,2},{5,4},{6,5},{7,6},{9,8},{10,9},{11,10},{13,12},{... | collective-permute-start | bytes 196616 | tf_op jit(solution)/shard_map/ppermute | solution.py:31
  49.0 0.1 dynamic-slice_compare_fusion
  49.1 0.1 subtract_add_fusion
  49.2 0.1 copy.44
  49.4 0.1 pad.14
  49.4 0.1 broadcast_in_dim.14
  49.6 0.1 broadcast_in_dim.15
  49.7 0.8 fusion.1.bias_ref
  50.5 2.2 %collective-permute-done.2 = bf16[256,128]{1,0:T(8,128)(2,1)S(1)} collective-permute-done((bf16[256,128]{1,0:T(8,128)(2,1)S(1)}, bf16[256,128]{1,0:T(8,128)(2,1)S(1)}, u32[]{:S(2)}, u32[]{:S(2)}) %collective-permute-start.2) | collective-permute-done | bytes 65568 | tf_op jit(solution)/shard_map/ppermute | solution.py:31
  52.7 1.0 pad_maximum_fusion.1.kv_ref
  53.7 85.4 %all-to-all-done = bf16[32,112,128]{2,1,0:T(8,128)(2,1)S(1)} async-done(((bf16[32,112,128]{2,1,0:T(8,128)(2,1)}), bf16[32,112,128]{2,1,0:T(8,128)(2,1)S(1)}, u32[]{:S(2)}, u32[]{:S(2)}) %all-to-all-start) | async-done | bytes 917536 | tf_op jit(solution)/shard_map/all_to_all | solution.py:164
  139.2 0.1 reshape.66
  139.4 0.7 add.50.dl_ref
  140.1 11.5 %shard_map.77 = (bf16[64,3072]{1,0:T(8,128)(2,1)}, bf16[3072,128]{1,0:T(8,128)(2,1)}, f32[256,128]{1,0:T(8,128)}, f32[256,128]{1,0:T(8,128)}, f32[256,128]{1,0:T(8,128)}, /*index=5*/f32[256,128]{1,0:T(8,128)}) custom-call(bf16[3584,128]{1,0:T(8,128)(2,1)} %bitcast.51, bf16[3584,128]{1,0:T(8,128)(2,1)} %pad_maximum_fusion.1.kv_ref, ...), custom_call_target="tpu_custom_call" | custom-call | flops 3019898880 | bytes 3039232 | tf_op jit(solution)/shard_map/pallas_call | solution.py:94
  151.6 3.5 %collective-permute-start.3 = (f32[256,128]{1,0:T(8,128)}, f32[256,128]{1,0:T(8,128)S(1)}, u32[]{:S(2)}, u32[]{:S(2)}) collective-permute-start(f32[256,128]{1,0:T(8,128)} %get-tuple-element.10), channel_id=1, source_target_pairs={{0,1},{1,2},{2,3},{4,5},{5,6},{6,7},{8,9},{9,10},{10,11},{12,13},{... | collective-permute-start | bytes 393224 | tf_op jit(solution)/shard_map/ppermute | solution.py:26
  155.1 2.4 %collective-permute-start.4 = (f32[256,128]{1,0:T(8,128)}, f32[256,128]{1,0:T(8,128)S(1)}, u32[]{:S(2)}, u32[]{:S(2)}) collective-permute-start(f32[256,128]{1,0:T(8,128)} %get-tuple-element.13), channel_id=1, source_target_pairs={{1,0},{2,1},{3,2},{5,4},{6,5},{7,6},{9,8},{10,9},{11,10},{13,12},{... | collective-permute-start | bytes 393224 | tf_op jit(solution)/shard_map/ppermute | solution.py:31
  157.6 1.1 slice.47
  158.8 3.4 %collective-permute-done.4 = f32[256,128]{1,0:T(8,128)S(1)} collective-permute-done((f32[256,128]{1,0:T(8,128)}, f32[256,128]{1,0:T(8,128)S(1)}, u32[]{:S(2)}, u32[]{:S(2)}) %collective-permute-start.4) | collective-permute-done | bytes 131104 | tf_op jit(solution)/shard_map/ppermute | solution.py:31
  162.2 0.9 maximum_bitcast_fusion.1
  (36 shorter events, 0.5 us)
Async XLA Ops:
  0.6 3.8 %copy-start.2 = (bf16[1,1,96,2048]{3,2,1,0:T(8,128)(2,1)S(1)}, bf16[1,1,96,2048]{3,2,1,0:T(8,128)(2,1)}, u32[]{:S(2)}) copy-start(bf16[1,1,96,2048]{3,2,1,0:T(8,128)(2,1)} %param.8) | copy-start | bytes 1179652
  0.6 4.1 %copy-start.3 = (bf16[1,1,96,2048]{3,2,1,0:T(8,128)(2,1)S(1)}, bf16[1,1,96,2048]{3,2,1,0:T(8,128)(2,1)}, u32[]{:S(2)}) copy-start(bf16[1,1,96,2048]{3,2,1,0:T(8,128)(2,1)} %param.7) | copy-start | bytes 1179652
  2.0 9.2 %collective-permute-start = (bf16[1,1,96,2048]{2,3,1,0:T(8,128)(2,1)S(1)}, bf16[1,1,96,2048]{2,3,1,0:T(8,128)(2,1)S(1)}, u32[]{:S(2)}, u32[]{:S(2)}) collective-permute-start(bf16[1,1,96,2048]{2,3,1,0:T(8,128)(2,1)S(1)} %copy.39), channel_id=1, source_target_pairs={{0,896},{128,0},{256,128},{384,256},{512,384},{640,512},{768,640},... | collective-permute-start | bytes 1179656 | tf_op jit(solution)/shard_map/ppermute | solution.py:21
  14.3 28.9 %copy-start.1 = (bf16[1,1,1,3072,128]{4,3,2,1,0:T(8,128)(2,1)S(1)}, bf16[1,1,1,3072,128]{4,3,2,1,0:T(8,128)(2,1)}, u32[]{:S(2)}) copy-start(bf16[1,1,1,3072,128]{4,3,2,1,0:T(8,128)(2,1)} %param.9) | copy-start | bytes 2359300
  14.3 34.8 %copy-start.7 = (s32[192,7]{0,1:T(8,128)S(1)}, s32[192,7]{0,1:T(8,128)}, u32[]{:S(2)}) copy-start(s32[192,7]{0,1:T(8,128)} %param.11) | copy-start | bytes 16132
  14.3 35.4 %copy-start.6 = (f32[1,1,1,3072]{3,2,1,0:T(1,128)S(1)}, f32[1,1,1,3072]{3,2,1,0:T(1,128)}, u32[]{:S(2)}) copy-start(f32[1,1,1,3072]{3,2,1,0:T(1,128)} %param.10) | copy-start | bytes 36868
  14.3 124.9 %all-to-all-start = ((bf16[32,112,128]{2,1,0:T(8,128)(2,1)}), bf16[32,112,128]{2,1,0:T(8,128)(2,1)S(1)}, u32[]{:S(2)}, u32[]{:S(2)}) async-start(bf16[32,112,128]{2,1,0:T(8,128)(2,1)} %copy.43), calls=%async_computation | async-start | bytes 1835008 | tf_op jit(solution)/shard_map/all_to_all | solution.py:164
  43.2 7.3 %collective-permute-start.1 = (bf16[256,128]{1,0:T(8,128)(2,1)S(1)}, bf16[256,128]{1,0:T(8,128)(2,1)S(1)}, u32[]{:S(2)}, u32[]{:S(2)}) collective-permute-start(bf16[256,128]{1,0:T(8,128)(2,1)S(1)} %get-tuple-element.14), channel_id=1, source_target_pairs={{0,1},{1,2},{2,3},{4,5},{5,6},{6,7},{8,9},{9,10},{10,11},{12,13},{... | collective-permute-start | bytes 196616 | tf_op jit(solution)/shard_map/ppermute | solution.py:26
  46.6 6.2 %collective-permute-start.2 = (bf16[256,128]{1,0:T(8,128)(2,1)S(1)}, bf16[256,128]{1,0:T(8,128)(2,1)S(1)}, u32[]{:S(2)}, u32[]{:S(2)}) collective-permute-start(bf16[256,128]{1,0:T(8,128)(2,1)S(1)} %get-tuple-element.15), channel_id=1, source_target_pairs={{1,0},{2,1},{3,2},{5,4},{6,5},{7,6},{9,8},{10,9},{11,10},{13,12},{... | collective-permute-start | bytes 196616 | tf_op jit(solution)/shard_map/ppermute | solution.py:31
  139.1 1.0 copy-start
  151.6 7.2 %copy-start.5 = (f32[256,128]{1,0:T(8,128)S(1)}, f32[256,128]{1,0:T(8,128)}, u32[]{:S(2)}) copy-start(f32[256,128]{1,0:T(8,128)} %get-tuple-element.9) | copy-start | bytes 393220
  151.6 10.6 %copy-start.4 = (f32[256,128]{1,0:T(8,128)S(1)}, f32[256,128]{1,0:T(8,128)}, u32[]{:S(2)}) copy-start(f32[256,128]{1,0:T(8,128)} %get-tuple-element.12) | copy-start | bytes 393220
  151.6 7.2 %collective-permute-start.3 = (f32[256,128]{1,0:T(8,128)}, f32[256,128]{1,0:T(8,128)S(1)}, u32[]{:S(2)}, u32[]{:S(2)}) collective-permute-start(f32[256,128]{1,0:T(8,128)} %get-tuple-element.10), channel_id=1, source_target_pairs={{0,1},{1,2},{2,3},{4,5},{5,6},{6,7},{8,9},{9,10},{10,11},{12,13},{... | collective-permute-start | bytes 393224 | tf_op jit(solution)/shard_map/ppermute | solution.py:26
  155.1 7.1 %collective-permute-start.4 = (f32[256,128]{1,0:T(8,128)}, f32[256,128]{1,0:T(8,128)S(1)}, u32[]{:S(2)}, u32[]{:S(2)}) collective-permute-start(f32[256,128]{1,0:T(8,128)} %get-tuple-element.13), channel_id=1, source_target_pairs={{1,0},{2,1},{3,2},{5,4},{6,5},{7,6},{9,8},{10,9},{11,10},{13,12},{... | collective-permute-start | bytes 393224 | tf_op jit(solution)/shard_map/ppermute | solution.py:31
